TPU v7x, 32 devices: a whole 2x2x4 slice. The times are simulated.
32 devices in a mesh: tm: 8 (over z, y), col: 4 (over x, core).
Axes of the slice: x: 2, y: 2, z: 4, core: 2. Of those that a mesh axis runs over, the one named last changes fastest.
Arguments:
- observed: bfloat16 [16, 128, 512], P('tm', None, 'col'), may hold values from -6 to 6
- input_gain: float32 [512], P('col'), may hold values from 0.03 to 0.3
- persist: float32 [16, 512], P('tm', 'col'), may hold values from 0.5 to 1, as said below
- coupling: bfloat16 [16, 512, 512], P('tm', None, 'col'), may hold values from -0.02734375 to 0.02734375
- pattern: int32 [8, 8], replicated, may hold values 0 or 1
Outputs:
- filtered: float32 [16, 128, 512], P('tm', None, 'col')
- smoothed: float32 [16, 128, 512], P('tm', None, 'col')
Inputs may be any that keep to these rules, and one draw needn't show every extreme that they name: `persist`: persistence of each state component at each step.
All inputs are finite; a program needn't handle non-finite values.
Results may differ from a plain program's by a relative error of at most 0.0003.
Values may be sent and summed in bfloat16 or wider, within the bound.
No kernel may reach another device: no remote copies, remote signals or barrier semaphores. Data moves between devices by JAX's collectives and lax.ppermute only.
A program may use at most 64 MiB of HBM per device.

v0:
```python
import jax
import jax.numpy as jnp
from jax import lax
from jax.sharding import PartitionSpec as P


def passed_along(shard, axis, by):
    length = lax.axis_size(axis)
    pairs = [(i, i + by) for i in range(length) if 0 <= i + by < length]
    return lax.ppermute(shard, axis, pairs)


def matmul(left, right):
    return jnp.dot(left, right, precision=lax.Precision.HIGHEST, preferred_element_type=jnp.float32)


def advance(state, matrix):
    return matmul(lax.all_gather(state, "col", axis=1, tiled=True), matrix)


def smooth_step(later, state_full, state_part, cols_matrix, rows_matrix):
    predicted = matmul(state_full, cols_matrix)
    residual = later - predicted
    residual_full = lax.all_gather(residual, "col", axis=1, tiled=True)
    return state_part + matmul(residual_full, rows_matrix.T)


def local(observed, input_gain, persist, coupling, pattern):
    step_count = observed.shape[0]
    panels = observed.shape[1]
    state_width = coupling.shape[1]
    col_count = coupling.shape[2]
    block_count = pattern.shape[0]
    block_size = state_width // block_count
    col_pos = lax.axis_index("col")
    tm_pos = lax.axis_index("tm")
    time_block_groups = lax.axis_size("tm")
    first_col = col_pos * col_count
    pattern_real = pattern.astype(jnp.float32)
    row_ids = jnp.arange(state_width)
    col_ids = first_col + jnp.arange(col_count)
    block_labels = jnp.arange(block_count)
    row_hot = (row_ids[:, None] // block_size == block_labels[None, :]).astype(jnp.float32)
    col_hot = (col_ids[:, None] // block_size == block_labels[None, :]).astype(jnp.float32)
    mask_cols = matmul(matmul(row_hot, pattern_real), col_hot.T)
    mask_rows = matmul(matmul(col_hot, pattern_real), row_hot.T)
    diag_cols = (row_ids[:, None] == col_ids[None, :]).astype(jnp.float32)
    diag_rows = diag_cols.T
    trans_cols = (
        coupling.astype(jnp.float32) * mask_cols[None] + diag_cols[None] * persist[:, None, :]
    )
    rows_coupling = lax.all_to_all(coupling, "col", split_axis=1, concat_axis=2, tiled=True)
    trans_rows = (
        rows_coupling.astype(jnp.float32) * mask_rows[None] + diag_rows[None] * persist[:, :, None]
    )
    driven = input_gain[None, None, :] * observed.astype(jnp.float32)
    top_zeros = jnp.zeros((state_width, col_count), jnp.float32)
    state = jnp.concatenate([diag_cols, jnp.zeros((panels, col_count), jnp.float32)], axis=0)
    history = []
    for position in range(step_count):
        state = advance(state, trans_cols[position]) + jnp.concatenate(
            [top_zeros, driven[position]], axis=0
        )
        history.append(state)
    stacked_rows = jnp.stack(history)
    element = history[-1]
    saved = []
    stride = 1
    whole = lax.all_gather(element, "col", axis=1, tiled=True)
    whole_zeros = jnp.zeros((state_width, state_width), jnp.float32)
    while stride < time_block_groups:
        own_prod = whole[:state_width]
        saved.append(lax.dynamic_slice_in_dim(own_prod, first_col, col_count, 1))
        prior_values = passed_along(whole, "tm", stride)
        joined = matmul(prior_values, own_prod) + jnp.concatenate(
            [whole_zeros, whole[state_width:]], axis=0
        )
        whole = jnp.where(tm_pos >= stride, joined, whole)
        stride = stride * 2
    end_slice = lax.dynamic_slice_in_dim(whole[state_width:], first_col, col_count, 1)
    start_slice = passed_along(end_slice, "tm", 1)
    start_full = lax.all_gather(start_slice, "col", axis=1, tiled=True)
    filtered = (
        jnp.einsum(
            "bs,lsc->lbc",
            start_full,
            stacked_rows[:, :state_width],
            precision=lax.Precision.HIGHEST,
        )
        + stacked_rows[:, state_width:]
    )
    filtered_full = lax.all_gather(filtered, "col", axis=2, tiled=True)
    later = jnp.zeros((panels, col_count), jnp.float32)
    for position in range(step_count - 1, -1, -1):
        if position > 0:
            later = smooth_step(
                later,
                filtered_full[position - 1],
                filtered[position - 1],
                trans_cols[position],
                trans_rows[position],
            )
        else:
            later = smooth_step(
                later, start_full, start_slice, trans_cols[position], trans_rows[position]
            )
    offset = later
    from_next = passed_along(offset, "tm", -1)
    carried = jnp.where(tm_pos == time_block_groups - 1, filtered[step_count - 1], from_next)
    stride = 1
    for level_prod in saved:
        partial_value = matmul(carried, level_prod.T)
        shares = lax.psum_scatter(partial_value, "col", scatter_dimension=1, tiled=True)
        carried = carried + passed_along(shares, "tm", -stride)
        stride = stride * 2
    later = carried
    smoothed_list = [carried]
    position = 1
    later = smooth_step(
        later,
        filtered_full[position - 1],
        filtered[position - 1],
        trans_cols[position],
        trans_rows[position],
    )
    smoothed_list.append(later)
    smoothed = jnp.stack(smoothed_list[::-1])
    return (filtered, smoothed)


def solution(mesh):
    return jax.shard_map(
        local,
        mesh=mesh,
        in_specs=(P("tm", None, "col"), P("col"), P("tm", "col"), P("tm", None, "col"), P()),
        out_specs=(P("tm", None, "col"), P("tm", None, "col")),
        check_vma=False,
    )
```

profile of v0, /device:TPU:0, one launch (start us, length us, event | category | flops | bytes accessed | tf_op | source)
XLA Modules:
  0.0 347.9 jit_solution(4081061395193366817)
XLA Ops:
  7.3 0.7 concatenate.18
  8.1 1.0 fusion.16
  9.1 0.7 convert_multiply_fusion
  10.4 20.2 %all-gather.4.cloned.1.call-done = f32[640,512]{1,0:T(8,128)} async-done(((f32[640,128]{1,0:T(8,128)}), f32[640,512]{1,0:T(8,128)}) %all-gather.4.cloned.1.call-update) | async-done | bytes 1310736 | tf_op jit(solution)/shard_map/all_gather | solution.py:18
  30.6 3.2 convolution_add_fusion.3
  33.9 18.4 %all-gather.6.cloned.1.call-done = f32[640,512]{1,0:T(8,128)} async-done(((f32[640,128]{1,0:T(8,128)}), f32[640,512]{1,0:T(8,128)}) %all-gather.6.cloned.1.call-update) | async-done | bytes 1310736 | tf_op jit(solution)/shard_map/all_gather | solution.py:18
  52.3 3.2 convolution_add_fusion.2
  55.6 18.5 %all-gather.8.cloned.1.call-done = f32[640,512]{1,0:T(8,128)} async-done(((f32[640,128]{1,0:T(8,128)}), f32[640,512]{1,0:T(8,128)}) %all-gather.8.cloned.1.call-update) | async-done | bytes 1310736 | tf_op jit(solution)/shard_map/all_gather | solution.py:69
  74.1 3.4 collective-permute-start
  77.5 1.0 slice.85
  78.5 27.7 %collective-permute-done = f32[640,512]{1,0:T(8,128)S(1)} collective-permute-done((f32[640,512]{1,0:T(8,128)}, f32[640,512]{1,0:T(8,128)S(1)}, u32[]{:S(2)}, u32[]{:S(2)}) %collective-permute-start) | collective-permute-done | bytes 1310752 | tf_op jit(solution)/shard_map/ppermute | solution.py:10
  106.2 3.9 %fusion = f32[640,512]{1,0:T(8,128)S(1)} fusion(f32[640,512]{1,0:T(8,128)} %all-gather.8.cloned.1.call-done, f32[640,512]{1,0:T(8,128)S(1)} %collective-permute-done, f32[128,512]{1,0:T(8,128)S(1)} %slice.85, pred[]{:T(512)S(6)} %ge.11), kind=kOutput, calls=%fused_computation.2 | convolution fusion | flops 2013921280 | bytes 5242881 | tf_op jit(solution)/shard_map/dot_general | solution.py:14
  110.1 6.3 %collective-permute-start.1 = (f32[640,512]{1,0:T(8,128)S(1)}, f32[640,512]{1,0:T(8,128)}, u32[]{:S(2)}, u32[]{:S(2)}) collective-permute-start(f32[640,512]{1,0:T(8,128)S(1)} %fusion), channel_id=1, source_target_pairs={{0,8},{4,12},{8,16},{12,20},{16,24},{20,28},{1,9},{5,13},{9,17},{1... | collective-permute-start | bytes 3932168 | tf_op jit(solution)/shard_map/ppermute | solution.py:10
  116.5 26.5 %collective-permute-done.1 = f32[640,512]{1,0:T(8,128)} collective-permute-done((f32[640,512]{1,0:T(8,128)S(1)}, f32[640,512]{1,0:T(8,128)}, u32[]{:S(2)}, u32[]{:S(2)}) %collective-permute-start.1) | collective-permute-done | bytes 1310752 | tf_op jit(solution)/shard_map/ppermute | solution.py:10
  142.9 3.6 %fusion.1 = f32[640,512]{1,0:T(8,128)S(1)} fusion(f32[640,512]{1,0:T(8,128)S(1)} %fusion, f32[640,512]{1,0:T(8,128)} %collective-permute-done.1, f32[128,512]{1,0:T(8,128)S(1)} %slice.87, pred[]{:T(512)S(6)} %ge.10), kind=kOutput, calls=%fused_computation.3 | convolution fusion | flops 2013921280 | bytes 5242881 | tf_op jit(solution)/shard_map/dot_general | solution.py:14
  146.5 6.5 %collective-permute-start.2 = (f32[640,512]{1,0:T(8,128)S(1)}, f32[640,512]{1,0:T(8,128)}, u32[]{:S(2)}, u32[]{:S(2)}) collective-permute-start(f32[640,512]{1,0:T(8,128)S(1)} %fusion.1), channel_id=1, source_target_pairs={{0,16},{4,20},{8,24},{12,28},{1,17},{5,21},{9,25},{13,29},{2,18},{... | collective-permute-start | bytes 3932168 | tf_op jit(solution)/shard_map/ppermute | solution.py:10
  153.0 1.0 copy.18
  154.0 3.4 all-to-all-start
  157.6 1.1 fusion.15
  158.7 0.7 fusion.18
  159.5 3.9 %all-to-all-done = bf16[2,512,128]{2,0,1:T(2,128)(2,1)S(1)} async-done(((bf16[2,512,128]{2,0,1:T(2,128)(2,1)}), bf16[2,512,128]{2,0,1:T(2,128)(2,1)S(1)}, u32[]{:S(2)}, u32[]{:S(2)}) %all-to-all-start) | async-done | bytes 262176 | tf_op jit(solution)/shard_map/all_to_all | solution.py:52
  163.4 0.8 convert_bitcast_fusion
  164.2 2.0 copy.20
  166.3 12.4 %collective-permute-done.2 = f32[640,512]{1,0:T(8,128)} collective-permute-done((f32[640,512]{1,0:T(8,128)S(1)}, f32[640,512]{1,0:T(8,128)}, u32[]{:S(2)}, u32[]{:S(2)}) %collective-permute-start.2) | collective-permute-done | bytes 1310752 | tf_op jit(solution)/shard_map/ppermute | solution.py:10
  178.7 3.6 %fusion.39 = f32[640,512]{1,0:T(8,128)S(1)} fusion(f32[640,512]{1,0:T(8,128)} %collective-permute-done.2, f32[640,512]{1,0:T(8,128)S(1)} %fusion.1), kind=kOutput, calls=%fused_computation.80 | convolution fusion | flops 2013265920 | bytes 3670016 | tf_op jit(solution)/shard_map/dot_general | solution.py:14
  182.3 2.6 collective-permute-start.3
  185.1 1.8 collective-permute-done.3
  186.9 5.9 %all_gather.27 = f32[128,512]{1,0:T(8,128)S(1)} all-gather(f32[128,128]{1,0:T(8,128)S(1)} %collective-permute-done.3), channel_id=1, replica_groups=mesh['tm'=8,'col'=4] {'col'}, dimensions={1}, use_global_device_ids=true | all-gather | bytes 327680 | tf_op jit(solution)/shard_map/all_gather | solution.py:82
  193.3 7.3 %all_gather.28 = f32[2,128,512]{2,1,0:T(8,128)S(1)} all-gather(f32[2,128,128]{2,1,0:T(8,128)S(1)} %fusion.2), channel_id=1, replica_groups=mesh['tm'=8,'col'=4] {'col'}, dimensions={2}, use_global_device_ids=true | all-gather | bytes 655360 | tf_op jit(solution)/shard_map/all_gather | solution.py:92
  200.9 5.9 %all_gather.29 = f32[128,512]{1,0:T(8,128)S(1)} all-gather(f32[128,128]{1,0:T(8,128)S(1)} %get-tuple-element.6), channel_id=1, replica_groups=mesh['tm'=8,'col'=4] {'col'}, dimensions={1}, use_global_device_ids=true | all-gather | bytes 327680 | tf_op jit(solution)/shard_map/all_gather | solution.py:24
  207.6 5.9 %all_gather.30 = f32[128,512]{1,0:T(8,128)S(1)} all-gather(f32[128,128]{1,0:T(8,128)S(1)} %convolution_subtract_fusion), channel_id=1, replica_groups=mesh['tm'=8,'col'=4] {'col'}, dimensions={1}, use_global_device_ids=true | all-gather | bytes 327680 | tf_op jit(solution)/shard_map/all_gather | solution.py:24
  213.8 1.3 collective-permute-start.4
  215.1 1.3 slice.84
  216.4 32.3 %collective-permute-done.4 = f32[128,128]{1,0:T(8,128)S(1)} collective-permute-done((f32[128,128]{1,0:T(8,128)S(1)}, f32[128,128]{1,0:T(8,128)S(1)}, u32[]{:S(2)}, u32[]{:S(2)}) %collective-permute-start.4) | collective-permute-done | bytes 65568 | tf_op jit(solution)/shard_map/ppermute | solution.py:10
  248.7 1.1 fusion.13
  249.9 22.4 %reduce-scatter.4.cloned.1.call-done = f32[128,128]{1,0:T(8,128)} async-done(((f32[128,512]{1,0:T(8,128)}), f32[128,128]{1,0:T(8,128)}) %reduce-scatter.4.cloned.1.call-update) | async-done | bytes 65552 | tf_op jit(solution)/shard_map/reduce_scatter | solution.py:113
  272.2 1.3 collective-permute-start.5
  273.6 5.0 %collective-permute-done.5 = f32[128,128]{1,0:T(8,128)S(1)} collective-permute-done((f32[128,128]{1,0:T(8,128)}, f32[128,128]{1,0:T(8,128)S(1)}, u32[]{:S(2)}, u32[]{:S(2)}) %collective-permute-start.5) | collective-permute-done | bytes 65568 | tf_op jit(solution)/shard_map/ppermute | solution.py:10
  278.6 1.1 fusion.11
  279.8 20.2 %reduce-scatter.6.cloned.1.call-done = f32[128,128]{1,0:T(8,128)} async-done(((f32[128,512]{1,0:T(8,128)}), f32[128,128]{1,0:T(8,128)}) %reduce-scatter.6.cloned.1.call-update) | async-done | bytes 65552 | tf_op jit(solution)/shard_map/reduce_scatter | solution.py:113
  299.9 1.3 collective-permute-start.6
  301.3 5.0 %collective-permute-done.6 = f32[128,128]{1,0:T(8,128)S(1)} collective-permute-done((f32[128,128]{1,0:T(8,128)}, f32[128,128]{1,0:T(8,128)S(1)}, u32[]{:S(2)}, u32[]{:S(2)}) %collective-permute-start.6) | collective-permute-done | bytes 65568 | tf_op jit(solution)/shard_map/ppermute | solution.py:10
  306.3 1.1 fusion.9
  307.4 19.3 %reduce-scatter.8.cloned.1.call-done = f32[128,128]{1,0:T(8,128)} async-done(((f32[128,512]{1,0:T(8,128)}), f32[128,128]{1,0:T(8,128)}) %reduce-scatter.8.cloned.1.call-update) | async-done | bytes 65552 | tf_op jit(solution)/shard_map/reduce_scatter | solution.py:113
  326.7 1.3 collective-permute-start.7
  328.0 6.3 %collective-permute-done.7 = f32[128,128]{1,0:T(8,128)S(1)} collective-permute-done((f32[128,128]{1,0:T(8,128)}, f32[128,128]{1,0:T(8,128)S(1)}, u32[]{:S(2)}, u32[]{:S(2)}) %collective-permute-start.7) | collective-permute-done | bytes 65568 | tf_op jit(solution)/shard_map/ppermute | solution.py:10
  334.3 5.8 %all_gather.31 = f32[128,512]{1,0:T(8,128)S(1)} all-gather(f32[128,128]{1,0:T(8,128)S(1)} %get-tuple-element.2), channel_id=1, replica_groups=mesh['tm'=8,'col'=4] {'col'}, dimensions={1}, use_global_device_ids=true | all-gather | bytes 327680 | tf_op jit(solution)/shard_map/all_gather | solution.py:24
  340.4 0.7 pad_maximum_fusion.1
  (60 shorter events, 3.9 us)
Async XLA Ops:
  7.2 2.0 copy-start.9
  7.2 3.1 copy-start.10
  7.2 3.1 copy-start.6
  7.2 23.4 %all-gather.4.cloned.1.call-start = ((), (), s32[]{:S(2)}) async-start(), calls=%async_computation.4 | async-start | bytes 1638400 | tf_op jit(solution)/shard_map/all_gather | solution.py:18
  8.1 44.3 %all-gather.6.cloned.1.call-start = ((), (), s32[]{:S(2)}) async-start(), calls=%async_computation.5 | async-start | bytes 1638400 | tf_op jit(solution)/shard_map/all_gather | solution.py:18
  33.9 40.2 %all-gather.8.cloned.1.call-start = ((), (), s32[]{:S(2)}) async-start(), calls=%async_computation.6 | async-start | bytes 1638400 | tf_op jit(solution)/shard_map/all_gather | solution.py:69
  74.1 32.1 %collective-permute-start = (f32[640,512]{1,0:T(8,128)}, f32[640,512]{1,0:T(8,128)S(1)}, u32[]{:S(2)}, u32[]{:S(2)}) collective-permute-start(f32[640,512]{1,0:T(8,128)} %all-gather.8.cloned.1.call-done), channel_id=1, source_target_pairs={{0,4},{4,8},{8,12},{12,16},{16,20},{20,24},{24,28},{1,5},{5,9},{9,... | collective-permute-start | bytes 3932168 | tf_op jit(solution)/shard_map/ppermute | solution.py:10
  110.1 32.8 %collective-permute-start.1 = (f32[640,512]{1,0:T(8,128)S(1)}, f32[640,512]{1,0:T(8,128)}, u32[]{:S(2)}, u32[]{:S(2)}) collective-permute-start(f32[640,512]{1,0:T(8,128)S(1)} %fusion), channel_id=1, source_target_pairs={{0,8},{4,12},{8,16},{12,20},{16,24},{20,28},{1,9},{5,13},{9,17},{1... | collective-permute-start | bytes 3932168 | tf_op jit(solution)/shard_map/ppermute | solution.py:10
  116.4 41.0 %copy-start.11 = (s32[8,8]{1,0:T(8,128)S(1)}, s32[8,8]{1,0:T(8,128)}, u32[]{:S(2)}) copy-start(s32[8,8]{1,0:T(8,128)} %param.9) | copy-start | bytes 772
  146.5 32.2 %collective-permute-start.2 = (f32[640,512]{1,0:T(8,128)S(1)}, f32[640,512]{1,0:T(8,128)}, u32[]{:S(2)}, u32[]{:S(2)}) collective-permute-start(f32[640,512]{1,0:T(8,128)S(1)} %fusion.1), channel_id=1, source_target_pairs={{0,16},{4,20},{8,24},{12,28},{1,17},{5,21},{9,25},{13,29},{2,18},{... | collective-permute-start | bytes 3932168 | tf_op jit(solution)/shard_map/ppermute | solution.py:10
  154.0 9.4 %all-to-all-start = ((bf16[2,512,128]{2,0,1:T(2,128)(2,1)}), bf16[2,512,128]{2,0,1:T(2,128)(2,1)S(1)}, u32[]{:S(2)}, u32[]{:S(2)}) async-start(bf16[2,512,128]{2,0,1:T(2,128)(2,1)} %copy.18), calls=%async_computation | async-start | bytes 524288 | tf_op jit(solution)/shard_map/all_to_all | solution.py:52
  157.4 114.9 %reduce-scatter.4.cloned.1.call-start = ((), (), s32[]{:S(2)}) async-start(), calls=%async_computation.7 | async-start | bytes 327680 | tf_op jit(solution)/shard_map/reduce_scatter | solution.py:113
  166.3 18.7 %copy-start.7 = (f32[128,512]{0,1:T(8,128)S(1)}, f32[128,512]{0,1:T(8,128)}, u32[]{:S(2)}) copy-start(f32[128,512]{0,1:T(8,128)} %fusion.15) | copy-start | bytes 786436
  166.3 18.7 %copy-start.8 = (f32[128,512]{0,1:T(8,128)S(1)}, f32[128,512]{0,1:T(8,128)}, u32[]{:S(2)}) copy-start(f32[128,512]{0,1:T(8,128)} %fusion.18) | copy-start | bytes 786436
  182.3 2.7 copy-start.5
  182.3 10.5 %copy-start = (f32[640,128]{1,0:T(8,128)S(1)}, f32[640,128]{1,0:T(8,128)}, u32[]{:S(2)}) copy-start(f32[640,128]{1,0:T(8,128)} %convolution_add_fusion.3) | copy-start | bytes 983044
  182.3 10.5 %copy-start.1 = (f32[640,128]{1,0:T(8,128)S(1)}, f32[640,128]{1,0:T(8,128)}, u32[]{:S(2)}) copy-start(f32[640,128]{1,0:T(8,128)} %convolution_add_fusion.2) | copy-start | bytes 983044
  182.3 4.5 %collective-permute-start.3 = (f32[128,128]{1,0:T(8,128)S(1)}, f32[128,128]{1,0:T(8,128)S(1)}, u32[]{:S(2)}, u32[]{:S(2)}) collective-permute-start(f32[128,128]{1,0:T(8,128)S(1)} %fusion.22), channel_id=1, source_target_pairs={{0,4},{4,8},{8,12},{12,16},{16,20},{20,24},{24,28},{1,5},{5,9},{9,... | collective-permute-start | bytes 196616 | tf_op jit(solution)/shard_map/ppermute | solution.py:10
  185.1 28.4 %copy-start.2 = (f32[2,128,512]{1,2,0:T(8,128)}, f32[2,128,512]{1,2,0:T(8,128)S(1)}, u32[]{:S(2)}) copy-start(f32[2,128,512]{1,2,0:T(8,128)S(1)} %fusion.6) | copy-start | bytes 1572868
  193.2 146.8 %copy-start.4 = (f32[2,128,128]{2,1,0:T(8,128)}, f32[2,128,128]{2,1,0:T(8,128)S(1)}, u32[]{:S(2)}) copy-start(f32[2,128,128]{2,1,0:T(8,128)S(1)} %fusion.2) | copy-start | bytes 393220
  213.8 34.9 %collective-permute-start.4 = (f32[128,128]{1,0:T(8,128)S(1)}, f32[128,128]{1,0:T(8,128)S(1)}, u32[]{:S(2)}, u32[]{:S(2)}) collective-permute-start(f32[128,128]{1,0:T(8,128)S(1)} %convolution_add_fusion.5), channel_id=1, source_target_pairs={{4,0},{8,4},{12,8},{16,12},{20,16},{24,20},{28,24},{5,1},{9,5},{13... | collective-permute-start | bytes 196616 | tf_op jit(solution)/shard_map/ppermute | solution.py:10
  249.8 50.1 %reduce-scatter.6.cloned.1.call-start = ((), (), s32[]{:S(2)}) async-start(), calls=%async_computation.8 | async-start | bytes 327680 | tf_op jit(solution)/shard_map/reduce_scatter | solution.py:113
  272.2 6.4 %collective-permute-start.5 = (f32[128,128]{1,0:T(8,128)}, f32[128,128]{1,0:T(8,128)S(1)}, u32[]{:S(2)}, u32[]{:S(2)}) collective-permute-start(f32[128,128]{1,0:T(8,128)} %reduce-scatter.4.cloned.1.call-done), channel_id=1, source_target_pairs={{4,0},{8,4},{12,8},{16,12},{20,16},{24,20},{28,24},{5,1},{9,5},{13... | collective-permute-start | bytes 196616 | tf_op jit(solution)/shard_map/ppermute | solution.py:10
  279.7 47.0 %reduce-scatter.8.cloned.1.call-start = ((), (), s32[]{:S(2)}) async-start(), calls=%async_computation.9 | async-start | bytes 327680 | tf_op jit(solution)/shard_map/reduce_scatter | solution.py:113
  299.9 6.4 %collective-permute-start.6 = (f32[128,128]{1,0:T(8,128)}, f32[128,128]{1,0:T(8,128)S(1)}, u32[]{:S(2)}, u32[]{:S(2)}) collective-permute-start(f32[128,128]{1,0:T(8,128)} %reduce-scatter.6.cloned.1.call-done), channel_id=1, source_target_pairs={{8,0},{12,4},{16,8},{20,12},{24,16},{28,20},{9,1},{13,5},{17,9},{2... | collective-permute-start | bytes 196616 | tf_op jit(solution)/shard_map/ppermute | solution.py:10
  301.3 38.7 %copy-start.3 = (f32[2,128,512]{1,2,0:T(8,128)S(1)}, f32[2,128,512]{1,2,0:T(8,128)}, u32[]{:S(2)}) copy-start(f32[2,128,512]{1,2,0:T(8,128)} %copy-done.2) | copy-start | bytes 1572868
  326.7 7.6 %collective-permute-start.7 = (f32[128,128]{1,0:T(8,128)}, f32[128,128]{1,0:T(8,128)S(1)}, u32[]{:S(2)}, u32[]{:S(2)}) collective-permute-start(f32[128,128]{1,0:T(8,128)} %reduce-scatter.8.cloned.1.call-done), channel_id=1, source_target_pairs={{16,0},{20,4},{24,8},{28,12},{17,1},{21,5},{25,9},{29,13},{18,2},{... | collective-permute-start | bytes 196616 | tf_op jit(solution)/shard_map/ppermute | solution.py:10
Sparse Core Ops, SparseCore 0:
  9.6 21.0 all-gather.3
  34.0 18.3 all-gather.5
  55.7 18.3 all-gather.7
  249.9 22.2 reduce-scatter.3
  279.8 20.0 reduce-scatter.5
  307.5 19.1 reduce-scatter.7
where the time goes:
time: 349 us; the launch traced here: 348 us
  waiting for transfers between devices  240 us (69%)
  blocking collectives  30.7 us (9%)
  starting transfers between devices  27.6 us (8%)
  matrix products  25.9 us (7%)
  between operations  14.5 us (4%)
  local copies, waits for them, and re-layouts  6.3 us (2%)
    ppermute x8, waiting for transfers between devices, passed_along(): return lax.ppermute(shard, axis, pairs)  117 us
    reduce_scatter x3, waiting for transfers between devices, local(): lax.psum_scatter(partial_value, 'col', scatter_dimension=1, tiled=True)  61.8 us
    all_gather x2, waiting for transfers between devices, advance(): return matmul(lax.all_gather(state, 'col', axis=1, tiled=True), matrix)  38.7 us
    dot_general x17, matrix products, matmul(): jnp.dot(left, right, precision=lax.Precision.HIGHEST, preferred_element_t...  25.4 us
    ppermute x8, starting transfers between devices, passed_along(): return lax.ppermute(shard, axis, pairs)  24 us
    all_gather x1, waiting for transfers between devices, local(): whole = lax.all_gather(element, 'col', axis=1, tiled=True)  18.5 us
    all_gather x3, blocking collectives, smooth_step(): residual_full = lax.all_gather(residual, 'col', axis=1, tiled=True)  17.5 us
    all_gather x1, blocking collectives, local(): filtered_full = lax.all_gather(filtered, 'col', axis=2, tiled=True)  7.28 us
  transfers between devices with their start and end apart: 15, of which 15 were waited for; matrix products, arithmetic and copies ran while one was open for 3% of the time, Pallas kernels for 0%

commit v1 on v0

v1 whole, which is shorter than its diff:
```python
import jax
import jax.numpy as jnp
from jax import lax
from jax.sharding import PartitionSpec as P


def passed_along(shard, axis, by):
    length = lax.axis_size(axis)
    pairs = [(i, i + by) for i in range(length) if 0 <= i + by < length]
    return lax.ppermute(shard, axis, pairs)


def split_dot(state, weights, transposed):
    high = state.astype(jnp.bfloat16)
    low = (state - high.astype(jnp.float32)).astype(jnp.bfloat16)
    both = jnp.concatenate([high, low], axis=0)
    contract = 1 if transposed else 0
    prod = lax.dot_general(
        both, weights, (((1,), (contract,)), ((), ())), preferred_element_type=jnp.float32
    )
    rows = state.shape[0]
    return prod[:rows] + prod[rows:]


def local(observed, input_gain, persist, coupling, pattern):
    step_count = observed.shape[0]
    state_width = coupling.shape[1]
    block_count = pattern.shape[0]
    block_size = state_width // block_count
    time_groups = lax.axis_size("tm")

    full_coupling = lax.all_gather(coupling, "col", axis=2, tiled=True)
    small = jnp.concatenate([persist, input_gain[None]], axis=0)
    small = lax.all_gather(small, "col", axis=1, tiled=True)
    diag = small[:step_count]
    gain = small[step_count]
    seen = lax.all_to_all(observed, "col", split_axis=1, concat_axis=2, tiled=True)

    mask = jnp.broadcast_to(
        pattern.astype(jnp.bfloat16)[:, None, :, None],
        (block_count, block_size, block_count, block_size),
    ).reshape(state_width, state_width)
    weights = full_coupling * mask[None]
    driven = gain[None, None, :] * seen.astype(jnp.float32)

    def forward(x):
        out = []
        for k in range(step_count):
            x = split_dot(x, weights[k], False) + x * diag[k][None] + driven[k]
            out.append(x)
        return out

    def backward(e):
        out = [None] * step_count
        out[step_count - 1] = e
        for k in range(step_count - 1, -1, -1):
            w = e + driven[k]
            e = split_dot(w, weights[k], True) + w * diag[k][None]
            if k > 0:
                out[k - 1] = e
        return out, e

    def stage(carry):
        x_in, e_in = carry
        xs = forward(x_in)
        _, e_out = backward(e_in)
        return passed_along(xs[-1], "tm", 1), passed_along(e_out, "tm", -1)

    zeros = jnp.zeros(driven.shape[1:], jnp.float32)
    carry = (zeros, zeros)
    if time_groups <= 8:
        for _ in range(time_groups - 1):
            carry = stage(carry)
    else:
        carry = lax.fori_loop(0, time_groups - 1, lambda _, c: stage(c), carry)
    x_in, e_in = carry
    xs = forward(x_in)
    es, _ = backward(e_in)
    filtered = jnp.stack(xs)
    smoothed = jnp.stack([x + e for x, e in zip(xs, es)])
    both = jnp.stack([filtered, smoothed])
    both = lax.all_to_all(both, "col", split_axis=3, concat_axis=2, tiled=True)
    return both[0], both[1]


def solution(mesh):
    return jax.shard_map(
        local,
        mesh=mesh,
        in_specs=(P("tm", None, "col"), P("col"), P("tm", "col"), P("tm", None, "col"), P()),
        out_specs=(P("tm", None, "col"), P("tm", None, "col")),
        check_vma=False,
    )
```

time: 349 us -> 151 us (0.43)
  waiting for transfers between devices: 240 us -> 55.9 us
  starting transfers between devices: 27.6 us -> 46.2 us
  matrix products: 25.9 us -> 7.36 us
  blocking collectives: 30.7 us -> 13.7 us
    ppermute x8 -> x14, waiting for transfers between devices: 117 us -> 46.7 us  [passed_along(): return lax.ppermute(shard, axis, pairs)]
    reduce_scatter x3 -> x0, waiting for transfers between devices: 61.8 us -> none  [local(): lax.psum_scatter(partial_value, 'col', scatter_dimension=1, tiled=True)]
    all_gather x3 -> x1, waiting for transfers between devices: 57.1 us -> 8.51 us  [local(): full_coupling = lax.all_gather(coupling, 'col', axis=2, tiled=True)]
    all_gather x5 -> x1, blocking collectives: 30.7 us -> 5.29 us  [local(): small = lax.all_gather(small, 'col', axis=1, tiled=True)]
    dot_general x18 -> x31, matrix products: 25.9 us -> 7.36 us  [split_dot(): lax.dot_general(both, weights, (((1,), (contract,)), ((), ())), preferred...]
    ppermute x8 -> x14, starting transfers between devices: 24 us -> 41.9 us  [passed_along(): return lax.ppermute(shard, axis, pairs)]
    all_to_all x0 -> x1, blocking collectives: none -> 8.39 us  [local(): both = lax.all_to_all(both, 'col', split_axis=3, concat_axis=2, tiled=True)]
    all_to_all x1, waiting for transfers between devices: 3.89 us -> 0.01 us  [local(): lax.all_to_all(observed, 'col', split_axis=1, concat_axis=2, tiled=True)]
  transfers between devices with their start and end apart: 15 -> 16, of which waited for: 15 -> 15; matrix products, arithmetic and copies ran while one was open for 3% -> 2% of each run, Pallas kernels for 0% -> 0%
where the time goes in v1:
time: 151 us; the launch traced here: 150 us
  waiting for transfers between devices  55.9 us (37%)
  starting transfers between devices  46.2 us (31%)
  between operations  14.6 us (10%)
  blocking collectives  13.7 us (9%)
  local copies, waits for them, and re-layouts  8.34 us (6%)
  matrix products  7.36 us (5%)
  other arithmetic  3.76 us (2%)
    ppermute x14, waiting for transfers between devices, passed_along(): return lax.ppermute(shard, axis, pairs)  46.7 us
    ppermute x14, starting transfers between devices, passed_along(): return lax.ppermute(shard, axis, pairs)  41.9 us
    all_gather x1, waiting for transfers between devices, local(): full_coupling = lax.all_gather(coupling, 'col', axis=2, tiled=True)  8.51 us
    all_to_all x1, blocking collectives, local(): both = lax.all_to_all(both, 'col', split_axis=3, concat_axis=2, tiled=True)  8.39 us
    dot_general x31, matrix products, split_dot(): lax.dot_general(both, weights, (((1,), (contract,)), ((), ())), preferred...  7.36 us
    all_gather x1, blocking collectives, local(): small = lax.all_gather(small, 'col', axis=1, tiled=True)  5.29 us
    all_to_all x1, starting transfers between devices, local(): lax.all_to_all(observed, 'col', split_axis=1, concat_axis=2, tiled=True)  4.24 us
    unnamed x11, local copies, waits for them, and re-layouts  4.14 us
  transfers between devices with their start and end apart: 16, of which 15 were waited for; matrix products, arithmetic and copies ran while one was open for 2% of the time, Pallas kernels for 0%

profile of v1, /device:TPU:0, one launch (start us, length us, event | category | flops | bytes accessed | tf_op | source)
XLA Modules:
  0.0 149.8 jit_solution(448652533752614488)
XLA Ops:
  7.2 0.7 all-gather.2.cloned.1.call-update
  8.0 0.7 copy.10
  8.7 4.2 %all-to-all-start = ((bf16[2,128,128]{2,0,1:T(2,128)(2,1)}), bf16[2,128,128]{2,0,1:T(2,128)(2,1)S(1)}, u32[]{:S(2)}, u32[]{:S(2)}) async-start(bf16[2,128,128]{2,0,1:T(2,128)(2,1)} %copy.10), calls=%async_computation | async-start | bytes 131072 | tf_op jit(solution)/shard_map/all_to_all | solution.py:37
  12.9 0.7 copy-done.2
  13.6 5.3 %all_gather.7 = f32[3,512]{1,0:T(4,128)S(1)} all-gather(f32[3,128]{1,0:T(4,128)S(1)} %pad_maximum_fusion.1), channel_id=1, replica_groups=mesh['tm'=8,'col'=4] {'col'}, dimensions={1}, use_global_device_ids=true | all-gather | bytes 7680 | tf_op jit(solution)/shard_map/all_gather | solution.py:34
  18.9 0.7 copy-done.1
  19.8 0.6 mul.82
  20.6 8.5 %all-gather.2.cloned.1.call-done = bf16[2,512,512]{2,1,0:T(8,128)(2,1)} async-done(((bf16[2,512,128]{2,1,0:T(8,128)(2,1)}), bf16[2,512,512]{2,1,0:T(8,128)(2,1)}) %all-gather.2.cloned.1.call-update) | async-done | bytes 1048592 | tf_op jit(solution)/shard_map/all_gather | solution.py:32
  29.1 1.3 broadcast_multiply_fusion
  30.9 3.4 %collective-permute-start = (f32[32,512]{1,0:T(8,128)S(1)}, f32[32,512]{1,0:T(8,128)S(1)}, u32[]{:S(2)}, u32[]{:S(2)}) collective-permute-start(f32[32,512]{1,0:T(8,128)S(1)} %fusion.53), channel_id=1, source_target_pairs={{0,4},{4,8},{8,12},{12,16},{16,20},{20,24},{24,28},{1,5},{5,9},{9,... | collective-permute-start | bytes 196616 | tf_op jit(solution)/shard_map/ppermute | solution.py:10
  34.3 1.9 %collective-permute-done = f32[32,512]{1,0:T(8,128)S(1)} collective-permute-done((f32[32,512]{1,0:T(8,128)S(1)}, f32[32,512]{1,0:T(8,128)S(1)}, u32[]{:S(2)}, u32[]{:S(2)}) %collective-permute-start) | collective-permute-done | bytes 65568 | tf_op jit(solution)/shard_map/ppermute | solution.py:10
  36.7 4.3 %collective-permute-start.1 = (f32[32,512]{1,0:T(8,128)S(1)}, f32[32,512]{1,0:T(8,128)S(1)}, u32[]{:S(2)}, u32[]{:S(2)}) collective-permute-start(f32[32,512]{1,0:T(8,128)S(1)} %fusion.49), channel_id=1, source_target_pairs={{0,4},{4,8},{8,12},{12,16},{16,20},{20,24},{24,28},{1,5},{5,9},{9,... | collective-permute-start | bytes 196616 | tf_op jit(solution)/shard_map/ppermute | solution.py:10
  40.9 1.9 %collective-permute-done.1 = f32[32,512]{1,0:T(8,128)S(1)} collective-permute-done((f32[32,512]{1,0:T(8,128)S(1)}, f32[32,512]{1,0:T(8,128)S(1)}, u32[]{:S(2)}, u32[]{:S(2)}) %collective-permute-start.1) | collective-permute-done | bytes 65568 | tf_op jit(solution)/shard_map/ppermute | solution.py:10
  43.3 4.3 %collective-permute-start.2 = (f32[32,512]{1,0:T(8,128)S(1)}, f32[32,512]{1,0:T(8,128)S(1)}, u32[]{:S(2)}, u32[]{:S(2)}) collective-permute-start(f32[32,512]{1,0:T(8,128)S(1)} %fusion.45), channel_id=1, source_target_pairs={{0,4},{4,8},{8,12},{12,16},{16,20},{20,24},{24,28},{1,5},{5,9},{9,... | collective-permute-start | bytes 196616 | tf_op jit(solution)/shard_map/ppermute | solution.py:10
  47.6 1.9 %collective-permute-done.2 = f32[32,512]{1,0:T(8,128)S(1)} collective-permute-done((f32[32,512]{1,0:T(8,128)S(1)}, f32[32,512]{1,0:T(8,128)S(1)}, u32[]{:S(2)}, u32[]{:S(2)}) %collective-permute-start.2) | collective-permute-done | bytes 65568 | tf_op jit(solution)/shard_map/ppermute | solution.py:10
  50.0 5.2 %collective-permute-start.3 = (f32[32,512]{1,0:T(8,128)S(1)}, f32[32,512]{1,0:T(8,128)S(1)}, u32[]{:S(2)}, u32[]{:S(2)}) collective-permute-start(f32[32,512]{1,0:T(8,128)S(1)} %fusion.41), channel_id=1, source_target_pairs={{0,4},{4,8},{8,12},{12,16},{16,20},{20,24},{24,28},{1,5},{5,9},{9,... | collective-permute-start | bytes 196616 | tf_op jit(solution)/shard_map/ppermute | solution.py:10
  55.2 1.9 %collective-permute-done.3 = f32[32,512]{1,0:T(8,128)S(1)} collective-permute-done((f32[32,512]{1,0:T(8,128)S(1)}, f32[32,512]{1,0:T(8,128)S(1)}, u32[]{:S(2)}, u32[]{:S(2)}) %collective-permute-start.3) | collective-permute-done | bytes 65568 | tf_op jit(solution)/shard_map/ppermute | solution.py:10
  57.5 5.2 %collective-permute-start.4 = (f32[32,512]{1,0:T(8,128)S(1)}, f32[32,512]{1,0:T(8,128)S(1)}, u32[]{:S(2)}, u32[]{:S(2)}) collective-permute-start(f32[32,512]{1,0:T(8,128)S(1)} %fusion.37), channel_id=1, source_target_pairs={{0,4},{4,8},{8,12},{12,16},{16,20},{20,24},{24,28},{1,5},{5,9},{9,... | collective-permute-start | bytes 196616 | tf_op jit(solution)/shard_map/ppermute | solution.py:10
  62.7 1.9 %collective-permute-done.4 = f32[32,512]{1,0:T(8,128)S(1)} collective-permute-done((f32[32,512]{1,0:T(8,128)S(1)}, f32[32,512]{1,0:T(8,128)S(1)}, u32[]{:S(2)}, u32[]{:S(2)}) %collective-permute-start.4) | collective-permute-done | bytes 65568 | tf_op jit(solution)/shard_map/ppermute | solution.py:10
  65.1 5.2 %collective-permute-start.5 = (f32[32,512]{1,0:T(8,128)S(1)}, f32[32,512]{1,0:T(8,128)S(1)}, u32[]{:S(2)}, u32[]{:S(2)}) collective-permute-start(f32[32,512]{1,0:T(8,128)S(1)} %fusion.33), channel_id=1, source_target_pairs={{0,4},{4,8},{8,12},{12,16},{16,20},{20,24},{24,28},{1,5},{5,9},{9,... | collective-permute-start | bytes 196616 | tf_op jit(solution)/shard_map/ppermute | solution.py:10
  70.2 1.9 %collective-permute-done.5 = f32[32,512]{1,0:T(8,128)S(1)} collective-permute-done((f32[32,512]{1,0:T(8,128)S(1)}, f32[32,512]{1,0:T(8,128)S(1)}, u32[]{:S(2)}, u32[]{:S(2)}) %collective-permute-start.5) | collective-permute-done | bytes 65568 | tf_op jit(solution)/shard_map/ppermute | solution.py:10
  72.6 0.3 fusion.116
  73.2 1.3 collective-permute-start.7
  74.5 6.6 %collective-permute-done.7 = f32[32,512]{1,0:T(8,128)S(1)} collective-permute-done((f32[32,512]{1,0:T(8,128)S(1)}, f32[32,512]{1,0:T(8,128)S(1)}, u32[]{:S(2)}, u32[]{:S(2)}) %collective-permute-start.7) | collective-permute-done | bytes 65568 | tf_op jit(solution)/shard_map/ppermute | solution.py:10
  81.2 0.3 fusion.124
  81.5 0.3 fusion.128
  81.8 1.3 collective-permute-start.8
  83.1 5.7 %collective-permute-done.8 = f32[32,512]{1,0:T(8,128)S(1)} collective-permute-done((f32[32,512]{1,0:T(8,128)S(1)}, f32[32,512]{1,0:T(8,128)S(1)}, u32[]{:S(2)}, u32[]{:S(2)}) %collective-permute-start.8) | collective-permute-done | bytes 65568 | tf_op jit(solution)/shard_map/ppermute | solution.py:10
  89.4 1.3 collective-permute-start.9
  90.7 5.8 %collective-permute-done.9 = f32[32,512]{1,0:T(8,128)S(1)} collective-permute-done((f32[32,512]{1,0:T(8,128)S(1)}, f32[32,512]{1,0:T(8,128)S(1)}, u32[]{:S(2)}, u32[]{:S(2)}) %collective-permute-start.9) | collective-permute-done | bytes 65568 | tf_op jit(solution)/shard_map/ppermute | solution.py:10
  97.1 1.3 collective-permute-start.10
  98.4 5.8 %collective-permute-done.10 = f32[32,512]{1,0:T(8,128)S(1)} collective-permute-done((f32[32,512]{1,0:T(8,128)S(1)}, f32[32,512]{1,0:T(8,128)S(1)}, u32[]{:S(2)}, u32[]{:S(2)}) %collective-permute-start.10) | collective-permute-done | bytes 65568 | tf_op jit(solution)/shard_map/ppermute | solution.py:10
  104.8 1.3 collective-permute-start.11
  106.1 5.4 %collective-permute-start.6 = (f32[32,512]{1,0:T(8,128)S(1)}, f32[32,512]{1,0:T(8,128)S(1)}, u32[]{:S(2)}, u32[]{:S(2)}) collective-permute-start(f32[32,512]{1,0:T(8,128)S(1)} %get-tuple-element.82), channel_id=1, source_target_pairs={{0,4},{4,8},{8,12},{12,16},{16,20},{20,24},{24,28},{1,5},{5,9},{9,... | collective-permute-start | bytes 196616 | tf_op jit(solution)/shard_map/ppermute | solution.py:10
  111.6 0.3 collective-permute-done.11
  112.5 1.3 collective-permute-start.12
  114.1 5.5 %collective-permute-done.12 = f32[32,512]{1,0:T(8,128)S(1)} collective-permute-done((f32[32,512]{1,0:T(8,128)S(1)}, f32[32,512]{1,0:T(8,128)S(1)}, u32[]{:S(2)}, u32[]{:S(2)}) %collective-permute-start.12) | collective-permute-done | bytes 65568 | tf_op jit(solution)/shard_map/ppermute | solution.py:10
  120.2 1.3 collective-permute-start.13
  121.7 5.5 %collective-permute-done.13 = f32[32,512]{1,0:T(8,128)S(1)} collective-permute-done((f32[32,512]{1,0:T(8,128)S(1)}, f32[32,512]{1,0:T(8,128)S(1)}, u32[]{:S(2)}, u32[]{:S(2)}) %collective-permute-start.13) | collective-permute-done | bytes 65568 | tf_op jit(solution)/shard_map/ppermute | solution.py:10
  127.9 0.7 copy.12
  128.7 1.1 reshape.17
  129.7 8.4 %all_to_all.24 = f32[4,1,16384]{2,1,0:T(1,128)S(1)} all-to-all(f32[4,1,16384]{2,1,0:T(1,128)S(1)} %reshape.17), channel_id=1, replica_groups=mesh['tm'=8,'col'=4] {'col'}, dimensions={0} | all-to-all | bytes 524288 | tf_op jit(solution)/shard_map/all_to_all | solution.py:82
  138.1 0.5 broadcast.3
  138.6 1.4 reduce
  140.0 0.9 reshape.18
  140.9 0.4 fusion.248
  141.3 0.8 copy.13
  142.2 0.8 copy.14
  (91 shorter events, 8.3 us)
Async XLA Ops:
  7.2 0.8 copy-start
  7.2 21.9 %all-gather.2.cloned.1.call-start = ((), (), s32[]{:S(2)}) async-start(), calls=%async_computation.2 | async-start | bytes 1310720 | tf_op jit(solution)/shard_map/all_gather | solution.py:32
  8.7 11.7 %all-to-all-start = ((bf16[2,128,128]{2,0,1:T(2,128)(2,1)}), bf16[2,128,128]{2,0,1:T(2,128)(2,1)S(1)}, u32[]{:S(2)}, u32[]{:S(2)}) async-start(bf16[2,128,128]{2,0,1:T(2,128)(2,1)} %copy.10), calls=%async_computation | async-start | bytes 131072 | tf_op jit(solution)/shard_map/all_to_all | solution.py:37
  12.9 0.7 copy-start.2
  12.9 0.7 copy-start.3
  18.9 0.7 copy-start.1
  30.9 5.3 %collective-permute-start = (f32[32,512]{1,0:T(8,128)S(1)}, f32[32,512]{1,0:T(8,128)S(1)}, u32[]{:S(2)}, u32[]{:S(2)}) collective-permute-start(f32[32,512]{1,0:T(8,128)S(1)} %fusion.53), channel_id=1, source_target_pairs={{0,4},{4,8},{8,12},{12,16},{16,20},{20,24},{24,28},{1,5},{5,9},{9,... | collective-permute-start | bytes 196616 | tf_op jit(solution)/shard_map/ppermute | solution.py:10
  36.7 6.2 %collective-permute-start.1 = (f32[32,512]{1,0:T(8,128)S(1)}, f32[32,512]{1,0:T(8,128)S(1)}, u32[]{:S(2)}, u32[]{:S(2)}) collective-permute-start(f32[32,512]{1,0:T(8,128)S(1)} %fusion.49), channel_id=1, source_target_pairs={{0,4},{4,8},{8,12},{12,16},{16,20},{20,24},{24,28},{1,5},{5,9},{9,... | collective-permute-start | bytes 196616 | tf_op jit(solution)/shard_map/ppermute | solution.py:10
  43.3 6.2 %collective-permute-start.2 = (f32[32,512]{1,0:T(8,128)S(1)}, f32[32,512]{1,0:T(8,128)S(1)}, u32[]{:S(2)}, u32[]{:S(2)}) collective-permute-start(f32[32,512]{1,0:T(8,128)S(1)} %fusion.45), channel_id=1, source_target_pairs={{0,4},{4,8},{8,12},{12,16},{16,20},{20,24},{24,28},{1,5},{5,9},{9,... | collective-permute-start | bytes 196616 | tf_op jit(solution)/shard_map/ppermute | solution.py:10
  50.0 7.1 %collective-permute-start.3 = (f32[32,512]{1,0:T(8,128)S(1)}, f32[32,512]{1,0:T(8,128)S(1)}, u32[]{:S(2)}, u32[]{:S(2)}) collective-permute-start(f32[32,512]{1,0:T(8,128)S(1)} %fusion.41), channel_id=1, source_target_pairs={{0,4},{4,8},{8,12},{12,16},{16,20},{20,24},{24,28},{1,5},{5,9},{9,... | collective-permute-start | bytes 196616 | tf_op jit(solution)/shard_map/ppermute | solution.py:10
  57.5 7.1 %collective-permute-start.4 = (f32[32,512]{1,0:T(8,128)S(1)}, f32[32,512]{1,0:T(8,128)S(1)}, u32[]{:S(2)}, u32[]{:S(2)}) collective-permute-start(f32[32,512]{1,0:T(8,128)S(1)} %fusion.37), channel_id=1, source_target_pairs={{0,4},{4,8},{8,12},{12,16},{16,20},{20,24},{24,28},{1,5},{5,9},{9,... | collective-permute-start | bytes 196616 | tf_op jit(solution)/shard_map/ppermute | solution.py:10
  65.1 7.1 %collective-permute-start.5 = (f32[32,512]{1,0:T(8,128)S(1)}, f32[32,512]{1,0:T(8,128)S(1)}, u32[]{:S(2)}, u32[]{:S(2)}) collective-permute-start(f32[32,512]{1,0:T(8,128)S(1)} %fusion.33), channel_id=1, source_target_pairs={{0,4},{4,8},{8,12},{12,16},{16,20},{20,24},{24,28},{1,5},{5,9},{9,... | collective-permute-start | bytes 196616 | tf_op jit(solution)/shard_map/ppermute | solution.py:10
  73.2 7.9 %collective-permute-start.7 = (f32[32,512]{1,0:T(8,128)S(1)}, f32[32,512]{1,0:T(8,128)S(1)}, u32[]{:S(2)}, u32[]{:S(2)}) collective-permute-start(f32[32,512]{1,0:T(8,128)S(1)} %fusion.21), channel_id=1, source_target_pairs={{4,0},{8,4},{12,8},{16,12},{20,16},{24,20},{28,24},{5,1},{9,5},{13... | collective-permute-start | bytes 196616 | tf_op jit(solution)/shard_map/ppermute | solution.py:10
  81.8 7.0 %collective-permute-start.8 = (f32[32,512]{1,0:T(8,128)S(1)}, f32[32,512]{1,0:T(8,128)S(1)}, u32[]{:S(2)}, u32[]{:S(2)}) collective-permute-start(f32[32,512]{1,0:T(8,128)S(1)} %fusion.18), channel_id=1, source_target_pairs={{4,0},{8,4},{12,8},{16,12},{20,16},{24,20},{28,24},{5,1},{9,5},{13... | collective-permute-start | bytes 196616 | tf_op jit(solution)/shard_map/ppermute | solution.py:10
  89.4 7.1 %collective-permute-start.9 = (f32[32,512]{1,0:T(8,128)S(1)}, f32[32,512]{1,0:T(8,128)S(1)}, u32[]{:S(2)}, u32[]{:S(2)}) collective-permute-start(f32[32,512]{1,0:T(8,128)S(1)} %fusion.15), channel_id=1, source_target_pairs={{4,0},{8,4},{12,8},{16,12},{20,16},{24,20},{28,24},{5,1},{9,5},{13... | collective-permute-start | bytes 196616 | tf_op jit(solution)/shard_map/ppermute | solution.py:10
  97.1 7.1 %collective-permute-start.10 = (f32[32,512]{1,0:T(8,128)S(1)}, f32[32,512]{1,0:T(8,128)S(1)}, u32[]{:S(2)}, u32[]{:S(2)}) collective-permute-start(f32[32,512]{1,0:T(8,128)S(1)} %fusion.12), channel_id=1, source_target_pairs={{4,0},{8,4},{12,8},{16,12},{20,16},{24,20},{28,24},{5,1},{9,5},{13... | collective-permute-start | bytes 196616 | tf_op jit(solution)/shard_map/ppermute | solution.py:10
  104.8 7.1 %collective-permute-start.11 = (f32[32,512]{1,0:T(8,128)S(1)}, f32[32,512]{1,0:T(8,128)S(1)}, u32[]{:S(2)}, u32[]{:S(2)}) collective-permute-start(f32[32,512]{1,0:T(8,128)S(1)} %fusion.9), channel_id=1, source_target_pairs={{4,0},{8,4},{12,8},{16,12},{20,16},{24,20},{28,24},{5,1},{9,5},{13... | collective-permute-start | bytes 196616 | tf_op jit(solution)/shard_map/ppermute | solution.py:10
  106.1 7.9 %collective-permute-start.6 = (f32[32,512]{1,0:T(8,128)S(1)}, f32[32,512]{1,0:T(8,128)S(1)}, u32[]{:S(2)}, u32[]{:S(2)}) collective-permute-start(f32[32,512]{1,0:T(8,128)S(1)} %get-tuple-element.82), channel_id=1, source_target_pairs={{0,4},{4,8},{8,12},{12,16},{16,20},{20,24},{24,28},{1,5},{5,9},{9,... | collective-permute-start | bytes 196616 | tf_op jit(solution)/shard_map/ppermute | solution.py:10
  112.5 7.1 %collective-permute-start.12 = (f32[32,512]{1,0:T(8,128)S(1)}, f32[32,512]{1,0:T(8,128)S(1)}, u32[]{:S(2)}, u32[]{:S(2)}) collective-permute-start(f32[32,512]{1,0:T(8,128)S(1)} %fusion.6), channel_id=1, source_target_pairs={{4,0},{8,4},{12,8},{16,12},{20,16},{24,20},{28,24},{5,1},{9,5},{13... | collective-permute-start | bytes 196616 | tf_op jit(solution)/shard_map/ppermute | solution.py:10
  120.2 7.1 %collective-permute-start.13 = (f32[32,512]{1,0:T(8,128)S(1)}, f32[32,512]{1,0:T(8,128)S(1)}, u32[]{:S(2)}, u32[]{:S(2)}) collective-permute-start(f32[32,512]{1,0:T(8,128)S(1)} %fusion.3), channel_id=1, source_target_pairs={{4,0},{8,4},{12,8},{16,12},{20,16},{24,20},{28,24},{5,1},{9,5},{13... | collective-permute-start | bytes 196616 | tf_op jit(solution)/shard_map/ppermute | solution.py:10
Sparse Core Ops, SparseCore 0:
  9.5 19.5 all-gather.1

commit v2 on v1

--- a/solution.py
+++ b/solution.py
@@ -10,10 +10,14 @@
     return lax.ppermute(shard, axis, pairs)
 
 
+def bf16_part(value):
+    return lax.reduce_precision(value, exponent_bits=8, mantissa_bits=7)
+
+
 def split_dot(state, weights, transposed):
-    high = state.astype(jnp.bfloat16)
-    low = (state - high.astype(jnp.float32)).astype(jnp.bfloat16)
-    both = jnp.concatenate([high, low], axis=0)
+    high = bf16_part(state)
+    low = state - high
+    both = jnp.concatenate([high, low], axis=0).astype(jnp.bfloat16)
     contract = 1 if transposed else 0
     prod = lax.dot_general(
         both, weights, (((1,), (contract,)), ((), ())), preferred_element_type=jnp.float32
@@ -22,19 +26,57 @@
     return prod[:rows] + prod[rows:]
 
 
+def three_pieces(value):
+    high = bf16_part(value)
+    rest = value - high
+    mid = bf16_part(rest)
+    return jnp.stack([high, mid, rest - mid]).astype(jnp.bfloat16)
+
+
 def local(observed, input_gain, persist, coupling, pattern):
-    step_count = observed.shape[0]
+    step_count, rows, cols = observed.shape
     state_width = coupling.shape[1]
     block_count = pattern.shape[0]
     block_size = state_width // block_count
     time_groups = lax.axis_size("tm")
+    col_groups = lax.axis_size("col")
+    own_rows = rows // col_groups
 
-    full_coupling = lax.all_gather(coupling, "col", axis=2, tiled=True)
     small = jnp.concatenate([persist, input_gain[None]], axis=0)
-    small = lax.all_gather(small, "col", axis=1, tiled=True)
+    small_pieces = three_pieces(small).reshape(-1)
+    coupling_flat = coupling.reshape(-1)
+    seen_parts = observed.reshape(step_count, col_groups, own_rows, cols).transpose(1, 0, 2, 3)
+    packet = jnp.concatenate(
+        [
+            jnp.broadcast_to(coupling_flat[None], (col_groups,) + coupling_flat.shape),
+            seen_parts.reshape(col_groups, -1),
+            jnp.broadcast_to(small_pieces[None], (col_groups,) + small_pieces.shape),
+        ],
+        axis=1,
+    )
+    packet = lax.all_to_all(packet, "col", split_axis=0, concat_axis=0, tiled=True)
+    n_coupling = coupling_flat.shape[0]
+    n_seen = step_count * own_rows * cols
+    full_coupling = (
+        packet[:, :n_coupling]
+        .reshape(col_groups, step_count, state_width, cols)
+        .transpose(1, 2, 0, 3)
+        .reshape(step_count, state_width, state_width)
+    )
+    seen = (
+        packet[:, n_coupling : n_coupling + n_seen]
+        .reshape(col_groups, step_count, own_rows, cols)
+        .transpose(1, 2, 0, 3)
+        .reshape(step_count, own_rows, state_width)
+    )
+    small = (
+        packet[:, n_coupling + n_seen :]
+        .astype(jnp.float32)
+        .reshape(col_groups, 3, step_count + 1, cols)
+    )
+    small = (small[:, 0] + small[:, 1] + small[:, 2]).transpose(1, 0, 2).reshape(step_count + 1, state_width)
     diag = small[:step_count]
     gain = small[step_count]
-    seen = lax.all_to_all(observed, "col", split_axis=1, concat_axis=2, tiled=True)
 
     mask = jnp.broadcast_to(
         pattern.astype(jnp.bfloat16)[:, None, :, None],
@@ -64,7 +106,9 @@
         x_in, e_in = carry
         xs = forward(x_in)
         _, e_out = backward(e_in)
-        return passed_along(xs[-1], "tm", 1), passed_along(e_out, "tm", -1)
+        x_out, e_out = lax.optimization_barrier((xs[-1], e_out))
+        sent = (passed_along(x_out, "tm", 1), passed_along(e_out, "tm", -1))
+        return lax.optimization_barrier(sent)
 
     zeros = jnp.zeros(driven.shape[1:], jnp.float32)
     carry = (zeros, zeros)
@@ -79,7 +123,9 @@
     filtered = jnp.stack(xs)
     smoothed = jnp.stack([x + e for x, e in zip(xs, es)])
     both = jnp.stack([filtered, smoothed])
-    both = lax.all_to_all(both, "col", split_axis=3, concat_axis=2, tiled=True)
+    both = both.reshape(2, step_count, own_rows, col_groups, cols).transpose(3, 0, 1, 2, 4)
+    both = lax.all_to_all(both, "col", split_axis=0, concat_axis=0, tiled=True)
+    both = both.transpose(1, 2, 0, 3, 4).reshape(2, step_count, rows, cols)
     return both[0], both[1]
 
 

time: 151 us -> 138 us (0.914)
  between operations: 14.6 us -> 1.45 us
  other arithmetic: 3.76 us -> 15.5 us
  waiting for transfers between devices: 55.9 us -> 47.7 us
  local copies, waits for them, and re-layouts: 8.34 us -> 14.8 us
  blocking collectives: 13.7 us -> 8.39 us
  starting transfers between devices: 46.2 us -> 41.7 us
    all_to_all x1, waiting for transfers between devices: 0.01 us -> 13.6 us  [local(): lax.all_to_all(packet, 'col', split_axis=0, concat_axis=0, tiled=True)]
    ppermute x14, waiting for transfers between devices: 46.7 us -> 34.1 us  [passed_along(): return lax.ppermute(shard, axis, pairs)]
    all_to_all x1 -> x2, other arithmetic: 1.37 us -> 13.5 us  [local(): lax.all_to_all(packet, 'col', split_axis=0, concat_axis=0, tiled=True)]
    all_gather x1 -> x0, waiting for transfers between devices: 8.51 us -> none  [local(): full_coupling = lax.all_gather(coupling, 'col', axis=2, tiled=True)]
    all_gather x1 -> x0, blocking collectives: 5.29 us -> none  [local(): small = lax.all_gather(small, 'col', axis=1, tiled=True)]
    unnamed x11 -> x10, local copies, waits for them, and re-layouts: 4.14 us -> 9.23 us
    ppermute x14, starting transfers between devices: 41.9 us -> 37.3 us  [passed_along(): return lax.ppermute(shard, axis, pairs)]
  transfers between devices with their start and end apart: 16 -> 15, of which waited for: 15 -> 15; matrix products, arithmetic and copies ran while one was open for 2% -> 1% of each run, Pallas kernels for 0% -> 0%
where the time goes in v2:
time: 138 us; the launch traced here: 137 us
  waiting for transfers between devices  47.7 us (35%)
  starting transfers between devices  41.7 us (30%)
  other arithmetic  15.5 us (11%)
  local copies, waits for them, and re-layouts  14.8 us (11%)
  blocking collectives  8.39 us (6%)
  matrix products  7.44 us (5%)
  between operations  1.45 us (1%)
    ppermute x14, starting transfers between devices, passed_along(): return lax.ppermute(shard, axis, pairs)  37.3 us
    ppermute x14, waiting for transfers between devices, passed_along(): return lax.ppermute(shard, axis, pairs)  34.1 us
    all_to_all x1, waiting for transfers between devices, local(): lax.all_to_all(packet, 'col', split_axis=0, concat_axis=0, tiled=True)  13.6 us
    all_to_all x2, other arithmetic, local(): lax.all_to_all(packet, 'col', split_axis=0, concat_axis=0, tiled=True)  13.5 us
    unnamed x10, local copies, waits for them, and re-layouts  9.23 us
    all_to_all x1, blocking collectives, local(): both = lax.all_to_all(both, 'col', split_axis=0, concat_axis=0, tiled=True)  8.39 us
    dot_general x31, matrix products, split_dot(): lax.dot_general(both, weights, (((1,), (contract,)), ((), ())), preferred...  7.44 us
    all_to_all x1, starting transfers between devices, local(): lax.all_to_all(packet, 'col', split_axis=0, concat_axis=0, tiled=True)  4.37 us
  transfers between devices with their start and end apart: 15, of which 15 were waited for; matrix products, arithmetic and copies ran while one was open for 1% of the time, Pallas kernels for 0%

profile of v2, /device:TPU:0, one launch (start us, length us, event | category | flops | bytes accessed | tf_op | source)
XLA Modules:
  0.0 136.9 jit_solution(1275068306583109217)
XLA Ops:
  0.6 0.8 copy.28
  1.5 0.7 reduce-precision_convert_fusion.31
  2.3 1.0 pad.65.clone
  3.3 7.8 %maximum_bitcast_fusion = bf16[4,1,140416]{2,0,1:T(4,128)(2,1)S(1)} fusion(bf16[4,8192]{1,0:T(4,128)(2,1)S(1)} %bitcast.228, bf16[140416]{0:T(1024)(128)(2,1)S(1)} %pad.67.clone, bf16[140416]{0:T(1024)(128)(2,1)S(1)} %pad.65.clone), kind=kLoop, calls=%fused_computation | loop fusion | flops 3369984 | bytes 1750528 | tf_op jit(solution)/shard_map/all_to_all | solution.py:57
  11.1 0.5 broadcast.18
  11.6 5.7 %reduce = bf16[4,140416]{1,0:T(4,128)(2,1)S(1)} reduce(bf16[4,1,140416]{2,0,1:T(4,128)(2,1)S(1)} %maximum_bitcast_fusion, bf16[]{:T(256)} %broadcast.18), dimensions={1}, to_apply=%copy.29.reduce_sub_computation | reduce | bytes 2246658 | tf_op jit(solution)/shard_map/all_to_all | solution.py:57
  17.3 2.4 %reshape.176 = bf16[4,2,70208]{2,1,0:T(2,128)(2,1)} reshape(bf16[4,140416]{1,0:T(4,128)(2,1)S(1)} %reduce) | data formatting | bytes 2246656
  19.7 4.4 %all-to-all-start = ((bf16[4,2,70208]{2,1,0:T(2,128)(2,1)}), bf16[4,2,70208]{2,1,0:T(2,128)(2,1)S(1)}, u32[]{:S(2)}, u32[]{:S(2)}) async-start(bf16[4,2,70208]{2,1,0:T(2,128)(2,1)} %reshape.176), calls=%async_computation | async-start | bytes 2248704 | tf_op jit(solution)/shard_map/all_to_all | solution.py:57
  24.4 1.4 %mul.82 = bf16[512,512]{0,1:T(8,128)(2,1)} reshape(bf16[8,64,8,64]{1,0,3,2:T(8,128)(2,1)S(1)} %broadcast_in_dim.28) | data formatting | bytes 1048576 | tf_op jit(solution)/shard_map/mul | solution.py:85
  25.8 13.6 %all-to-all-done = bf16[4,2,70208]{2,1,0:T(2,128)(2,1)S(1)} async-done(((bf16[4,2,70208]{2,1,0:T(2,128)(2,1)}), bf16[4,2,70208]{2,1,0:T(2,128)(2,1)S(1)}, u32[]{:S(2)}, u32[]{:S(2)}) %all-to-all-start) | async-done | bytes 1123360 | tf_op jit(solution)/shard_map/all_to_all | solution.py:57
  39.4 4.3 %reshape.177 = bf16[4,1,140416]{2,1,0:T(2,128)(2,1)S(1)} reshape(bf16[4,2,70208]{2,1,0:T(2,128)(2,1)S(1)} %all-to-all-done) | data formatting | bytes 2246656
  43.7 1.5 %copy.44 = bf16[4,1,140416]{2,0,1:T(4,128)(2,1)S(1)} copy(bf16[4,1,140416]{2,1,0:T(2,128)(2,1)S(1)} %reshape.177) | data formatting | bytes 2246656
  45.3 0.4 slice_bitcast_fusion
  45.9 0.5 copy.30
  46.5 0.5 copy-done
  47.6 0.3 fusion.85
  48.2 4.1 %collective-permute-start = (f32[32,512]{1,0:T(8,128)S(1)}, f32[32,512]{1,0:T(8,128)S(1)}, u32[]{:S(2)}, u32[]{:S(2)}) collective-permute-start(f32[32,512]{1,0:T(8,128)S(1)} %get-tuple-element.30), channel_id=1, source_target_pairs={{0,4},{4,8},{8,12},{12,16},{16,20},{20,24},{24,28},{1,5},{5,9},{9,... | collective-permute-start | bytes 196616 | tf_op jit(solution)/shard_map/ppermute | solution.py:10
  52.3 1.3 collective-permute-start.1
  53.6 0.6 collective-permute-done
  54.2 4.3 %collective-permute-done.1 = f32[32,512]{1,0:T(8,128)S(1)} collective-permute-done((f32[32,512]{1,0:T(8,128)S(1)}, f32[32,512]{1,0:T(8,128)S(1)}, u32[]{:S(2)}, u32[]{:S(2)}) %collective-permute-start.1) | collective-permute-done | bytes 65568 | tf_op jit(solution)/shard_map/ppermute | solution.py:10
  59.6 4.3 %collective-permute-start.2 = (f32[32,512]{1,0:T(8,128)S(1)}, f32[32,512]{1,0:T(8,128)S(1)}, u32[]{:S(2)}, u32[]{:S(2)}) collective-permute-start(f32[32,512]{1,0:T(8,128)S(1)} %get-tuple-element.34), channel_id=1, source_target_pairs={{0,4},{4,8},{8,12},{12,16},{16,20},{20,24},{24,28},{1,5},{5,9},{9,... | collective-permute-start | bytes 196616 | tf_op jit(solution)/shard_map/ppermute | solution.py:10
  63.9 1.3 collective-permute-start.3
  65.2 1.2 collective-permute-done.2
  66.4 3.7 %collective-permute-done.3 = f32[32,512]{1,0:T(8,128)S(1)} collective-permute-done((f32[32,512]{1,0:T(8,128)S(1)}, f32[32,512]{1,0:T(8,128)S(1)}, u32[]{:S(2)}, u32[]{:S(2)}) %collective-permute-start.3) | collective-permute-done | bytes 65568 | tf_op jit(solution)/shard_map/ppermute | solution.py:10
  70.7 0.3 fusion.117
  71.3 3.4 %collective-permute-start.4 = (f32[32,512]{1,0:T(8,128)S(1)}, f32[32,512]{1,0:T(8,128)S(1)}, u32[]{:S(2)}, u32[]{:S(2)}) collective-permute-start(f32[32,512]{1,0:T(8,128)S(1)} %get-tuple-element.38), channel_id=1, source_target_pairs={{0,4},{4,8},{8,12},{12,16},{16,20},{20,24},{24,28},{1,5},{5,9},{9,... | collective-permute-start | bytes 196616 | tf_op jit(solution)/shard_map/ppermute | solution.py:10
  74.7 1.3 collective-permute-start.5
  76.0 1.2 collective-permute-done.4
  77.2 3.7 %collective-permute-done.5 = f32[32,512]{1,0:T(8,128)S(1)} collective-permute-done((f32[32,512]{1,0:T(8,128)S(1)}, f32[32,512]{1,0:T(8,128)S(1)}, u32[]{:S(2)}, u32[]{:S(2)}) %collective-permute-start.5) | collective-permute-done | bytes 65568 | tf_op jit(solution)/shard_map/ppermute | solution.py:10
  81.4 0.3 fusion.133
  82.0 4.3 %collective-permute-start.6 = (f32[32,512]{1,0:T(8,128)S(1)}, f32[32,512]{1,0:T(8,128)S(1)}, u32[]{:S(2)}, u32[]{:S(2)}) collective-permute-start(f32[32,512]{1,0:T(8,128)S(1)} %get-tuple-element.42), channel_id=1, source_target_pairs={{0,4},{4,8},{8,12},{12,16},{16,20},{20,24},{24,28},{1,5},{5,9},{9,... | collective-permute-start | bytes 196616 | tf_op jit(solution)/shard_map/ppermute | solution.py:10
  86.4 1.3 collective-permute-start.7
  87.7 0.6 collective-permute-done.6
  88.2 4.3 %collective-permute-done.7 = f32[32,512]{1,0:T(8,128)S(1)} collective-permute-done((f32[32,512]{1,0:T(8,128)S(1)}, f32[32,512]{1,0:T(8,128)S(1)}, u32[]{:S(2)}, u32[]{:S(2)}) %collective-permute-start.7) | collective-permute-done | bytes 65568 | tf_op jit(solution)/shard_map/ppermute | solution.py:10
  93.7 3.5 %collective-permute-start.8 = (f32[32,512]{1,0:T(8,128)S(1)}, f32[32,512]{1,0:T(8,128)S(1)}, u32[]{:S(2)}, u32[]{:S(2)}) collective-permute-start(f32[32,512]{1,0:T(8,128)S(1)} %get-tuple-element.46), channel_id=1, source_target_pairs={{0,4},{4,8},{8,12},{12,16},{16,20},{20,24},{24,28},{1,5},{5,9},{9,... | collective-permute-start | bytes 196616 | tf_op jit(solution)/shard_map/ppermute | solution.py:10
  97.1 1.3 collective-permute-start.9
  98.4 0.6 collective-permute-done.8
  99.0 4.3 %collective-permute-done.9 = f32[32,512]{1,0:T(8,128)S(1)} collective-permute-done((f32[32,512]{1,0:T(8,128)S(1)}, f32[32,512]{1,0:T(8,128)S(1)}, u32[]{:S(2)}, u32[]{:S(2)}) %collective-permute-start.9) | collective-permute-done | bytes 65568 | tf_op jit(solution)/shard_map/ppermute | solution.py:10
  104.5 4.3 %collective-permute-start.10 = (f32[32,512]{1,0:T(8,128)S(1)}, f32[32,512]{1,0:T(8,128)S(1)}, u32[]{:S(2)}, u32[]{:S(2)}) collective-permute-start(f32[32,512]{1,0:T(8,128)S(1)} %get-tuple-element.50), channel_id=1, source_target_pairs={{0,4},{4,8},{8,12},{12,16},{16,20},{20,24},{24,28},{1,5},{5,9},{9,... | collective-permute-start | bytes 196616 | tf_op jit(solution)/shard_map/ppermute | solution.py:10
  108.8 1.3 collective-permute-start.11
  110.1 0.6 collective-permute-done.10
  110.6 4.3 %collective-permute-done.11 = f32[32,512]{1,0:T(8,128)S(1)} collective-permute-done((f32[32,512]{1,0:T(8,128)S(1)}, f32[32,512]{1,0:T(8,128)S(1)}, u32[]{:S(2)}, u32[]{:S(2)}) %collective-permute-start.11) | collective-permute-done | bytes 65568 | tf_op jit(solution)/shard_map/ppermute | solution.py:10
  116.1 4.4 %collective-permute-start.12 = (f32[32,512]{1,0:T(8,128)S(1)}, f32[32,512]{1,0:T(8,128)S(1)}, u32[]{:S(2)}, u32[]{:S(2)}) collective-permute-start(f32[32,512]{1,0:T(8,128)S(1)} %get-tuple-element.54), channel_id=1, source_target_pairs={{0,4},{4,8},{8,12},{12,16},{16,20},{20,24},{24,28},{1,5},{5,9},{9,... | collective-permute-start | bytes 196616 | tf_op jit(solution)/shard_map/ppermute | solution.py:10
  120.5 1.3 collective-permute-start.13
  121.8 0.6 collective-permute-done.12
  122.4 4.3 %collective-permute-done.13 = f32[32,512]{1,0:T(8,128)S(1)} collective-permute-done((f32[32,512]{1,0:T(8,128)S(1)}, f32[32,512]{1,0:T(8,128)S(1)}, u32[]{:S(2)}, u32[]{:S(2)}) %collective-permute-start.13) | collective-permute-done | bytes 65568 | tf_op jit(solution)/shard_map/ppermute | solution.py:10
  127.8 8.4 %all_to_all.17 = f32[4,2,2,32,128]{4,3,2,1,0:T(8,128)S(1)} all-to-all(f32[4,2,2,32,128]{4,3,2,1,0:T(8,128)S(1)} %maximum_bitcast_fusion.1), channel_id=1, replica_groups=mesh['tm'=8,'col'=4] {'col'}, dimensions={0} | all-to-all | bytes 524288 | tf_op jit(solution)/shard_map/all_to_all | solution.py:127
  136.2 0.7 fusion.263
  (106 shorter events, 8.7 us)
Async XLA Ops:
  19.7 4.4 %copy-start.1 = (s32[8,8]{1,0:T(8,128)S(1)}, s32[8,8]{1,0:T(8,128)}, u32[]{:S(2)}) copy-start(s32[8,8]{1,0:T(8,128)} %param.9) | copy-start | bytes 772
  19.7 19.7 %all-to-all-start = ((bf16[4,2,70208]{2,1,0:T(2,128)(2,1)}), bf16[4,2,70208]{2,1,0:T(2,128)(2,1)S(1)}, u32[]{:S(2)}, u32[]{:S(2)}) async-start(bf16[4,2,70208]{2,1,0:T(2,128)(2,1)} %reshape.176), calls=%async_computation | async-start | bytes 2248704 | tf_op jit(solution)/shard_map/all_to_all | solution.py:57
  45.9 1.0 copy-start
  48.2 6.0 %collective-permute-start = (f32[32,512]{1,0:T(8,128)S(1)}, f32[32,512]{1,0:T(8,128)S(1)}, u32[]{:S(2)}, u32[]{:S(2)}) collective-permute-start(f32[32,512]{1,0:T(8,128)S(1)} %get-tuple-element.30), channel_id=1, source_target_pairs={{0,4},{4,8},{8,12},{12,16},{16,20},{20,24},{24,28},{1,5},{5,9},{9,... | collective-permute-start | bytes 196616 | tf_op jit(solution)/shard_map/ppermute | solution.py:10
  52.3 6.2 %collective-permute-start.1 = (f32[32,512]{1,0:T(8,128)S(1)}, f32[32,512]{1,0:T(8,128)S(1)}, u32[]{:S(2)}, u32[]{:S(2)}) collective-permute-start(f32[32,512]{1,0:T(8,128)S(1)} %fusion.78), channel_id=1, source_target_pairs={{4,0},{8,4},{12,8},{16,12},{20,16},{24,20},{28,24},{5,1},{9,5},{13... | collective-permute-start | bytes 196616 | tf_op jit(solution)/shard_map/ppermute | solution.py:10
  59.6 6.8 %collective-permute-start.2 = (f32[32,512]{1,0:T(8,128)S(1)}, f32[32,512]{1,0:T(8,128)S(1)}, u32[]{:S(2)}, u32[]{:S(2)}) collective-permute-start(f32[32,512]{1,0:T(8,128)S(1)} %get-tuple-element.34), channel_id=1, source_target_pairs={{0,4},{4,8},{8,12},{12,16},{16,20},{20,24},{24,28},{1,5},{5,9},{9,... | collective-permute-start | bytes 196616 | tf_op jit(solution)/shard_map/ppermute | solution.py:10
  63.9 6.2 %collective-permute-start.3 = (f32[32,512]{1,0:T(8,128)S(1)}, f32[32,512]{1,0:T(8,128)S(1)}, u32[]{:S(2)}, u32[]{:S(2)}) collective-permute-start(f32[32,512]{1,0:T(8,128)S(1)} %fusion.71), channel_id=1, source_target_pairs={{4,0},{8,4},{12,8},{16,12},{20,16},{24,20},{28,24},{5,1},{9,5},{13... | collective-permute-start | bytes 196616 | tf_op jit(solution)/shard_map/ppermute | solution.py:10
  71.3 5.9 %collective-permute-start.4 = (f32[32,512]{1,0:T(8,128)S(1)}, f32[32,512]{1,0:T(8,128)S(1)}, u32[]{:S(2)}, u32[]{:S(2)}) collective-permute-start(f32[32,512]{1,0:T(8,128)S(1)} %get-tuple-element.38), channel_id=1, source_target_pairs={{0,4},{4,8},{8,12},{12,16},{16,20},{20,24},{24,28},{1,5},{5,9},{9,... | collective-permute-start | bytes 196616 | tf_op jit(solution)/shard_map/ppermute | solution.py:10
  74.7 6.2 %collective-permute-start.5 = (f32[32,512]{1,0:T(8,128)S(1)}, f32[32,512]{1,0:T(8,128)S(1)}, u32[]{:S(2)}, u32[]{:S(2)}) collective-permute-start(f32[32,512]{1,0:T(8,128)S(1)} %fusion.64), channel_id=1, source_target_pairs={{4,0},{8,4},{12,8},{16,12},{20,16},{24,20},{28,24},{5,1},{9,5},{13... | collective-permute-start | bytes 196616 | tf_op jit(solution)/shard_map/ppermute | solution.py:10
  82.0 6.2 %collective-permute-start.6 = (f32[32,512]{1,0:T(8,128)S(1)}, f32[32,512]{1,0:T(8,128)S(1)}, u32[]{:S(2)}, u32[]{:S(2)}) collective-permute-start(f32[32,512]{1,0:T(8,128)S(1)} %get-tuple-element.42), channel_id=1, source_target_pairs={{0,4},{4,8},{8,12},{12,16},{16,20},{20,24},{24,28},{1,5},{5,9},{9,... | collective-permute-start | bytes 196616 | tf_op jit(solution)/shard_map/ppermute | solution.py:10
  86.4 6.2 %collective-permute-start.7 = (f32[32,512]{1,0:T(8,128)S(1)}, f32[32,512]{1,0:T(8,128)S(1)}, u32[]{:S(2)}, u32[]{:S(2)}) collective-permute-start(f32[32,512]{1,0:T(8,128)S(1)} %fusion.57), channel_id=1, source_target_pairs={{4,0},{8,4},{12,8},{16,12},{20,16},{24,20},{28,24},{5,1},{9,5},{13... | collective-permute-start | bytes 196616 | tf_op jit(solution)/shard_map/ppermute | solution.py:10
  93.7 5.3 %collective-permute-start.8 = (f32[32,512]{1,0:T(8,128)S(1)}, f32[32,512]{1,0:T(8,128)S(1)}, u32[]{:S(2)}, u32[]{:S(2)}) collective-permute-start(f32[32,512]{1,0:T(8,128)S(1)} %get-tuple-element.46), channel_id=1, source_target_pairs={{0,4},{4,8},{8,12},{12,16},{16,20},{20,24},{24,28},{1,5},{5,9},{9,... | collective-permute-start | bytes 196616 | tf_op jit(solution)/shard_map/ppermute | solution.py:10
  97.1 6.2 %collective-permute-start.9 = (f32[32,512]{1,0:T(8,128)S(1)}, f32[32,512]{1,0:T(8,128)S(1)}, u32[]{:S(2)}, u32[]{:S(2)}) collective-permute-start(f32[32,512]{1,0:T(8,128)S(1)} %fusion.50), channel_id=1, source_target_pairs={{4,0},{8,4},{12,8},{16,12},{20,16},{24,20},{28,24},{5,1},{9,5},{13... | collective-permute-start | bytes 196616 | tf_op jit(solution)/shard_map/ppermute | solution.py:10
  104.5 6.2 %collective-permute-start.10 = (f32[32,512]{1,0:T(8,128)S(1)}, f32[32,512]{1,0:T(8,128)S(1)}, u32[]{:S(2)}, u32[]{:S(2)}) collective-permute-start(f32[32,512]{1,0:T(8,128)S(1)} %get-tuple-element.50), channel_id=1, source_target_pairs={{0,4},{4,8},{8,12},{12,16},{16,20},{20,24},{24,28},{1,5},{5,9},{9,... | collective-permute-start | bytes 196616 | tf_op jit(solution)/shard_map/ppermute | solution.py:10
  108.8 6.2 %collective-permute-start.11 = (f32[32,512]{1,0:T(8,128)S(1)}, f32[32,512]{1,0:T(8,128)S(1)}, u32[]{:S(2)}, u32[]{:S(2)}) collective-permute-start(f32[32,512]{1,0:T(8,128)S(1)} %fusion.43), channel_id=1, source_target_pairs={{4,0},{8,4},{12,8},{16,12},{20,16},{24,20},{28,24},{5,1},{9,5},{13... | collective-permute-start | bytes 196616 | tf_op jit(solution)/shard_map/ppermute | solution.py:10
  116.1 6.3 %collective-permute-start.12 = (f32[32,512]{1,0:T(8,128)S(1)}, f32[32,512]{1,0:T(8,128)S(1)}, u32[]{:S(2)}, u32[]{:S(2)}) collective-permute-start(f32[32,512]{1,0:T(8,128)S(1)} %get-tuple-element.54), channel_id=1, source_target_pairs={{0,4},{4,8},{8,12},{12,16},{16,20},{20,24},{24,28},{1,5},{5,9},{9,... | collective-permute-start | bytes 196616 | tf_op jit(solution)/shard_map/ppermute | solution.py:10
  120.5 6.2 %collective-permute-start.13 = (f32[32,512]{1,0:T(8,128)S(1)}, f32[32,512]{1,0:T(8,128)S(1)}, u32[]{:S(2)}, u32[]{:S(2)}) collective-permute-start(f32[32,512]{1,0:T(8,128)S(1)} %fusion.36), channel_id=1, source_target_pairs={{4,0},{8,4},{12,8},{16,12},{20,16},{24,20},{28,24},{5,1},{9,5},{13... | collective-permute-start | bytes 196616 | tf_op jit(solution)/shard_map/ppermute | solution.py:10

commit v3 on v2

v3 whole, which is shorter than its diff:
```python
import jax
import jax.numpy as jnp
from jax import lax
from jax.sharding import PartitionSpec as P


def bf16_part(value):
    return lax.reduce_precision(value, exponent_bits=8, mantissa_bits=7)


def split_dot(state, weights):
    high = bf16_part(state)
    low = state - high
    both = jnp.concatenate([high, low], axis=0).astype(jnp.bfloat16)
    prod = jnp.dot(both, weights, preferred_element_type=jnp.float32)
    rows = state.shape[0]
    return prod[:rows] + prod[rows:]


def three_pieces(value):
    high = bf16_part(value)
    rest = value - high
    mid = bf16_part(rest)
    return jnp.stack([high, mid, rest - mid]).astype(jnp.bfloat16)


def local(observed, input_gain, persist, coupling, pattern):
    step_count, rows, cols = observed.shape
    state_width = coupling.shape[1]
    block_count = pattern.shape[0]
    block_size = state_width // block_count
    time_groups = lax.axis_size("tm")
    col_groups = lax.axis_size("col")
    half = col_groups // 2
    own_rows = rows // half
    col_pos = lax.axis_index("col")
    backward = col_pos >= half

    small = jnp.concatenate([persist, input_gain[None]], axis=0)
    small_rows = 3 * (step_count + 1)
    small_pad = -small_rows % 16
    small_pieces = jnp.pad(three_pieces(small).reshape(small_rows, cols), ((0, small_pad), (0, 0)))
    coupling_rows = coupling.reshape(step_count * state_width, cols)
    seen_parts = observed.reshape(step_count, half, own_rows, cols).transpose(1, 0, 2, 3)
    seen_parts = seen_parts.reshape(half, step_count * own_rows, cols)
    seen_parts = jnp.concatenate([seen_parts] * (col_groups // half), axis=0)
    packet = jnp.concatenate(
        [
            jnp.broadcast_to(coupling_rows[None], (col_groups,) + coupling_rows.shape),
            seen_parts,
            jnp.broadcast_to(small_pieces[None], (col_groups,) + small_pieces.shape),
        ],
        axis=1,
    )
    packet = lax.all_to_all(packet, "col", split_axis=0, concat_axis=0, tiled=True)
    n_coupling = step_count * state_width
    n_seen = step_count * own_rows
    blocks = packet[:, :n_coupling].reshape(col_groups, step_count, state_width, cols)
    straight = blocks.transpose(1, 2, 0, 3).reshape(step_count, state_width, state_width)
    turned = blocks.transpose(1, 0, 3, 2).reshape(step_count, state_width, state_width)[::-1]
    pattern_used = jnp.where(backward, pattern.T, pattern).astype(jnp.bfloat16)
    mask = jnp.broadcast_to(
        pattern_used[:, None, :, None],
        (block_count, block_size, block_count, block_size),
    ).reshape(state_width, state_width)
    weights = jnp.where(backward, turned, straight) * mask[None]

    seen = (
        packet[:, n_coupling : n_coupling + n_seen]
        .reshape(col_groups, step_count, own_rows, cols)
        .transpose(1, 2, 0, 3)
        .reshape(step_count, own_rows, state_width)
    )
    small = packet[:, n_coupling + n_seen : n_coupling + n_seen + small_rows].astype(jnp.float32)
    small = small.reshape(col_groups, 3, step_count + 1, cols)
    small = (small[:, 0] + small[:, 1] + small[:, 2]).transpose(1, 0, 2)
    small = small.reshape(step_count + 1, state_width)
    diag = small[:step_count]
    gain = small[step_count]
    driven = gain[None, None, :] * seen.astype(jnp.float32)

    zeros = jnp.zeros_like(driven)
    before = jnp.where(backward, driven[::-1], zeros)
    after = jnp.where(backward, zeros, driven)
    diag = jnp.where(backward, diag[::-1], diag)

    def chain(y):
        out = []
        for k in range(step_count):
            z = y + before[k]
            y = split_dot(z, weights[k]) + z * diag[k][None] + after[k]
            out.append(y)
        return out

    pairs = []
    for t in range(time_groups):
        for c in range(col_groups):
            to = t + (-1 if c >= half else 1)
            if 0 <= to < time_groups:
                pairs.append((t * col_groups + c, to * col_groups + c))

    def stage(y):
        return lax.ppermute(chain(y)[-1], ("tm", "col"), pairs)

    y = jnp.zeros(driven.shape[1:], jnp.float32)
    if time_groups <= 8:
        for _ in range(time_groups - 1):
            y = stage(y)
    else:
        y = lax.fori_loop(0, time_groups - 1, lambda _, c: stage(c), y)
    ys = chain(y)
    mine = jnp.where(backward, jnp.stack([ys[0], y]), jnp.stack(ys))
    mine = mine.reshape(step_count, own_rows, col_groups, cols).transpose(2, 0, 1, 3)
    got = lax.all_to_all(mine, "col", split_axis=0, concat_axis=0, tiled=True)
    got = got.reshape(2, half, step_count, own_rows, cols).transpose(0, 2, 1, 3, 4)
    got = got.reshape(2, step_count, rows, cols)
    filtered = got[0]
    return filtered, filtered + got[1]


def solution(mesh):
    return jax.shard_map(
        local,
        mesh=mesh,
        in_specs=(P("tm", None, "col"), P("col"), P("tm", "col"), P("tm", None, "col"), P()),
        out_specs=(P("tm", None, "col"), P("tm", None, "col")),
        check_vma=False,
    )
```

time: 138 us -> 100 us (0.72)
  waiting for transfers between devices: 47.7 us -> 33.6 us
  other arithmetic: 15.5 us -> 5.53 us
  local copies, waits for them, and re-layouts: 14.8 us -> 6.71 us
  matrix products: 7.44 us -> 3.64 us
  starting transfers between devices: 41.7 us -> 38.7 us
    ppermute x14 -> x7, waiting for transfers between devices: 34.1 us -> 18.5 us  [stage(): return lax.ppermute(chain(y)[-1], ('tm', 'col'), pairs)]
    all_to_all x2 -> x0, other arithmetic: 13.5 us -> none  [local(): lax.all_to_all(packet, 'col', split_axis=0, concat_axis=0, tiled=True)]
    unnamed x10 -> x9, local copies, waits for them, and re-layouts: 9.23 us -> 0.09 us
    dot_general x31 -> x16, matrix products: 7.44 us -> 3.64 us  [split_dot(): prod = jnp.dot(both, weights, preferred_element_type=jnp.float32)]
    ppermute x14 -> x7, starting transfers between devices: 37.3 us -> 34.4 us  [stage(): return lax.ppermute(chain(y)[-1], ('tm', 'col'), pairs)]
    transpose x1 -> x3, local copies, waits for them, and re-layouts: 0.53 us -> 2.68 us  [the longest x1 1.31 us: local(): blocks.transpose(1, 0, 3, 2).reshape(step_count, state_width, state_width)]
    all_to_all x1, waiting for transfers between devices: 13.6 us -> 15.1 us  [local(): lax.all_to_all(packet, 'col', split_axis=0, concat_axis=0, tiled=True)]
    mul x2 -> x1, other arithmetic: 0.19 us -> 1.58 us  [local(): weights = jnp.where(backward, turned, straight) * mask[None]]
  transfers between devices with their start and end apart: 15 -> 8, of which waited for: 15 -> 8; matrix products, arithmetic and copies ran while one was open for 1% -> 1% of each run, Pallas kernels for 0% -> 0%
where the time goes in v3:
time: 100 us; the launch traced here: 98.6 us
  starting transfers between devices  38.7 us (39%)
  waiting for transfers between devices  33.6 us (34%)
  blocking collectives  9.27 us (9%)
  local copies, waits for them, and re-layouts  6.71 us (7%)
  other arithmetic  5.53 us (6%)
  matrix products  3.64 us (4%)
  between operations  1.18 us (1%)
    ppermute x7, starting transfers between devices, stage(): return lax.ppermute(chain(y)[-1], ('tm', 'col'), pairs)  34.4 us
    ppermute x7, waiting for transfers between devices, stage(): return lax.ppermute(chain(y)[-1], ('tm', 'col'), pairs)  18.5 us
    all_to_all x1, waiting for transfers between devices, local(): lax.all_to_all(packet, 'col', split_axis=0, concat_axis=0, tiled=True)  15.1 us
    all_to_all x1, blocking collectives, local(): got = lax.all_to_all(mine, 'col', split_axis=0, concat_axis=0, tiled=True)  9.27 us
    all_to_all x1, starting transfers between devices, local(): lax.all_to_all(packet, 'col', split_axis=0, concat_axis=0, tiled=True)  4.37 us
    dot_general x16, matrix products, split_dot(): prod = jnp.dot(both, weights, preferred_element_type=jnp.float32)  3.64 us
  transfers between devices with their start and end apart: 8, of which 8 were waited for; matrix products, arithmetic and copies ran while one was open for 1% of the time, Pallas kernels for 0%

profile of v3, /device:TPU:0, one launch (start us, length us, event | category | flops | bytes accessed | tf_op | source)
XLA Modules:
  0.0 98.6 jit_solution(8816378514466138134)
XLA Ops:
  0.6 0.7 reduce-precision_convert_fusion.17
  1.4 0.8 copy.39
  2.2 1.1 %broadcast_in_dim.11 = bf16[4,1024,128]{2,1,0:T(8,128)(2,1)S(1)} broadcast(bf16[1024,128]{1,0:T(8,128)(2,1)} %bitcast.225), dimensions={1,2} | broadcast | bytes 1310720 | tf_op jit(solution)/shard_map/broadcast_in_dim | solution.py:49
  3.3 1.1 %pad_maximum_fusion = bf16[4,1168,128]{2,1,0:T(8,128)(2,1)} fusion(bf16[4,16,128]{2,1,0:T(8,128)(2,1)S(1)} %broadcast_in_dim.12, bf16[2,128,128]{2,1,0:T(8,128)(2,1)S(1)} %bitcast.226, bf16[4,1024,128]{2,1,0:T(8,128)(2,1)S(1)} %broadcast_in_dim.11), kind=kLoop, calls=%fused_computation | loop fusion | flops 4784128 | bytes 2326528 | tf_op jit(solution)/shard_map/concatenate | solution.py:47
  4.4 4.4 %all-to-all-start = ((bf16[4,1168,128]{2,1,0:T(8,128)(2,1)}), bf16[4,1168,128]{2,1,0:T(8,128)(2,1)S(1)}, u32[]{:S(2)}, u32[]{:S(2)}) async-start(bf16[4,1168,128]{2,1,0:T(8,128)(2,1)} %pad_maximum_fusion), calls=%async_computation | async-start | bytes 2392064 | tf_op jit(solution)/shard_map/all_to_all | solution.py:55
  8.9 0.2 broadcast_in_dim.27
  9.1 0.6 mul.55
  9.7 15.1 %all-to-all-done = bf16[4,1168,128]{2,1,0:T(8,128)(2,1)S(1)} async-done(((bf16[4,1168,128]{2,1,0:T(8,128)(2,1)}), bf16[4,1168,128]{2,1,0:T(8,128)(2,1)S(1)}, u32[]{:S(2)}, u32[]{:S(2)}) %all-to-all-start) | async-done | bytes 1196064 | tf_op jit(solution)/shard_map/all_to_all | solution.py:55
  24.9 0.1 rev.11
  25.1 0.1 copy.57
  25.2 0.1 reshape.168
  25.5 0.5 copy.43
  26.0 1.3 %copy.44 = bf16[2,512,512]{2,1,0:T(8,128)(2,1)} copy(bf16[2,512,512]{1,2,0:T(8,128)(2,1)S(1)} %bitcast.217) | data formatting | bytes 2097152 | tf_op jit(solution)/shard_map/reshape | solution.py:59
  27.4 1.3 %copy.42 = bf16[2,4,128,512]{3,2,1,0:T(8,128)(2,1)} copy(bf16[2,4,128,512]{2,3,0,1:T(8,128)(2,1)S(1)} %bitcast.216) | data formatting | bytes 2097152 | tf_op jit(solution)/shard_map/transpose | solution.py:60
  28.7 1.6 %select_multiply_fusion = bf16[2,512,512]{2,1,0:T(8,128)(2,1)S(1)} fusion(bf16[2,512,512]{2,1,0:T(8,128)(2,1)S(1)} %copy-done, bf16[2,512,512]{2,1,0:T(8,128)(2,1)} %bitcast.218, pred[]{:T(512)S(6)} %ge.3, bf16[512,512]{1,0:T(8,128)(2,1)S(1)} %mul.55), kind=kLoop, calls=%fused_computation.1 | loop fusion | flops 2621440 | bytes 3670017 | tf_op jit(solution)/shard_map/mul | solution.py:66
  30.3 0.2 fusion.57
  30.6 0.2 fusion.61
  30.9 4.2 %collective-permute-start = (f32[64,512]{1,0:T(8,128)S(1)}, f32[64,512]{1,0:T(8,128)S(1)}, u32[]{:S(2)}, u32[]{:S(2)}) collective-permute-start(f32[64,512]{1,0:T(8,128)S(1)} %fusion.53), channel_id=1, source_target_pairs={{0,4},{1,5},{4,8},{5,9},{6,2},{7,3},{8,12},{9,13},{10,6},{11,7},{1... | collective-permute-start | bytes 393224 | tf_op jit(solution)/shard_map/ppermute | solution.py:103
  35.1 2.5 %collective-permute-done = f32[64,512]{1,0:T(8,128)S(1)} collective-permute-done((f32[64,512]{1,0:T(8,128)S(1)}, f32[64,512]{1,0:T(8,128)S(1)}, u32[]{:S(2)}, u32[]{:S(2)}) %collective-permute-start) | collective-permute-done | bytes 131104 | tf_op jit(solution)/shard_map/ppermute | solution.py:103
  37.6 0.2 fusion.65
  37.9 0.2 fusion.69
  38.2 4.4 %collective-permute-start.1 = (f32[64,512]{1,0:T(8,128)S(1)}, f32[64,512]{1,0:T(8,128)S(1)}, u32[]{:S(2)}, u32[]{:S(2)}) collective-permute-start(f32[64,512]{1,0:T(8,128)S(1)} %fusion.48), channel_id=1, source_target_pairs={{0,4},{1,5},{4,8},{5,9},{6,2},{7,3},{8,12},{9,13},{10,6},{11,7},{1... | collective-permute-start | bytes 393224 | tf_op jit(solution)/shard_map/ppermute | solution.py:103
  42.6 2.5 %collective-permute-done.1 = f32[64,512]{1,0:T(8,128)S(1)} collective-permute-done((f32[64,512]{1,0:T(8,128)S(1)}, f32[64,512]{1,0:T(8,128)S(1)}, u32[]{:S(2)}, u32[]{:S(2)}) %collective-permute-start.1) | collective-permute-done | bytes 131104 | tf_op jit(solution)/shard_map/ppermute | solution.py:103
  45.1 0.2 fusion.73
  45.3 0.1 reduce-precision_convert_fusion.10
  45.4 0.2 fusion.77
  45.7 4.4 %collective-permute-start.2 = (f32[64,512]{1,0:T(8,128)S(1)}, f32[64,512]{1,0:T(8,128)S(1)}, u32[]{:S(2)}, u32[]{:S(2)}) collective-permute-start(f32[64,512]{1,0:T(8,128)S(1)} %fusion.43), channel_id=1, source_target_pairs={{0,4},{1,5},{4,8},{5,9},{6,2},{7,3},{8,12},{9,13},{10,6},{11,7},{1... | collective-permute-start | bytes 393224 | tf_op jit(solution)/shard_map/ppermute | solution.py:103
  50.1 2.5 %collective-permute-done.2 = f32[64,512]{1,0:T(8,128)S(1)} collective-permute-done((f32[64,512]{1,0:T(8,128)S(1)}, f32[64,512]{1,0:T(8,128)S(1)}, u32[]{:S(2)}, u32[]{:S(2)}) %collective-permute-start.2) | collective-permute-done | bytes 131104 | tf_op jit(solution)/shard_map/ppermute | solution.py:103
  52.6 0.2 fusion.81
  52.9 0.2 fusion.85
  53.2 5.2 %collective-permute-start.3 = (f32[64,512]{1,0:T(8,128)S(1)}, f32[64,512]{1,0:T(8,128)S(1)}, u32[]{:S(2)}, u32[]{:S(2)}) collective-permute-start(f32[64,512]{1,0:T(8,128)S(1)} %fusion.38), channel_id=1, source_target_pairs={{0,4},{1,5},{4,8},{5,9},{6,2},{7,3},{8,12},{9,13},{10,6},{11,7},{1... | collective-permute-start | bytes 393224 | tf_op jit(solution)/shard_map/ppermute | solution.py:103
  58.5 2.5 %collective-permute-done.3 = f32[64,512]{1,0:T(8,128)S(1)} collective-permute-done((f32[64,512]{1,0:T(8,128)S(1)}, f32[64,512]{1,0:T(8,128)S(1)}, u32[]{:S(2)}, u32[]{:S(2)}) %collective-permute-start.3) | collective-permute-done | bytes 131104 | tf_op jit(solution)/shard_map/ppermute | solution.py:103
  61.0 0.2 fusion.89
  61.3 0.2 fusion.93
  61.6 5.3 %collective-permute-start.4 = (f32[64,512]{1,0:T(8,128)S(1)}, f32[64,512]{1,0:T(8,128)S(1)}, u32[]{:S(2)}, u32[]{:S(2)}) collective-permute-start(f32[64,512]{1,0:T(8,128)S(1)} %fusion.33), channel_id=1, source_target_pairs={{0,4},{1,5},{4,8},{5,9},{6,2},{7,3},{8,12},{9,13},{10,6},{11,7},{1... | collective-permute-start | bytes 393224 | tf_op jit(solution)/shard_map/ppermute | solution.py:103
  66.9 2.5 %collective-permute-done.4 = f32[64,512]{1,0:T(8,128)S(1)} collective-permute-done((f32[64,512]{1,0:T(8,128)S(1)}, f32[64,512]{1,0:T(8,128)S(1)}, u32[]{:S(2)}, u32[]{:S(2)}) %collective-permute-start.4) | collective-permute-done | bytes 131104 | tf_op jit(solution)/shard_map/ppermute | solution.py:103
  69.4 0.2 fusion.97
  69.7 0.2 fusion.101
  70.0 5.4 %collective-permute-start.5 = (f32[64,512]{1,0:T(8,128)S(1)}, f32[64,512]{1,0:T(8,128)S(1)}, u32[]{:S(2)}, u32[]{:S(2)}) collective-permute-start(f32[64,512]{1,0:T(8,128)S(1)} %fusion.28), channel_id=1, source_target_pairs={{0,4},{1,5},{4,8},{5,9},{6,2},{7,3},{8,12},{9,13},{10,6},{11,7},{1... | collective-permute-start | bytes 393224 | tf_op jit(solution)/shard_map/ppermute | solution.py:103
  75.4 3.5 %collective-permute-done.5 = f32[64,512]{1,0:T(8,128)S(1)} collective-permute-done((f32[64,512]{1,0:T(8,128)S(1)}, f32[64,512]{1,0:T(8,128)S(1)}, u32[]{:S(2)}, u32[]{:S(2)}) %collective-permute-start.5) | collective-permute-done | bytes 131104 | tf_op jit(solution)/shard_map/ppermute | solution.py:103
  78.9 0.2 fusion.105
  79.3 0.2 fusion.109
  79.6 5.6 %collective-permute-start.6 = (f32[64,512]{1,0:T(8,128)S(1)}, f32[64,512]{1,0:T(8,128)S(1)}, u32[]{:S(2)}, u32[]{:S(2)}) collective-permute-start(f32[64,512]{1,0:T(8,128)S(1)} %fusion.23), channel_id=1, source_target_pairs={{0,4},{1,5},{4,8},{5,9},{6,2},{7,3},{8,12},{9,13},{10,6},{11,7},{1... | collective-permute-start | bytes 393224 | tf_op jit(solution)/shard_map/ppermute | solution.py:103
  85.2 2.5 %collective-permute-done.6 = f32[64,512]{1,0:T(8,128)S(1)} collective-permute-done((f32[64,512]{1,0:T(8,128)S(1)}, f32[64,512]{1,0:T(8,128)S(1)}, u32[]{:S(2)}, u32[]{:S(2)}) %collective-permute-start.6) | collective-permute-done | bytes 131104 | tf_op jit(solution)/shard_map/ppermute | solution.py:103
  87.7 0.2 fusion.113
  88.2 0.2 fusion.117
  88.6 9.3 %all_to_all.10 = f32[4,2,64,128]{3,2,1,0:T(8,128)S(1)} all-to-all(f32[4,2,64,128]{3,2,1,0:T(8,128)S(1)} %fusion.1), channel_id=1, replica_groups=mesh['tm'=8,'col'=4] {'col'}, dimensions={0} | all-to-all | bytes 524288 | tf_op jit(solution)/shard_map/all_to_all | solution.py:114
  97.9 0.7 add.270
  (65 shorter events, 1.8 us)
Async XLA Ops:
  4.4 4.4 %copy-start.2 = (s32[8,8]{1,0:T(8,128)S(1)}, s32[8,8]{1,0:T(8,128)}, u32[]{:S(2)}) copy-start(s32[8,8]{1,0:T(8,128)} %param.9) | copy-start | bytes 772
  4.4 20.4 %all-to-all-start = ((bf16[4,1168,128]{2,1,0:T(8,128)(2,1)}), bf16[4,1168,128]{2,1,0:T(8,128)(2,1)S(1)}, u32[]{:S(2)}, u32[]{:S(2)}) async-start(bf16[4,1168,128]{2,1,0:T(8,128)(2,1)} %pad_maximum_fusion), calls=%async_computation | async-start | bytes 2392064 | tf_op jit(solution)/shard_map/all_to_all | solution.py:55
  27.4 1.3 %copy-start = (bf16[2,512,512]{2,1,0:T(8,128)(2,1)S(1)}, bf16[2,512,512]{2,1,0:T(8,128)(2,1)}, u32[]{:S(2)}) copy-start(bf16[2,512,512]{2,1,0:T(8,128)(2,1)} %copy.44) | copy-start | bytes 3145732
  30.9 6.7 %collective-permute-start = (f32[64,512]{1,0:T(8,128)S(1)}, f32[64,512]{1,0:T(8,128)S(1)}, u32[]{:S(2)}, u32[]{:S(2)}) collective-permute-start(f32[64,512]{1,0:T(8,128)S(1)} %fusion.53), channel_id=1, source_target_pairs={{0,4},{1,5},{4,8},{5,9},{6,2},{7,3},{8,12},{9,13},{10,6},{11,7},{1... | collective-permute-start | bytes 393224 | tf_op jit(solution)/shard_map/ppermute | solution.py:103
  38.2 6.9 %collective-permute-start.1 = (f32[64,512]{1,0:T(8,128)S(1)}, f32[64,512]{1,0:T(8,128)S(1)}, u32[]{:S(2)}, u32[]{:S(2)}) collective-permute-start(f32[64,512]{1,0:T(8,128)S(1)} %fusion.48), channel_id=1, source_target_pairs={{0,4},{1,5},{4,8},{5,9},{6,2},{7,3},{8,12},{9,13},{10,6},{11,7},{1... | collective-permute-start | bytes 393224 | tf_op jit(solution)/shard_map/ppermute | solution.py:103
  45.7 6.9 %collective-permute-start.2 = (f32[64,512]{1,0:T(8,128)S(1)}, f32[64,512]{1,0:T(8,128)S(1)}, u32[]{:S(2)}, u32[]{:S(2)}) collective-permute-start(f32[64,512]{1,0:T(8,128)S(1)} %fusion.43), channel_id=1, source_target_pairs={{0,4},{1,5},{4,8},{5,9},{6,2},{7,3},{8,12},{9,13},{10,6},{11,7},{1... | collective-permute-start | bytes 393224 | tf_op jit(solution)/shard_map/ppermute | solution.py:103
  53.2 7.7 %collective-permute-start.3 = (f32[64,512]{1,0:T(8,128)S(1)}, f32[64,512]{1,0:T(8,128)S(1)}, u32[]{:S(2)}, u32[]{:S(2)}) collective-permute-start(f32[64,512]{1,0:T(8,128)S(1)} %fusion.38), channel_id=1, source_target_pairs={{0,4},{1,5},{4,8},{5,9},{6,2},{7,3},{8,12},{9,13},{10,6},{11,7},{1... | collective-permute-start | bytes 393224 | tf_op jit(solution)/shard_map/ppermute | solution.py:103
  61.6 7.8 %collective-permute-start.4 = (f32[64,512]{1,0:T(8,128)S(1)}, f32[64,512]{1,0:T(8,128)S(1)}, u32[]{:S(2)}, u32[]{:S(2)}) collective-permute-start(f32[64,512]{1,0:T(8,128)S(1)} %fusion.33), channel_id=1, source_target_pairs={{0,4},{1,5},{4,8},{5,9},{6,2},{7,3},{8,12},{9,13},{10,6},{11,7},{1... | collective-permute-start | bytes 393224 | tf_op jit(solution)/shard_map/ppermute | solution.py:103
  70.0 8.9 %collective-permute-start.5 = (f32[64,512]{1,0:T(8,128)S(1)}, f32[64,512]{1,0:T(8,128)S(1)}, u32[]{:S(2)}, u32[]{:S(2)}) collective-permute-start(f32[64,512]{1,0:T(8,128)S(1)} %fusion.28), channel_id=1, source_target_pairs={{0,4},{1,5},{4,8},{5,9},{6,2},{7,3},{8,12},{9,13},{10,6},{11,7},{1... | collective-permute-start | bytes 393224 | tf_op jit(solution)/shard_map/ppermute | solution.py:103
  79.6 8.1 %collective-permute-start.6 = (f32[64,512]{1,0:T(8,128)S(1)}, f32[64,512]{1,0:T(8,128)S(1)}, u32[]{:S(2)}, u32[]{:S(2)}) collective-permute-start(f32[64,512]{1,0:T(8,128)S(1)} %fusion.23), channel_id=1, source_target_pairs={{0,4},{1,5},{4,8},{5,9},{6,2},{7,3},{8,12},{9,13},{10,6},{11,7},{1... | collective-permute-start | bytes 393224 | tf_op jit(solution)/shard_map/ppermute | solution.py:103
  97.9 0.7 copy-start.1

commit v4 on v3

--- a/solution.py
+++ b/solution.py
@@ -56,14 +56,21 @@
     n_coupling = step_count * state_width
     n_seen = step_count * own_rows
     blocks = packet[:, :n_coupling].reshape(col_groups, step_count, state_width, cols)
-    straight = blocks.transpose(1, 2, 0, 3).reshape(step_count, state_width, state_width)
-    turned = blocks.transpose(1, 0, 3, 2).reshape(step_count, state_width, state_width)[::-1]
-    pattern_used = jnp.where(backward, pattern.T, pattern).astype(jnp.bfloat16)
-    mask = jnp.broadcast_to(
-        pattern_used[:, None, :, None],
-        (block_count, block_size, block_count, block_size),
-    ).reshape(state_width, state_width)
-    weights = jnp.where(backward, turned, straight) * mask[None]
+    def expanded(bits):
+        return jnp.broadcast_to(
+            bits.astype(jnp.bfloat16)[:, None, :, None],
+            (block_count, block_size, block_count, block_size),
+        ).reshape(state_width, state_width)
+
+    def straight(b):
+        full = b.transpose(1, 2, 0, 3).reshape(step_count, state_width, state_width)
+        return full * expanded(pattern)[None]
+
+    def turned(b):
+        full = b.transpose(1, 0, 3, 2).reshape(step_count, state_width, state_width)
+        return full[::-1] * expanded(pattern.T)[None]
+
+    weights = lax.cond(backward, turned, straight, blocks)
 
     seen = (
         packet[:, n_coupling : n_coupling + n_seen]

time: 100 us -> 98.1 us (0.981)
  the two profiles are of different devices: /device:TPU:0 before, /device:TPU:8 now
where the time goes in v4:
time: 98.1 us; the launch traced here: 97.6 us
  waiting for transfers between devices  56.2 us (57%)
  starting transfers between devices  19.1 us (19%)
  blocking collectives  8.39 us (9%)
  local copies, waits for them, and re-layouts  5.04 us (5%)
  other arithmetic  4.05 us (4%)
  matrix products  3.64 us (4%)
  between operations  1.17 us (1%)
    ppermute x7, waiting for transfers between devices, stage(): return lax.ppermute(chain(y)[-1], ('tm', 'col'), pairs)  40.2 us
    all_to_all x1, waiting for transfers between devices, local(): lax.all_to_all(packet, 'col', split_axis=0, concat_axis=0, tiled=True)  16 us
    ppermute x7, starting transfers between devices, stage(): return lax.ppermute(chain(y)[-1], ('tm', 'col'), pairs)  15.6 us
    all_to_all x1, blocking collectives, local(): got = lax.all_to_all(mine, 'col', split_axis=0, concat_axis=0, tiled=True)  8.39 us
    dot_general x16, matrix products, split_dot(): prod = jnp.dot(both, weights, preferred_element_type=jnp.float32)  3.64 us
    all_to_all x1, starting transfers between devices, local(): lax.all_to_all(packet, 'col', split_axis=0, concat_axis=0, tiled=True)  3.53 us
  transfers between devices with their start and end apart: 8, of which 8 were waited for; matrix products, arithmetic and copies ran while one was open for 0% of the time, Pallas kernels for 0%

profile of v4, /device:TPU:8, one launch (start us, length us, event | category | flops | bytes accessed | tf_op | source)
XLA Modules:
  0.0 97.6 jit_solution(2405175187190645233)
XLA Ops:
  0.6 0.7 reduce-precision_convert_fusion.17
  1.4 0.8 copy.25
  2.2 1.1 %broadcast_in_dim.38 = bf16[4,1024,128]{2,1,0:T(8,128)(2,1)S(1)} broadcast(bf16[1024,128]{1,0:T(8,128)(2,1)} %bitcast.226), dimensions={1,2} | broadcast | bytes 1310720 | tf_op jit(solution)/shard_map/broadcast_in_dim | solution.py:49
  3.3 1.1 %pad_maximum_fusion = bf16[4,1168,128]{2,1,0:T(8,128)(2,1)} fusion(bf16[4,16,128]{2,1,0:T(8,128)(2,1)S(1)} %broadcast_in_dim.39, bf16[2,128,128]{2,1,0:T(8,128)(2,1)S(1)} %bitcast.227, bf16[4,1024,128]{2,1,0:T(8,128)(2,1)S(1)} %broadcast_in_dim.38), kind=kLoop, calls=%fused_computation.4 | loop fusion | flops 4784128 | bytes 2326528 | tf_op jit(solution)/shard_map/concatenate | solution.py:47
  4.5 3.5 %all-to-all-start = ((bf16[4,1168,128]{2,1,0:T(8,128)(2,1)}), bf16[4,1168,128]{2,1,0:T(8,128)(2,1)S(1)}, u32[]{:S(2)}, u32[]{:S(2)}) async-start(bf16[4,1168,128]{2,1,0:T(8,128)(2,1)} %pad_maximum_fusion), calls=%async_computation | async-start | bytes 2392064 | tf_op jit(solution)/shard_map/all_to_all | solution.py:55
  8.0 16.0 %all-to-all-done = bf16[4,1168,128]{2,1,0:T(8,128)(2,1)S(1)} async-done(((bf16[4,1168,128]{2,1,0:T(8,128)(2,1)}), bf16[4,1168,128]{2,1,0:T(8,128)(2,1)S(1)}, u32[]{:S(2)}, u32[]{:S(2)}) %all-to-all-start) | async-done | bytes 1196064 | tf_op jit(solution)/shard_map/all_to_all | solution.py:55
  24.0 0.1 rev.14
  24.2 0.1 copy.41
  24.3 0.1 reshape.189
  24.6 0.3 copy-done.1
  24.9 2.3 %conditional.1 = (bf16[2,512,512]{2,1,0:T(8,128)(2,1)S(1)}) conditional(s32[]{:T(128)} %convert_element_type.61, (bf16[4,1168,128]{2,1,0:T(8,128)(2,1)S(1)}, s32[8,8]{1,0:T(8,128)S(1)}) %tuple.65, (bf16[4,1168,128]{2,1,0:T(8,128)(2,1)S(1)}, s32[8,8]{1,0:T(8,128)S(1)}) %tuple.66), branch_computations={%region_0.1_spmd, %region_1.2_spmd} | conditional | flops 2097216 | bytes 10486280 | solution.py:73
  25.0 0.8 copy.40
  25.8 0.4 reshape.174
  26.3 0.2 broadcast_in_dim.18
  26.5 0.6 mul.61
  27.1 0.1 broadcast_multiply_fusion
  27.2 0.2 fusion.57
  27.5 0.2 fusion.61
  27.8 3.4 %collective-permute-start = (f32[64,512]{1,0:T(8,128)S(1)}, f32[64,512]{1,0:T(8,128)S(1)}, u32[]{:S(2)}, u32[]{:S(2)}) collective-permute-start(f32[64,512]{1,0:T(8,128)S(1)} %fusion.53), channel_id=1, source_target_pairs={{0,4},{1,5},{4,8},{5,9},{6,2},{7,3},{8,12},{9,13},{10,6},{11,7},{1... | collective-permute-start | bytes 393224 | tf_op jit(solution)/shard_map/ppermute | solution.py:110
  31.2 4.3 %collective-permute-done = f32[64,512]{1,0:T(8,128)S(1)} collective-permute-done((f32[64,512]{1,0:T(8,128)S(1)}, f32[64,512]{1,0:T(8,128)S(1)}, u32[]{:S(2)}, u32[]{:S(2)}) %collective-permute-start) | collective-permute-done | bytes 131104 | tf_op jit(solution)/shard_map/ppermute | solution.py:110
  35.6 0.2 fusion.65
  35.9 0.2 fusion.69
  36.2 2.5 %collective-permute-start.1 = (f32[64,512]{1,0:T(8,128)S(1)}, f32[64,512]{1,0:T(8,128)S(1)}, u32[]{:S(2)}, u32[]{:S(2)}) collective-permute-start(f32[64,512]{1,0:T(8,128)S(1)} %fusion.48), channel_id=1, source_target_pairs={{0,4},{1,5},{4,8},{5,9},{6,2},{7,3},{8,12},{9,13},{10,6},{11,7},{1... | collective-permute-start | bytes 393224 | tf_op jit(solution)/shard_map/ppermute | solution.py:110
  38.8 5.2 %collective-permute-done.1 = f32[64,512]{1,0:T(8,128)S(1)} collective-permute-done((f32[64,512]{1,0:T(8,128)S(1)}, f32[64,512]{1,0:T(8,128)S(1)}, u32[]{:S(2)}, u32[]{:S(2)}) %collective-permute-start.1) | collective-permute-done | bytes 131104 | tf_op jit(solution)/shard_map/ppermute | solution.py:110
  44.0 0.2 fusion.73
  44.3 0.2 fusion.77
  44.6 1.9 %collective-permute-start.2 = (f32[64,512]{1,0:T(8,128)S(1)}, f32[64,512]{1,0:T(8,128)S(1)}, u32[]{:S(2)}, u32[]{:S(2)}) collective-permute-start(f32[64,512]{1,0:T(8,128)S(1)} %fusion.43), channel_id=1, source_target_pairs={{0,4},{1,5},{4,8},{5,9},{6,2},{7,3},{8,12},{9,13},{10,6},{11,7},{1... | collective-permute-start | bytes 393224 | tf_op jit(solution)/shard_map/ppermute | solution.py:110
  46.6 5.8 %collective-permute-done.2 = f32[64,512]{1,0:T(8,128)S(1)} collective-permute-done((f32[64,512]{1,0:T(8,128)S(1)}, f32[64,512]{1,0:T(8,128)S(1)}, u32[]{:S(2)}, u32[]{:S(2)}) %collective-permute-start.2) | collective-permute-done | bytes 131104 | tf_op jit(solution)/shard_map/ppermute | solution.py:110
  52.4 0.2 fusion.81
  52.8 0.2 fusion.85
  53.0 1.9 %collective-permute-start.3 = (f32[64,512]{1,0:T(8,128)S(1)}, f32[64,512]{1,0:T(8,128)S(1)}, u32[]{:S(2)}, u32[]{:S(2)}) collective-permute-start(f32[64,512]{1,0:T(8,128)S(1)} %fusion.38), channel_id=1, source_target_pairs={{0,4},{1,5},{4,8},{5,9},{6,2},{7,3},{8,12},{9,13},{10,6},{11,7},{1... | collective-permute-start | bytes 393224 | tf_op jit(solution)/shard_map/ppermute | solution.py:110
  55.0 5.8 %collective-permute-done.3 = f32[64,512]{1,0:T(8,128)S(1)} collective-permute-done((f32[64,512]{1,0:T(8,128)S(1)}, f32[64,512]{1,0:T(8,128)S(1)}, u32[]{:S(2)}, u32[]{:S(2)}) %collective-permute-start.3) | collective-permute-done | bytes 131104 | tf_op jit(solution)/shard_map/ppermute | solution.py:110
  60.8 0.2 fusion.89
  61.2 0.2 fusion.93
  61.5 1.9 %collective-permute-start.4 = (f32[64,512]{1,0:T(8,128)S(1)}, f32[64,512]{1,0:T(8,128)S(1)}, u32[]{:S(2)}, u32[]{:S(2)}) collective-permute-start(f32[64,512]{1,0:T(8,128)S(1)} %fusion.33), channel_id=1, source_target_pairs={{0,4},{1,5},{4,8},{5,9},{6,2},{7,3},{8,12},{9,13},{10,6},{11,7},{1... | collective-permute-start | bytes 393224 | tf_op jit(solution)/shard_map/ppermute | solution.py:110
  63.4 6.0 %collective-permute-done.4 = f32[64,512]{1,0:T(8,128)S(1)} collective-permute-done((f32[64,512]{1,0:T(8,128)S(1)}, f32[64,512]{1,0:T(8,128)S(1)}, u32[]{:S(2)}, u32[]{:S(2)}) %collective-permute-start.4) | collective-permute-done | bytes 131104 | tf_op jit(solution)/shard_map/ppermute | solution.py:110
  69.4 0.2 fusion.97
  69.8 0.2 fusion.101
  70.0 1.9 %collective-permute-start.5 = (f32[64,512]{1,0:T(8,128)S(1)}, f32[64,512]{1,0:T(8,128)S(1)}, u32[]{:S(2)}, u32[]{:S(2)}) collective-permute-start(f32[64,512]{1,0:T(8,128)S(1)} %fusion.28), channel_id=1, source_target_pairs={{0,4},{1,5},{4,8},{5,9},{6,2},{7,3},{8,12},{9,13},{10,6},{11,7},{1... | collective-permute-start | bytes 393224 | tf_op jit(solution)/shard_map/ppermute | solution.py:110
  72.0 7.2 %collective-permute-done.5 = f32[64,512]{1,0:T(8,128)S(1)} collective-permute-done((f32[64,512]{1,0:T(8,128)S(1)}, f32[64,512]{1,0:T(8,128)S(1)}, u32[]{:S(2)}, u32[]{:S(2)}) %collective-permute-start.5) | collective-permute-done | bytes 131104 | tf_op jit(solution)/shard_map/ppermute | solution.py:110
  79.2 0.2 fusion.105
  79.5 0.2 fusion.109
  79.8 1.9 %collective-permute-start.6 = (f32[64,512]{1,0:T(8,128)S(1)}, f32[64,512]{1,0:T(8,128)S(1)}, u32[]{:S(2)}, u32[]{:S(2)}) collective-permute-start(f32[64,512]{1,0:T(8,128)S(1)} %fusion.23), channel_id=1, source_target_pairs={{0,4},{1,5},{4,8},{5,9},{6,2},{7,3},{8,12},{9,13},{10,6},{11,7},{1... | collective-permute-start | bytes 393224 | tf_op jit(solution)/shard_map/ppermute | solution.py:110
  81.7 5.8 %collective-permute-done.6 = f32[64,512]{1,0:T(8,128)S(1)} collective-permute-done((f32[64,512]{1,0:T(8,128)S(1)}, f32[64,512]{1,0:T(8,128)S(1)}, u32[]{:S(2)}, u32[]{:S(2)}) %collective-permute-start.6) | collective-permute-done | bytes 131104 | tf_op jit(solution)/shard_map/ppermute | solution.py:110
  87.6 0.2 fusion.113
  88.0 0.2 fusion.117
  88.5 8.4 %all_to_all.10 = f32[4,2,64,128]{3,2,1,0:T(8,128)S(1)} all-to-all(f32[4,2,64,128]{3,2,1,0:T(8,128)S(1)} %fusion.1), channel_id=1, replica_groups=mesh['tm'=8,'col'=4] {'col'}, dimensions={0} | all-to-all | bytes 524288 | tf_op jit(solution)/shard_map/all_to_all | solution.py:121
  96.9 0.7 add.270
  (62 shorter events, 1.8 us)
Async XLA Ops:
  4.5 19.5 %all-to-all-start = ((bf16[4,1168,128]{2,1,0:T(8,128)(2,1)}), bf16[4,1168,128]{2,1,0:T(8,128)(2,1)S(1)}, u32[]{:S(2)}, u32[]{:S(2)}) async-start(bf16[4,1168,128]{2,1,0:T(8,128)(2,1)} %pad_maximum_fusion), calls=%async_computation | async-start | bytes 2392064 | tf_op jit(solution)/shard_map/all_to_all | solution.py:55
  24.2 0.7 copy-start.1
  27.8 7.8 %collective-permute-start = (f32[64,512]{1,0:T(8,128)S(1)}, f32[64,512]{1,0:T(8,128)S(1)}, u32[]{:S(2)}, u32[]{:S(2)}) collective-permute-start(f32[64,512]{1,0:T(8,128)S(1)} %fusion.53), channel_id=1, source_target_pairs={{0,4},{1,5},{4,8},{5,9},{6,2},{7,3},{8,12},{9,13},{10,6},{11,7},{1... | collective-permute-start | bytes 393224 | tf_op jit(solution)/shard_map/ppermute | solution.py:110
  36.2 7.8 %collective-permute-start.1 = (f32[64,512]{1,0:T(8,128)S(1)}, f32[64,512]{1,0:T(8,128)S(1)}, u32[]{:S(2)}, u32[]{:S(2)}) collective-permute-start(f32[64,512]{1,0:T(8,128)S(1)} %fusion.48), channel_id=1, source_target_pairs={{0,4},{1,5},{4,8},{5,9},{6,2},{7,3},{8,12},{9,13},{10,6},{11,7},{1... | collective-permute-start | bytes 393224 | tf_op jit(solution)/shard_map/ppermute | solution.py:110
  44.6 7.8 %collective-permute-start.2 = (f32[64,512]{1,0:T(8,128)S(1)}, f32[64,512]{1,0:T(8,128)S(1)}, u32[]{:S(2)}, u32[]{:S(2)}) collective-permute-start(f32[64,512]{1,0:T(8,128)S(1)} %fusion.43), channel_id=1, source_target_pairs={{0,4},{1,5},{4,8},{5,9},{6,2},{7,3},{8,12},{9,13},{10,6},{11,7},{1... | collective-permute-start | bytes 393224 | tf_op jit(solution)/shard_map/ppermute | solution.py:110
  53.0 7.8 %collective-permute-start.3 = (f32[64,512]{1,0:T(8,128)S(1)}, f32[64,512]{1,0:T(8,128)S(1)}, u32[]{:S(2)}, u32[]{:S(2)}) collective-permute-start(f32[64,512]{1,0:T(8,128)S(1)} %fusion.38), channel_id=1, source_target_pairs={{0,4},{1,5},{4,8},{5,9},{6,2},{7,3},{8,12},{9,13},{10,6},{11,7},{1... | collective-permute-start | bytes 393224 | tf_op jit(solution)/shard_map/ppermute | solution.py:110
  61.5 7.9 %collective-permute-start.4 = (f32[64,512]{1,0:T(8,128)S(1)}, f32[64,512]{1,0:T(8,128)S(1)}, u32[]{:S(2)}, u32[]{:S(2)}) collective-permute-start(f32[64,512]{1,0:T(8,128)S(1)} %fusion.33), channel_id=1, source_target_pairs={{0,4},{1,5},{4,8},{5,9},{6,2},{7,3},{8,12},{9,13},{10,6},{11,7},{1... | collective-permute-start | bytes 393224 | tf_op jit(solution)/shard_map/ppermute | solution.py:110
  70.0 9.1 %collective-permute-start.5 = (f32[64,512]{1,0:T(8,128)S(1)}, f32[64,512]{1,0:T(8,128)S(1)}, u32[]{:S(2)}, u32[]{:S(2)}) collective-permute-start(f32[64,512]{1,0:T(8,128)S(1)} %fusion.28), channel_id=1, source_target_pairs={{0,4},{1,5},{4,8},{5,9},{6,2},{7,3},{8,12},{9,13},{10,6},{11,7},{1... | collective-permute-start | bytes 393224 | tf_op jit(solution)/shard_map/ppermute | solution.py:110
  79.8 7.8 %collective-permute-start.6 = (f32[64,512]{1,0:T(8,128)S(1)}, f32[64,512]{1,0:T(8,128)S(1)}, u32[]{:S(2)}, u32[]{:S(2)}) collective-permute-start(f32[64,512]{1,0:T(8,128)S(1)} %fusion.23), channel_id=1, source_target_pairs={{0,4},{1,5},{4,8},{5,9},{6,2},{7,3},{8,12},{9,13},{10,6},{11,7},{1... | collective-permute-start | bytes 393224 | tf_op jit(solution)/shard_map/ppermute | solution.py:110
  96.9 0.7 copy-start

commit v5 on v3

v5 whole, which is shorter than its diff:
```python
import jax
import jax.numpy as jnp
from jax import lax
from jax.sharding import PartitionSpec as P


def bf16_part(value):
    return lax.reduce_precision(value, exponent_bits=8, mantissa_bits=7)


def split_dot(state, weights, transposed):
    high = bf16_part(state)
    low = state - high
    both = jnp.concatenate([high, low], axis=0).astype(jnp.bfloat16)
    contract = 1 if transposed else 0
    prod = lax.dot_general(
        both, weights, (((1,), (contract,)), ((), ())), preferred_element_type=jnp.float32
    )
    rows = state.shape[0]
    return prod[:rows] + prod[rows:]


def three_pieces(value):
    high = bf16_part(value)
    rest = value - high
    mid = bf16_part(rest)
    return jnp.stack([high, mid, rest - mid]).astype(jnp.bfloat16)


def passed_along(shard, axis, by):
    length = lax.axis_size(axis)
    pairs = [(i, i + by) for i in range(length) if 0 <= i + by < length]
    return lax.ppermute(shard, axis, pairs)


def local(observed, input_gain, persist, coupling, pattern):
    step_count, rows, cols = observed.shape
    state_width = coupling.shape[1]
    block_count = pattern.shape[0]
    block_size = state_width // block_count
    time_groups = lax.axis_size("tm")
    col_groups = lax.axis_size("col")
    own_rows = rows // col_groups
    tm_pos = lax.axis_index("tm")

    small = jnp.concatenate([persist, input_gain[None]], axis=0)
    small_rows = 3 * (step_count + 1)
    small_pad = -small_rows % 16
    small_pieces = jnp.pad(three_pieces(small).reshape(small_rows, cols), ((0, small_pad), (0, 0)))
    coupling_rows = coupling.reshape(step_count * state_width, cols)
    seen_parts = observed.reshape(step_count, col_groups, own_rows, cols).transpose(1, 0, 2, 3)
    seen_parts = seen_parts.reshape(col_groups, step_count * own_rows, cols)
    packet = jnp.concatenate(
        [
            jnp.broadcast_to(coupling_rows[None], (col_groups,) + coupling_rows.shape),
            seen_parts,
            jnp.broadcast_to(small_pieces[None], (col_groups,) + small_pieces.shape),
        ],
        axis=1,
    )
    packet = lax.all_to_all(packet, "col", split_axis=0, concat_axis=0, tiled=True)
    n_coupling = step_count * state_width
    n_seen = step_count * own_rows
    mask = jnp.broadcast_to(
        pattern.astype(jnp.bfloat16)[:, None, :, None],
        (block_count, block_size, block_count, block_size),
    ).reshape(state_width, state_width)
    weights = (
        packet[:, :n_coupling]
        .reshape(col_groups, step_count, state_width, cols)
        .transpose(1, 2, 0, 3)
        .reshape(step_count, state_width, state_width)
    ) * mask[None]
    seen = (
        packet[:, n_coupling : n_coupling + n_seen]
        .reshape(col_groups, step_count, own_rows, cols)
        .transpose(1, 2, 0, 3)
        .reshape(step_count, own_rows, state_width)
    )
    small = packet[:, n_coupling + n_seen : n_coupling + n_seen + small_rows].astype(jnp.float32)
    small = small.reshape(col_groups, 3, step_count + 1, cols)
    small = (small[:, 0] + small[:, 1] + small[:, 2]).transpose(1, 0, 2)
    small = small.reshape(step_count + 1, state_width)
    diag = small[:step_count]
    gain = small[step_count]
    driven = gain[None, None, :] * seen.astype(jnp.float32)

    def forward(x):
        out = []
        for k in range(step_count):
            x = split_dot(x, weights[k], False) + x * diag[k][None] + driven[k]
            out.append(x)
        return out

    def backward(e):
        out = []
        for k in range(step_count - 1, -1, -1):
            w = e + driven[k]
            e = split_dot(w, weights[k], True) + w * diag[k][None]
            out.append(e)
        return out

    zeros = jnp.zeros(driven.shape[1:], jnp.float32)
    x_in, e_in = zeros, zeros
    if time_groups <= 8 and time_groups % 2 == 0:
        last = time_groups - 1
        for k in range(last):
            xs = forward(x_in)
            es = backward(e_in)
            send = jnp.where(tm_pos == k, xs[-1], es[-1])
            pairs = [(k * col_groups + c, (k + 1) * col_groups + c) for c in range(col_groups)]
            pairs += [((last - k) * col_groups + c, (last - k - 1) * col_groups + c) for c in range(col_groups)]
            got = lax.ppermute(send, ("tm", "col"), pairs)
            x_in = jnp.where(tm_pos == k + 1, got, x_in)
            e_in = jnp.where(tm_pos == last - k - 1, got, e_in)
    else:
        def stage(_, carry):
            x, e = carry
            return passed_along(forward(x)[-1], "tm", 1), passed_along(backward(e)[-1], "tm", -1)

        x_in, e_in = lax.fori_loop(0, time_groups - 1, stage, (x_in, e_in))
    xs = forward(x_in)
    es = backward(e_in)
    mine = jnp.stack([jnp.stack(xs), jnp.stack([es[step_count - 2 - k] if k < step_count - 1 else e_in for k in range(step_count)])])
    mine = mine.reshape(2, step_count, own_rows, col_groups, cols).transpose(3, 0, 1, 2, 4)
    got = lax.all_to_all(mine, "col", split_axis=0, concat_axis=0, tiled=True)
    got = got.transpose(1, 2, 0, 3, 4).reshape(2, step_count, rows, cols)
    filtered = got[0]
    return filtered, filtered + got[1]


def solution(mesh):
    return jax.shard_map(
        local,
        mesh=mesh,
        in_specs=(P("tm", None, "col"), P("col"), P("tm", "col"), P("tm", None, "col"), P()),
        out_specs=(P("tm", None, "col"), P("tm", None, "col")),
        check_vma=False,
    )
```

time: 100 us -> 83.1 us (0.83)
  starting transfers between devices: 38.7 us -> 13.1 us
  waiting for transfers between devices: 33.6 us -> 42.7 us
  matrix products: 3.64 us -> 7.44 us
  local copies, waits for them, and re-layouts: 6.71 us -> 4.56 us
    ppermute x7, starting transfers between devices: 34.4 us -> 8.78 us  [local(): got = lax.ppermute(send, ('tm', 'col'), pairs)]
    ppermute x7, waiting for transfers between devices: 18.5 us -> 29.1 us  [local(): got = lax.ppermute(send, ('tm', 'col'), pairs)]
    dot_general x16 -> x31, matrix products: 3.64 us -> 7.44 us  [split_dot(): lax.dot_general(both, weights, (((1,), (contract,)), ((), ())), preferred...]
    all_to_all x1, waiting for transfers between devices: 15.1 us -> 13.6 us  [local(): lax.all_to_all(packet, 'col', split_axis=0, concat_axis=0, tiled=True)]
    reshape x1 -> x0, local copies, waits for them, and re-layouts: 1.35 us -> none  [local(): blocks.transpose(1, 2, 0, 3).reshape(step_count, state_width, state_width)]
    transpose x3 -> x2, local copies, waits for them, and re-layouts: 2.68 us -> 1.38 us  [the longest x1 0.84 us: local(): observed.reshape(step_count, col_groups, own_rows, cols)]
  transfers between devices with their start and end apart: 8 -> 8, of which waited for: 8 -> 3; matrix products, arithmetic and copies ran while one was open for 1% -> 2% of each run, Pallas kernels for 0% -> 0%
where the time goes in v5:
time: 83.1 us; the launch traced here: 82.7 us
  waiting for transfers between devices  42.7 us (51%)
  starting transfers between devices  13.1 us (16%)
  blocking collectives  8.39 us (10%)
  matrix products  7.44 us (9%)
  other arithmetic  5 us (6%)
  local copies, waits for them, and re-layouts  4.56 us (5%)
  between operations  1.46 us (2%)
    ppermute x7, waiting for transfers between devices, local(): got = lax.ppermute(send, ('tm', 'col'), pairs)  29.1 us
    all_to_all x1, waiting for transfers between devices, local(): lax.all_to_all(packet, 'col', split_axis=0, concat_axis=0, tiled=True)  13.6 us
    ppermute x7, starting transfers between devices, local(): got = lax.ppermute(send, ('tm', 'col'), pairs)  8.78 us
    all_to_all x1, blocking collectives, local(): got = lax.all_to_all(mine, 'col', split_axis=0, concat_axis=0, tiled=True)  8.39 us
    dot_general x31, matrix products, split_dot(): lax.dot_general(both, weights, (((1,), (contract,)), ((), ())), preferred...  7.44 us
    all_to_all x1, starting transfers between devices, local(): lax.all_to_all(packet, 'col', split_axis=0, concat_axis=0, tiled=True)  4.37 us
  transfers between devices with their start and end apart: 8, of which 3 were waited for; matrix products, arithmetic and copies ran while one was open for 2% of the time, Pallas kernels for 0%

profile of v5, /device:TPU:0, one launch (start us, length us, event | category | flops | bytes accessed | tf_op | source)
XLA Modules:
  0.0 82.7 jit_solution(18379821047795007695)
XLA Ops:
  0.6 0.7 reduce-precision_convert_fusion.31
  1.4 0.8 %copy.31 = bf16[4,2,32,128]{3,2,1,0:T(8,128)(2,1)S(1)} copy(bf16[4,2,32,128]{3,2,0,1:T(8,128)(2,1)} %bitcast.202) | data formatting | bytes 131072 | tf_op jit(solution)/shard_map/transpose | solution.py:51
  2.2 1.1 %broadcast_in_dim.29 = bf16[4,1024,128]{2,1,0:T(8,128)(2,1)S(1)} broadcast(bf16[1024,128]{1,0:T(8,128)(2,1)} %bitcast.198), dimensions={1,2} | broadcast | bytes 1310720 | tf_op jit(solution)/shard_map/broadcast_in_dim | solution.py:55
  3.3 1.1 %pad_maximum_fusion = bf16[4,1104,128]{2,1,0:T(8,128)(2,1)} fusion(bf16[4,16,128]{2,1,0:T(8,128)(2,1)S(1)} %broadcast_in_dim.30, bf16[4,64,128]{2,1,0:T(8,128)(2,1)S(1)} %bitcast.199, bf16[4,1024,128]{2,1,0:T(8,128)(2,1)S(1)} %broadcast_in_dim.29), kind=kLoop, calls=%fused_computation | loop fusion | flops 3391488 | bytes 2260992 | tf_op jit(solution)/shard_map/concatenate | solution.py:53
  4.4 4.4 %all-to-all-start = ((bf16[4,1104,128]{2,1,0:T(8,128)(2,1)}), bf16[4,1104,128]{2,1,0:T(8,128)(2,1)S(1)}, u32[]{:S(2)}, u32[]{:S(2)}) async-start(bf16[4,1104,128]{2,1,0:T(8,128)(2,1)} %pad_maximum_fusion), calls=%async_computation | async-start | bytes 2260992 | tf_op jit(solution)/shard_map/all_to_all | solution.py:61
  8.9 0.2 broadcast_in_dim.31
  9.1 1.4 %mul.82 = bf16[512,512]{0,1:T(8,128)(2,1)} reshape(bf16[8,64,8,64]{1,0,3,2:T(8,128)(2,1)S(1)} %broadcast_in_dim.31) | data formatting | bytes 1048576 | tf_op jit(solution)/shard_map/mul | solution.py:68
  10.5 13.6 %all-to-all-done = bf16[4,1104,128]{2,1,0:T(8,128)(2,1)S(1)} async-done(((bf16[4,1104,128]{2,1,0:T(8,128)(2,1)}), bf16[4,1104,128]{2,1,0:T(8,128)(2,1)S(1)}, u32[]{:S(2)}, u32[]{:S(2)}) %all-to-all-start) | async-done | bytes 1130528 | tf_op jit(solution)/shard_map/all_to_all | solution.py:61
  24.4 0.5 copy.32
  24.9 1.2 %bitcast_multiply_fusion = bf16[2,512,512]{1,2,0:T(8,128)(2,1)S(1)} fusion(bf16[2,512,4,128]{1,3,2,0:T(8,128)(2,1)S(1)} %copy.32, bf16[512,512]{0,1:T(8,128)(2,1)} %mul.82), kind=kLoop, calls=%fused_computation.1 | loop fusion | flops 524288 | bytes 2621440 | tf_op jit(solution)/shard_map/mul | solution.py:68
  26.1 0.3 fusion.211
  26.5 0.2 fusion.95
  26.7 0.2 fusion.99
  26.9 0.3 fusion.91
  27.3 4.2 %collective-permute-start = (f32[32,512]{1,0:T(8,128)S(1)}, f32[32,512]{1,0:T(8,128)S(1)}, u32[]{:S(2)}, u32[]{:S(2)}) collective-permute-start(f32[32,512]{1,0:T(8,128)S(1)} %fusion.84), channel_id=1, source_target_pairs={{0,4},{1,5},{2,6},{3,7},{28,24},{29,25},{30,26},{31,27}} | collective-permute-start | bytes 196616 | tf_op jit(solution)/shard_map/ppermute | solution.py:113
  31.5 1.9 %collective-permute-done = f32[32,512]{1,0:T(8,128)S(1)} collective-permute-done((f32[32,512]{1,0:T(8,128)S(1)}, f32[32,512]{1,0:T(8,128)S(1)}, u32[]{:S(2)}, u32[]{:S(2)}) %collective-permute-start) | collective-permute-done | bytes 65568 | tf_op jit(solution)/shard_map/ppermute | solution.py:113
  33.4 0.3 fusion.103
  33.7 0.2 fusion.111
  33.9 0.2 fusion.115
  34.2 0.3 fusion.107
  34.5 0.7 collective-permute-start.1
  35.2 0.3 fusion.119
  35.5 0.2 fusion.127
  35.8 0.2 fusion.131
  36.0 0.3 fusion.123
  36.4 0.7 collective-permute-start.2
  37.1 0.3 fusion.135
  37.7 0.2 fusion.147
  37.9 0.3 fusion.139
  38.3 0.7 collective-permute-start.3
  39.0 0.3 fusion.151
  39.8 0.3 fusion.155
  40.1 0.7 collective-permute-start.4
  40.9 0.3 fusion.167
  41.5 0.2 fusion.179
  41.7 0.3 fusion.171
  42.0 0.7 collective-permute-start.5
  42.8 0.3 fusion.183
  43.1 0.2 fusion.191
  43.4 0.2 fusion.195
  43.6 0.3 fusion.187
  43.9 1.3 %collective-permute-start.6 = (f32[32,512]{1,0:T(8,128)S(1)}, f32[32,512]{1,0:T(8,128)S(1)}, u32[]{:S(2)}, u32[]{:S(2)}) collective-permute-start(f32[32,512]{1,0:T(8,128)S(1)} %fusion.36), channel_id=1, source_target_pairs={{24,28},{25,29},{26,30},{27,31},{4,0},{5,1},{6,2},{7,3}} | collective-permute-start | bytes 196616 | tf_op jit(solution)/shard_map/ppermute | solution.py:113
  45.2 27.2 %collective-permute-done.6 = f32[32,512]{1,0:T(8,128)S(1)} collective-permute-done((f32[32,512]{1,0:T(8,128)S(1)}, f32[32,512]{1,0:T(8,128)S(1)}, u32[]{:S(2)}, u32[]{:S(2)}) %collective-permute-start.6) | collective-permute-done | bytes 65568 | tf_op jit(solution)/shard_map/ppermute | solution.py:113
  72.5 0.3 fusion.199
  72.9 0.3 fusion.203
  73.1 0.2 fusion.207
  73.5 8.4 %all_to_all.10 = f32[4,2,2,32,128]{4,3,2,1,0:T(8,128)S(1)} all-to-all(f32[4,2,2,32,128]{4,3,2,1,0:T(8,128)S(1)} %maximum_bitcast_fusion), channel_id=1, replica_groups=mesh['tm'=8,'col'=4] {'col'}, dimensions={0} | all-to-all | bytes 524288 | tf_op jit(solution)/shard_map/all_to_all | solution.py:126
  82.0 0.7 add.388
  (95 shorter events, 2.6 us)
Async XLA Ops:
  4.4 4.4 %copy-start.1 = (s32[8,8]{1,0:T(8,128)S(1)}, s32[8,8]{1,0:T(8,128)}, u32[]{:S(2)}) copy-start(s32[8,8]{1,0:T(8,128)} %param.9) | copy-start | bytes 772
  4.4 19.7 %all-to-all-start = ((bf16[4,1104,128]{2,1,0:T(8,128)(2,1)}), bf16[4,1104,128]{2,1,0:T(8,128)(2,1)S(1)}, u32[]{:S(2)}, u32[]{:S(2)}) async-start(bf16[4,1104,128]{2,1,0:T(8,128)(2,1)} %pad_maximum_fusion), calls=%async_computation | async-start | bytes 2260992 | tf_op jit(solution)/shard_map/all_to_all | solution.py:61
  27.3 6.1 %collective-permute-start = (f32[32,512]{1,0:T(8,128)S(1)}, f32[32,512]{1,0:T(8,128)S(1)}, u32[]{:S(2)}, u32[]{:S(2)}) collective-permute-start(f32[32,512]{1,0:T(8,128)S(1)} %fusion.84), channel_id=1, source_target_pairs={{0,4},{1,5},{2,6},{3,7},{28,24},{29,25},{30,26},{31,27}} | collective-permute-start | bytes 196616 | tf_op jit(solution)/shard_map/ppermute | solution.py:113
  34.5 0.7 collective-permute-start.1
  36.4 0.7 collective-permute-start.2
  38.3 0.7 collective-permute-start.3
  40.1 0.7 collective-permute-start.4
  42.0 0.7 collective-permute-start.5
  43.9 28.5 %collective-permute-start.6 = (f32[32,512]{1,0:T(8,128)S(1)}, f32[32,512]{1,0:T(8,128)S(1)}, u32[]{:S(2)}, u32[]{:S(2)}) collective-permute-start(f32[32,512]{1,0:T(8,128)S(1)} %fusion.36), channel_id=1, source_target_pairs={{24,28},{25,29},{26,30},{27,31},{4,0},{5,1},{6,2},{7,3}} | collective-permute-start | bytes 196616 | tf_op jit(solution)/shard_map/ppermute | solution.py:113
  82.0 0.7 copy-start

commit v6 on v5

--- a/solution.py
+++ b/solution.py
@@ -105,9 +105,13 @@
     if time_groups <= 8 and time_groups % 2 == 0:
         last = time_groups - 1
         for k in range(last):
-            xs = forward(x_in)
-            es = backward(e_in)
-            send = jnp.where(tm_pos == k, xs[-1], es[-1])
+            send = lax.cond(
+                tm_pos == k,
+                lambda x, e: forward(x)[-1],
+                lambda x, e: backward(e)[-1],
+                x_in,
+                e_in,
+            )
             pairs = [(k * col_groups + c, (k + 1) * col_groups + c) for c in range(col_groups)]
             pairs += [((last - k) * col_groups + c, (last - k - 1) * col_groups + c) for c in range(col_groups)]
             got = lax.ppermute(send, ("tm", "col"), pairs)

time: 83.1 us -> 77.9 us (0.937)
  matrix products: 7.44 us -> 4.43 us
  other arithmetic: 5 us -> 3.47 us
  local copies, waits for them, and re-layouts: 4.56 us -> 3.19 us
    dot_general x31 -> x17, matrix products: 7.44 us -> 4.43 us  [split_dot(): lax.dot_general(both, weights, (((1,), (contract,)), ((), ())), preferred...]
    mul x1, other arithmetic: 1.22 us -> 0.22 us  [local(): packet[:, :n_coupling].reshape(col_groups, step_count, state_width, cols)...]
    all_to_all x1, waiting for transfers between devices: 13.6 us -> 14.5 us  [local(): lax.all_to_all(packet, 'col', split_axis=0, concat_axis=0, tiled=True)]
  transfers between devices with their start and end apart: 8 -> 8, of which waited for: 3 -> 3; matrix products, arithmetic and copies ran while one was open for 2% -> 1% of each run, Pallas kernels for 0% -> 0%
where the time goes in v6:
time: 77.9 us; the launch traced here: 77.5 us
  waiting for transfers between devices  43.3 us (56%)
  starting transfers between devices  13.2 us (17%)
  blocking collectives  8.39 us (11%)
  matrix products  4.43 us (6%)
  other arithmetic  3.47 us (4%)
  local copies, waits for them, and re-layouts  3.19 us (4%)
  between operations  1.1 us (1%)
    ppermute x7, waiting for transfers between devices, local(): got = lax.ppermute(send, ('tm', 'col'), pairs)  28.8 us
    all_to_all x1, waiting for transfers between devices, local(): lax.all_to_all(packet, 'col', split_axis=0, concat_axis=0, tiled=True)  14.5 us
    ppermute x7, starting transfers between devices, local(): got = lax.ppermute(send, ('tm', 'col'), pairs)  8.88 us
    all_to_all x1, blocking collectives, local(): got = lax.all_to_all(mine, 'col', split_axis=0, concat_axis=0, tiled=True)  8.39 us
    dot_general x17, matrix products, split_dot(): lax.dot_general(both, weights, (((1,), (contract,)), ((), ())), preferred...  4.43 us
    all_to_all x1, starting transfers between devices, local(): lax.all_to_all(packet, 'col', split_axis=0, concat_axis=0, tiled=True)  4.37 us
  transfers between devices with their start and end apart: 8, of which 3 were waited for; matrix products, arithmetic and copies ran while one was open for 1% of the time, Pallas kernels for 0%

profile of v6, /device:TPU:0, one launch (start us, length us, event | category | flops | bytes accessed | tf_op | source)
XLA Modules:
  0.0 77.5 jit_solution(14175987216981855931)
XLA Ops:
  0.6 0.7 reduce-precision_convert_fusion.31
  1.4 0.8 %copy.23 = bf16[4,2,32,128]{3,2,1,0:T(8,128)(2,1)S(1)} copy(bf16[4,2,32,128]{3,2,0,1:T(8,128)(2,1)} %bitcast.320) | data formatting | bytes 131072 | tf_op jit(solution)/shard_map/transpose | solution.py:51
  2.2 1.1 %broadcast_in_dim.29 = bf16[4,1024,128]{2,1,0:T(8,128)(2,1)S(1)} broadcast(bf16[1024,128]{1,0:T(8,128)(2,1)} %bitcast.316), dimensions={1,2} | broadcast | bytes 1310720 | tf_op jit(solution)/shard_map/broadcast_in_dim | solution.py:55
  3.3 1.1 %pad_maximum_fusion = bf16[4,1104,128]{2,1,0:T(8,128)(2,1)} fusion(bf16[4,16,128]{2,1,0:T(8,128)(2,1)S(1)} %broadcast_in_dim.30, bf16[4,64,128]{2,1,0:T(8,128)(2,1)S(1)} %bitcast.317, bf16[4,1024,128]{2,1,0:T(8,128)(2,1)S(1)} %broadcast_in_dim.29), kind=kLoop, calls=%fused_computation.359 | loop fusion | flops 3391488 | bytes 2260992 | tf_op jit(solution)/shard_map/concatenate | solution.py:53
  4.4 4.4 %all-to-all-start = ((bf16[4,1104,128]{2,1,0:T(8,128)(2,1)}), bf16[4,1104,128]{2,1,0:T(8,128)(2,1)S(1)}, u32[]{:S(2)}, u32[]{:S(2)}) async-start(bf16[4,1104,128]{2,1,0:T(8,128)(2,1)} %pad_maximum_fusion), calls=%async_computation | async-start | bytes 2260992 | tf_op jit(solution)/shard_map/all_to_all | solution.py:61
  8.8 0.2 broadcast_in_dim.31
  9.0 0.6 mul.324
  9.6 14.5 %all-to-all-done = bf16[4,1104,128]{2,1,0:T(8,128)(2,1)S(1)} async-done(((bf16[4,1104,128]{2,1,0:T(8,128)(2,1)}), bf16[4,1104,128]{2,1,0:T(8,128)(2,1)S(1)}, u32[]{:S(2)}, u32[]{:S(2)}) %all-to-all-start) | async-done | bytes 1130528 | tf_op jit(solution)/shard_map/all_to_all | solution.py:61
  24.1 0.1 copy.39
  24.2 0.1 reshape.170
  24.3 0.1 slice.584
  24.4 0.2 bitcast_multiply_fusion.1
  24.6 0.6 conditional.7
  24.6 0.2 fusion.21
  25.0 0.2 fusion.19
  25.2 4.3 %collective-permute-start = (f32[32,512]{1,0:T(8,128)S(1)}, f32[32,512]{1,0:T(8,128)S(1)}, u32[]{:S(2)}, u32[]{:S(2)}) collective-permute-start(f32[32,512]{1,0:T(8,128)S(1)} %get-tuple-element.298), channel_id=1, source_target_pairs={{0,4},{1,5},{2,6},{3,7},{28,24},{29,25},{30,26},{31,27}} | collective-permute-start | bytes 196616 | tf_op jit(solution)/shard_map/ppermute | solution.py:117
  29.5 1.9 %collective-permute-done = f32[32,512]{1,0:T(8,128)S(1)} collective-permute-done((f32[32,512]{1,0:T(8,128)S(1)}, f32[32,512]{1,0:T(8,128)S(1)}, u32[]{:S(2)}, u32[]{:S(2)}) %collective-permute-start) | collective-permute-done | bytes 65568 | tf_op jit(solution)/shard_map/ppermute | solution.py:117
  31.4 0.7 conditional.8
  31.4 0.3 fusion.37
  31.7 0.3 fusion.35
  32.1 0.7 collective-permute-start.1
  32.8 0.7 conditional.9
  32.8 0.3 fusion.76
  33.2 0.3 fusion.74
  33.5 0.7 collective-permute-start.2
  34.2 0.7 conditional.10
  34.2 0.3 fusion.115
  34.6 0.3 fusion.113
  34.9 0.7 collective-permute-start.3
  35.6 0.7 conditional.11
  35.6 0.3 fusion.154
  36.0 0.3 fusion.152
  36.3 0.7 collective-permute-start.4
  37.0 0.7 conditional.12
  37.0 0.3 fusion.193
  37.4 0.3 fusion.191
  37.7 0.7 collective-permute-start.5
  38.4 0.7 conditional.13
  38.4 0.3 fusion.232
  38.8 0.3 fusion.230
  39.1 1.3 %collective-permute-start.6 = (f32[32,512]{1,0:T(8,128)S(1)}, f32[32,512]{1,0:T(8,128)S(1)}, u32[]{:S(2)}, u32[]{:S(2)}) collective-permute-start(f32[32,512]{1,0:T(8,128)S(1)} %get-tuple-element.304), channel_id=1, source_target_pairs={{24,28},{25,29},{26,30},{27,31},{4,0},{5,1},{6,2},{7,3}} | collective-permute-start | bytes 196616 | tf_op jit(solution)/shard_map/ppermute | solution.py:117
  40.4 26.9 %collective-permute-done.6 = f32[32,512]{1,0:T(8,128)S(1)} collective-permute-done((f32[32,512]{1,0:T(8,128)S(1)}, f32[32,512]{1,0:T(8,128)S(1)}, u32[]{:S(2)}, u32[]{:S(2)}) %collective-permute-start.6) | collective-permute-done | bytes 65568 | tf_op jit(solution)/shard_map/ppermute | solution.py:117
  67.4 0.2 fusion.269
  67.7 0.3 fusion.270
  68.0 0.2 fusion.271
  68.4 8.4 %all_to_all.10 = f32[4,2,2,32,128]{4,3,2,1,0:T(8,128)S(1)} all-to-all(f32[4,2,2,32,128]{4,3,2,1,0:T(8,128)S(1)} %maximum_bitcast_fusion), channel_id=1, replica_groups=mesh['tm'=8,'col'=4] {'col'}, dimensions={0} | all-to-all | bytes 524288 | tf_op jit(solution)/shard_map/all_to_all | solution.py:130
  76.8 0.0 copy-start
  76.8 0.7 add.305
  (79 shorter events, 1.0 us)
Async XLA Ops:
  4.4 4.4 %copy-start.1 = (s32[8,8]{1,0:T(8,128)S(1)}, s32[8,8]{1,0:T(8,128)}, u32[]{:S(2)}) copy-start(s32[8,8]{1,0:T(8,128)} %param.23) | copy-start | bytes 772
  4.4 19.7 %all-to-all-start = ((bf16[4,1104,128]{2,1,0:T(8,128)(2,1)}), bf16[4,1104,128]{2,1,0:T(8,128)(2,1)S(1)}, u32[]{:S(2)}, u32[]{:S(2)}) async-start(bf16[4,1104,128]{2,1,0:T(8,128)(2,1)} %pad_maximum_fusion), calls=%async_computation | async-start | bytes 2260992 | tf_op jit(solution)/shard_map/all_to_all | solution.py:61
  25.2 6.2 %collective-permute-start = (f32[32,512]{1,0:T(8,128)S(1)}, f32[32,512]{1,0:T(8,128)S(1)}, u32[]{:S(2)}, u32[]{:S(2)}) collective-permute-start(f32[32,512]{1,0:T(8,128)S(1)} %get-tuple-element.298), channel_id=1, source_target_pairs={{0,4},{1,5},{2,6},{3,7},{28,24},{29,25},{30,26},{31,27}} | collective-permute-start | bytes 196616 | tf_op jit(solution)/shard_map/ppermute | solution.py:117
  32.1 0.7 collective-permute-start.1
  33.5 0.7 collective-permute-start.2
  34.9 0.7 collective-permute-start.3
  36.3 0.7 collective-permute-start.4
  37.7 0.7 collective-permute-start.5
  39.1 28.2 %collective-permute-start.6 = (f32[32,512]{1,0:T(8,128)S(1)}, f32[32,512]{1,0:T(8,128)S(1)}, u32[]{:S(2)}, u32[]{:S(2)}) collective-permute-start(f32[32,512]{1,0:T(8,128)S(1)} %get-tuple-element.304), channel_id=1, source_target_pairs={{24,28},{25,29},{26,30},{27,31},{4,0},{5,1},{6,2},{7,3}} | collective-permute-start | bytes 196616 | tf_op jit(solution)/shard_map/ppermute | solution.py:117
  76.8 0.7 copy-start

commit v7 on v6

--- a/solution.py
+++ b/solution.py
@@ -104,33 +104,44 @@
     x_in, e_in = zeros, zeros
     if time_groups <= 8 and time_groups % 2 == 0:
         last = time_groups - 1
-        for k in range(last):
-            send = lax.cond(
+        kept_x = jnp.zeros(driven.shape, jnp.float32)
+        kept_e = kept_x
+        for k in range(time_groups):
+            outs = lax.cond(
                 tm_pos == k,
-                lambda x, e: forward(x)[-1],
-                lambda x, e: backward(e)[-1],
+                lambda x, e: jnp.stack(forward(x)),
+                lambda x, e: jnp.stack(backward(e)),
                 x_in,
                 e_in,
             )
-            pairs = [(k * col_groups + c, (k + 1) * col_groups + c) for c in range(col_groups)]
-            pairs += [((last - k) * col_groups + c, (last - k - 1) * col_groups + c) for c in range(col_groups)]
-            got = lax.ppermute(send, ("tm", "col"), pairs)
-            x_in = jnp.where(tm_pos == k + 1, got, x_in)
-            e_in = jnp.where(tm_pos == last - k - 1, got, e_in)
+            kept_x = jnp.where(tm_pos == k, outs, kept_x)
+            kept_e = jnp.where(tm_pos == last - k, outs, kept_e)
+            if k < last:
+                pairs = [(k * col_groups + c, (k + 1) * col_groups + c) for c in range(col_groups)]
+                pairs += [
+                    ((last - k) * col_groups + c, (last - k - 1) * col_groups + c)
+                    for c in range(col_groups)
+                ]
+                got = lax.ppermute(outs[-1], ("tm", "col"), pairs)
+                x_in = jnp.where(tm_pos == k + 1, got, x_in)
+                e_in = jnp.where(tm_pos == last - k - 1, got, e_in)
+        xs = [kept_x[k] for k in range(step_count)]
+        es = [kept_e[k] for k in range(step_count)]
     else:
         def stage(_, carry):
             x, e = carry
             return passed_along(forward(x)[-1], "tm", 1), passed_along(backward(e)[-1], "tm", -1)
 
         x_in, e_in = lax.fori_loop(0, time_groups - 1, stage, (x_in, e_in))
-    xs = forward(x_in)
-    es = backward(e_in)
-    mine = jnp.stack([jnp.stack(xs), jnp.stack([es[step_count - 2 - k] if k < step_count - 1 else e_in for k in range(step_count)])])
+        xs = forward(x_in)
+        es = backward(e_in)
+    filtered = jnp.stack(xs)
+    correction = jnp.stack([es[step_count - 2 - k] for k in range(step_count - 1)] + [e_in])
+    mine = jnp.stack([filtered, filtered + correction])
     mine = mine.reshape(2, step_count, own_rows, col_groups, cols).transpose(3, 0, 1, 2, 4)
     got = lax.all_to_all(mine, "col", split_axis=0, concat_axis=0, tiled=True)
     got = got.transpose(1, 2, 0, 3, 4).reshape(2, step_count, rows, cols)
-    filtered = got[0]
-    return filtered, filtered + got[1]
+    return got[0], got[1]
 
 
 def solution(mesh):

time: 77.9 us -> 78.2 us (level)
    dot_general x17 -> x16, matrix products: 4.43 us -> 4.3 us  [split_dot(): lax.dot_general(both, weights, (((1,), (contract,)), ((), ())), preferred...]
where the time goes in v7:
time: 78.2 us; the launch traced here: 77.7 us
  waiting for transfers between devices  43.3 us (55%)
  starting transfers between devices  13.3 us (17%)
  blocking collectives  8.39 us (11%)
  matrix products  4.3 us (5%)
  local copies, waits for them, and re-layouts  3.81 us (5%)
  other arithmetic  3.1 us (4%)
  between operations  1.08 us (1%)
    ppermute x7, waiting for transfers between devices, local(): got = lax.ppermute(outs[-1], ('tm', 'col'), pairs)  28.8 us
    all_to_all x1, waiting for transfers between devices, local(): lax.all_to_all(packet, 'col', split_axis=0, concat_axis=0, tiled=True)  14.5 us
    ppermute x7, starting transfers between devices, local(): got = lax.ppermute(outs[-1], ('tm', 'col'), pairs)  8.88 us
    all_to_all x1, blocking collectives, local(): got = lax.all_to_all(mine, 'col', split_axis=0, concat_axis=0, tiled=True)  8.39 us
    all_to_all x1, starting transfers between devices, local(): lax.all_to_all(packet, 'col', split_axis=0, concat_axis=0, tiled=True)  4.37 us
    dot_general x16, matrix products, split_dot(): lax.dot_general(both, weights, (((1,), (contract,)), ((), ())), preferred...  4.3 us
  transfers between devices with their start and end apart: 8, of which 3 were waited for; matrix products, arithmetic and copies ran while one was open for 1% of the time, Pallas kernels for 0%

profile of v7, /device:TPU:0, one launch (start us, length us, event | category | flops | bytes accessed | tf_op | source)
XLA Modules:
  0.0 77.7 jit_solution(261184393862526636)
XLA Ops:
  0.6 0.7 reduce-precision_convert_fusion.32
  1.4 0.8 %copy.19 = bf16[4,2,32,128]{3,2,1,0:T(8,128)(2,1)S(1)} copy(bf16[4,2,32,128]{3,2,0,1:T(8,128)(2,1)} %bitcast.448) | data formatting | bytes 131072 | tf_op jit(solution)/shard_map/transpose | solution.py:51
  2.2 1.1 %broadcast_in_dim.32 = bf16[4,1024,128]{2,1,0:T(8,128)(2,1)S(1)} broadcast(bf16[1024,128]{1,0:T(8,128)(2,1)} %bitcast.442), dimensions={1,2} | broadcast | bytes 1310720 | tf_op jit(solution)/shard_map/broadcast_in_dim | solution.py:55
  3.3 1.1 %pad_maximum_fusion.16 = bf16[4,1104,128]{2,1,0:T(8,128)(2,1)} fusion(bf16[4,16,128]{2,1,0:T(8,128)(2,1)S(1)} %broadcast_in_dim.33, bf16[4,64,128]{2,1,0:T(8,128)(2,1)S(1)} %bitcast.443, bf16[4,1024,128]{2,1,0:T(8,128)(2,1)S(1)} %broadcast_in_dim.32), kind=kLoop, calls=%fused_computation.444 | loop fusion | flops 3391488 | bytes 2260992 | tf_op jit(solution)/shard_map/concatenate | solution.py:53
  4.4 4.4 %all-to-all-start = ((bf16[4,1104,128]{2,1,0:T(8,128)(2,1)}), bf16[4,1104,128]{2,1,0:T(8,128)(2,1)S(1)}, u32[]{:S(2)}, u32[]{:S(2)}) async-start(bf16[4,1104,128]{2,1,0:T(8,128)(2,1)} %pad_maximum_fusion.16), calls=%async_computation | async-start | bytes 2260992 | tf_op jit(solution)/shard_map/all_to_all | solution.py:61
  8.8 0.2 broadcast_in_dim.34
  9.0 0.6 mul.338
  9.6 14.5 %all-to-all-done = bf16[4,1104,128]{2,1,0:T(8,128)(2,1)S(1)} async-done(((bf16[4,1104,128]{2,1,0:T(8,128)(2,1)}), bf16[4,1104,128]{2,1,0:T(8,128)(2,1)S(1)}, u32[]{:S(2)}, u32[]{:S(2)}) %all-to-all-start) | async-done | bytes 1130528 | tf_op jit(solution)/shard_map/all_to_all | solution.py:61
  24.2 0.1 slice.632
  24.3 0.2 bitcast_multiply_fusion.1
  24.5 0.6 conditional.8
  24.5 0.2 fusion.21
  24.8 0.2 fusion.19
  25.1 4.3 %collective-permute-start = (f32[32,512]{1,0:T(8,128)S(1)}, f32[32,512]{1,0:T(8,128)S(1)}, u32[]{:S(2)}, u32[]{:S(2)}) collective-permute-start(f32[32,512]{1,0:T(8,128)S(1)} %slice_bitcast_fusion.6), channel_id=1, source_target_pairs={{0,4},{1,5},{2,6},{3,7},{28,24},{29,25},{30,26},{31,27}} | collective-permute-start | bytes 196616 | tf_op jit(solution)/shard_map/ppermute | solution.py:125
  29.4 1.9 %collective-permute-done = f32[32,512]{1,0:T(8,128)S(1)} collective-permute-done((f32[32,512]{1,0:T(8,128)S(1)}, f32[32,512]{1,0:T(8,128)S(1)}, u32[]{:S(2)}, u32[]{:S(2)}) %collective-permute-start) | collective-permute-done | bytes 65568 | tf_op jit(solution)/shard_map/ppermute | solution.py:125
  31.3 0.7 conditional.9
  31.3 0.3 fusion.38
  31.7 0.3 fusion.36
  32.0 0.7 collective-permute-start.1
  32.7 0.7 conditional.10
  32.8 0.3 fusion.78
  33.1 0.3 fusion.76
  33.5 0.7 collective-permute-start.2
  34.1 0.0 collective-permute-done.2
  34.2 0.7 conditional.11
  34.2 0.3 fusion.118
  34.6 0.3 fusion.116
  34.9 0.7 collective-permute-start.3
  35.6 0.7 conditional.12
  35.7 0.3 fusion.158
  36.0 0.3 fusion.156
  36.3 0.7 collective-permute-start.4
  37.1 0.7 conditional.13
  37.1 0.3 fusion.198
  37.4 0.3 fusion.196
  37.8 0.7 collective-permute-start.5
  38.5 0.7 conditional.14
  38.5 0.3 fusion.238
  38.9 0.3 fusion.236
  39.2 1.3 %collective-permute-start.6 = (f32[32,512]{1,0:T(8,128)S(1)}, f32[32,512]{1,0:T(8,128)S(1)}, u32[]{:S(2)}, u32[]{:S(2)}) collective-permute-start(f32[32,512]{1,0:T(8,128)S(1)} %slice_bitcast_fusion), channel_id=1, source_target_pairs={{24,28},{25,29},{26,30},{27,31},{4,0},{5,1},{6,2},{7,3}} | collective-permute-start | bytes 196616 | tf_op jit(solution)/shard_map/ppermute | solution.py:125
  40.6 26.9 %collective-permute-done.6 = f32[32,512]{1,0:T(8,128)S(1)} collective-permute-done((f32[32,512]{1,0:T(8,128)S(1)}, f32[32,512]{1,0:T(8,128)S(1)}, u32[]{:S(2)}, u32[]{:S(2)}) %collective-permute-start.6) | collective-permute-done | bytes 65568 | tf_op jit(solution)/shard_map/ppermute | solution.py:125
  67.5 0.7 conditional.15
  67.5 0.3 fusion.278
  67.9 0.3 fusion.276
  68.3 0.1 maximum_add_fusion
  68.5 0.1 maximum_bitcast_fusion
  68.6 8.4 %all_to_all.10 = f32[4,2,2,32,128]{4,3,2,1,0:T(8,128)S(1)} all-to-all(f32[4,2,2,32,128]{4,3,2,1,0:T(8,128)S(1)} %copy.23), channel_id=1, replica_groups=mesh['tm'=8,'col'=4] {'col'}, dimensions={0} | all-to-all | bytes 524288 | tf_op jit(solution)/shard_map/all_to_all | solution.py:142
  77.0 0.7 fusion.350
  (88 shorter events, 1.2 us)
Async XLA Ops:
  4.4 4.4 %copy-start = (s32[8,8]{1,0:T(8,128)S(1)}, s32[8,8]{1,0:T(8,128)}, u32[]{:S(2)}) copy-start(s32[8,8]{1,0:T(8,128)} %param.25) | copy-start | bytes 772
  4.4 19.7 %all-to-all-start = ((bf16[4,1104,128]{2,1,0:T(8,128)(2,1)}), bf16[4,1104,128]{2,1,0:T(8,128)(2,1)S(1)}, u32[]{:S(2)}, u32[]{:S(2)}) async-start(bf16[4,1104,128]{2,1,0:T(8,128)(2,1)} %pad_maximum_fusion.16), calls=%async_computation | async-start | bytes 2260992 | tf_op jit(solution)/shard_map/all_to_all | solution.py:61
  25.1 6.2 %collective-permute-start = (f32[32,512]{1,0:T(8,128)S(1)}, f32[32,512]{1,0:T(8,128)S(1)}, u32[]{:S(2)}, u32[]{:S(2)}) collective-permute-start(f32[32,512]{1,0:T(8,128)S(1)} %slice_bitcast_fusion.6), channel_id=1, source_target_pairs={{0,4},{1,5},{2,6},{3,7},{28,24},{29,25},{30,26},{31,27}} | collective-permute-start | bytes 196616 | tf_op jit(solution)/shard_map/ppermute | solution.py:125
  32.0 0.7 collective-permute-start.1
  33.5 0.7 collective-permute-start.2
  34.9 0.7 collective-permute-start.3
  36.3 0.7 collective-permute-start.4
  37.8 0.7 collective-permute-start.5
  39.2 28.3 %collective-permute-start.6 = (f32[32,512]{1,0:T(8,128)S(1)}, f32[32,512]{1,0:T(8,128)S(1)}, u32[]{:S(2)}, u32[]{:S(2)}) collective-permute-start(f32[32,512]{1,0:T(8,128)S(1)} %slice_bitcast_fusion), channel_id=1, source_target_pairs={{24,28},{25,29},{26,30},{27,31},{4,0},{5,1},{6,2},{7,3}} | collective-permute-start | bytes 196616 | tf_op jit(solution)/shard_map/ppermute | solution.py:125

commit v8 on v6

--- a/solution.py
+++ b/solution.py
@@ -43,6 +43,7 @@
     own_rows = rows // col_groups
     tm_pos = lax.axis_index("tm")
 
+    col_pos = lax.axis_index("col")
     small = jnp.concatenate([persist, input_gain[None]], axis=0)
     small_rows = 3 * (step_count + 1)
     small_pad = -small_rows % 16
@@ -50,15 +51,21 @@
     coupling_rows = coupling.reshape(step_count * state_width, cols)
     seen_parts = observed.reshape(step_count, col_groups, own_rows, cols).transpose(1, 0, 2, 3)
     seen_parts = seen_parts.reshape(col_groups, step_count * own_rows, cols)
-    packet = jnp.concatenate(
-        [
-            jnp.broadcast_to(coupling_rows[None], (col_groups,) + coupling_rows.shape),
-            seen_parts,
-            jnp.broadcast_to(small_pieces[None], (col_groups,) + small_pieces.shape),
-        ],
-        axis=1,
-    )
-    packet = lax.all_to_all(packet, "col", split_axis=0, concat_axis=0, tiled=True)
+    chunks = []
+    for shift in range(col_groups):
+        dest = (col_pos + shift) % col_groups
+        seen_d = lax.dynamic_index_in_dim(seen_parts, dest, 0, keepdims=False)
+        chunk = jnp.concatenate([coupling_rows, seen_d, small_pieces], axis=0)
+        if shift:
+            pairs = [
+                (t * col_groups + c, t * col_groups + (c + shift) % col_groups)
+                for t in range(time_groups)
+                for c in range(col_groups)
+            ]
+            chunk = lax.ppermute(chunk, ("tm", "col"), pairs)
+        chunks.append(chunk)
+    by_shift = jnp.stack(chunks[::-1] + chunks[::-1])
+    packet = lax.dynamic_slice_in_dim(by_shift, col_groups - 1 - col_pos, col_groups, 0)
     n_coupling = step_count * state_width
     n_seen = step_count * own_rows
     mask = jnp.broadcast_to(

time: 77.9 us -> 83.3 us (1.069)
  local copies, waits for them, and re-layouts: 3.19 us -> 9.04 us
  other arithmetic: 3.47 us -> 7.78 us
  waiting for transfers between devices: 43.3 us -> 39.8 us
  starting transfers between devices: 13.2 us -> 11.6 us
    all_to_all x1 -> x0, waiting for transfers between devices: 14.5 us -> none  [local(): lax.all_to_all(packet, 'col', split_axis=0, concat_axis=0, tiled=True)]
    ppermute x0 -> x3, waiting for transfers between devices: none -> 11 us  [local(): chunk = lax.ppermute(chunk, ('tm', 'col'), pairs)]
    unnamed x6 -> x12, local copies, waits for them, and re-layouts: 0.02 us -> 4.45 us
    all_to_all x1 -> x0, starting transfers between devices: 4.37 us -> none  [local(): lax.all_to_all(packet, 'col', split_axis=0, concat_axis=0, tiled=True)]
    ppermute x0 -> x3, starting transfers between devices: none -> 3.2 us  [local(): chunk = lax.ppermute(chunk, ('tm', 'col'), pairs)]
    slice x1 -> x2, local copies, waits for them, and re-layouts: 0.07 us -> 2.11 us  [local(): packet[:, :n_coupling].reshape(col_groups, step_count, state_width, cols)]
    broadcast_in_dim x2 -> x0, local copies, waits for them, and re-layouts: 1.09 us -> none  [the longest x1 1.09 us: local(): jnp.broadcast_to(coupling_rows[None], (col_groups,) + coupling_rows.shape)]
    convert_element_type x0 -> x1, other arithmetic: none -> 0.86 us  [local(): driven = gain[None, None, :] * seen.astype(jnp.float32)]
  transfers between devices with their start and end apart: 8 -> 10, of which waited for: 3 -> 4; matrix products, arithmetic and copies ran while one was open for 1% -> 4% of each run, Pallas kernels for 0% -> 0%
where the time goes in v8:
time: 83.3 us; the launch traced here: 82.8 us
  waiting for transfers between devices  39.8 us (48%)
  starting transfers between devices  11.6 us (14%)
  local copies, waits for them, and re-layouts  9.04 us (11%)
  blocking collectives  8.57 us (10%)
  other arithmetic  7.78 us (9%)
  matrix products  4.43 us (5%)
  between operations  1.18 us (1%)
    ppermute x7, waiting for transfers between devices, local(): got = lax.ppermute(send, ('tm', 'col'), pairs)  28.8 us
    ppermute x3, waiting for transfers between devices, local(): chunk = lax.ppermute(chunk, ('tm', 'col'), pairs)  11 us
    all_to_all x1, blocking collectives, local(): got = lax.all_to_all(mine, 'col', split_axis=0, concat_axis=0, tiled=True)  8.57 us
    ppermute x7, starting transfers between devices, local(): got = lax.ppermute(send, ('tm', 'col'), pairs)  8.39 us
    unnamed x12, local copies, waits for them, and re-layouts  4.45 us
    dot_general x17, matrix products, split_dot(): lax.dot_general(both, weights, (((1,), (contract,)), ((), ())), preferred...  4.43 us
    ppermute x3, starting transfers between devices, local(): chunk = lax.ppermute(chunk, ('tm', 'col'), pairs)  3.2 us
    slice x2, local copies, waits for them, and re-layouts, local(): packet[:, :n_coupling].reshape(col_groups, step_count, state_width, cols)  2.11 us
  transfers between devices with their start and end apart: 10, of which 4 were waited for; matrix products, arithmetic and copies ran while one was open for 4% of the time, Pallas kernels for 0%

profile of v8, /device:TPU:0, one launch (start us, length us, event | category | flops | bytes accessed | tf_op | source)
XLA Modules:
  0.0 82.8 jit_solution(2690698590683046076)
XLA Ops:
  0.7 0.8 %copy.31 = bf16[4,2,32,128]{3,2,1,0:T(8,128)(2,1)S(1)} copy(bf16[4,2,32,128]{3,2,0,1:T(8,128)(2,1)} %bitcast.339) | data formatting | bytes 131072 | tf_op jit(solution)/shard_map/transpose | solution.py:52
  1.5 0.7 reduce-precision_convert_fusion.31
  2.3 1.8 %fusion.273 = (bf16[1104,128]{1,0:T(8,128)(2,1)S(1)}, bf16[1104,128]{1,0:T(8,128)(2,1)}, bf16[1104,128]{1,0:T(8,128)(2,1)S(1)}) fusion(bf16[9,128]{1,0:T(8,128)(2,1)S(1)} %convert_element_type.57, bf16[64,128]{1,0:T(8,128)(2,1)S(1)} %get-tuple-element.296, bf16[1024,128]{1,0:T(8,128)(2,1)} %bitcast.315, bf16[64,128]{1,0:T(8,128)(2,1)S(1)} %get-tuple-element.298, ...), kind=kLoop, calls=%fused_computation.367 | loop fusion | flops 2260992 | bytes 1161472 | tf_op jit(solution)/shard_map/concatenate | solution.py:58
  4.1 2.4 %collective-permute-start = (bf16[1104,128]{1,0:T(8,128)(2,1)}, bf16[1104,128]{1,0:T(8,128)(2,1)S(1)}, u32[]{:S(2)}, u32[]{:S(2)}) collective-permute-start(bf16[1104,128]{1,0:T(8,128)(2,1)} %get-tuple-element.274), channel_id=1, source_target_pairs={{0,3},{1,0},{2,1},{3,2},{4,7},{5,4},{6,5},{7,6},{8,11},{9,8},{10,9... | collective-permute-start | bytes 847880 | tf_op jit(solution)/shard_map/ppermute | solution.py:65
  6.5 0.6 collective-permute-start.1
  7.3 0.7 convert_element_type.88
  8.2 0.6 mul.324
  8.8 5.1 %collective-permute-done = bf16[1104,128]{1,0:T(8,128)(2,1)S(1)} collective-permute-done((bf16[1104,128]{1,0:T(8,128)(2,1)}, bf16[1104,128]{1,0:T(8,128)(2,1)S(1)}, u32[]{:S(2)}, u32[]{:S(2)}) %collective-permute-start) | collective-permute-done | bytes 282656 | tf_op jit(solution)/shard_map/ppermute | solution.py:65
  13.9 0.7 bitcast_dynamic-update-slice_fusion.4
  14.7 5.9 %collective-permute-done.1 = bf16[1104,128]{1,0:T(8,128)(2,1)S(1)} collective-permute-done((bf16[1104,128]{1,0:T(8,128)(2,1)S(1)}, bf16[1104,128]{1,0:T(8,128)(2,1)S(1)}, u32[]{:S(2)}, u32[]{:S(2)}) %collective-permute-start.1) | collective-permute-done | bytes 282656 | tf_op jit(solution)/shard_map/ppermute | solution.py:65
  20.5 0.7 bitcast_dynamic-update-slice_fusion.2
  21.2 0.7 bitcast_dynamic-update-slice_fusion
  22.0 0.7 fusion.278
  22.7 0.7 bitcast_dynamic-update-slice_fusion.5
  23.5 0.7 bitcast_dynamic-update-slice_fusion.3
  24.2 0.8 bitcast_dynamic-update-slice_fusion.1
  25.0 0.7 fusion.279
  25.7 1.3 %constant_dynamic-slice_fusion = bf16[4,1024,128]{2,1,0:T(8,128)(2,1)S(1)} fusion(bf16[8,1104,128]{2,1,0:T(8,128)(2,1)} %fusion.279, s32[]{:T(128)S(6)} %select_n.118), kind=kLoop, calls=%fused_computation.447 | loop fusion | bytes 2097156 | tf_op jit(solution)/shard_map/slice | solution.py:76
  27.0 0.7 dynamic-slice_convert_fusion.1
  27.8 0.8 copy.34
  28.6 0.4 reshape.169
  29.0 0.9 %dynamic-slice_convert_fusion = f32[4,64,128]{2,1,0:T(8,128)S(1)} fusion(bf16[8,1104,128]{2,1,0:T(8,128)(2,1)} %fusion.279, s32[]{:T(128)S(6)} %select_n.118, s32[]{:T(128)S(6)} %add.358), kind=kLoop, calls=%fused_computation.401 | loop fusion | flops 32768 | bytes 196616 | tf_op jit(solution)/shard_map/convert_element_type | solution.py:93
  30.2 0.6 conditional.7
  30.8 3.8 %collective-permute-start.3 = (f32[32,512]{1,0:T(8,128)S(1)}, f32[32,512]{1,0:T(8,128)S(1)}, u32[]{:S(2)}, u32[]{:S(2)}) collective-permute-start(f32[32,512]{1,0:T(8,128)S(1)} %get-tuple-element.305), channel_id=1, source_target_pairs={{0,4},{1,5},{2,6},{3,7},{28,24},{29,25},{30,26},{31,27}} | collective-permute-start | bytes 196616 | tf_op jit(solution)/shard_map/ppermute | solution.py:124
  34.6 1.9 %collective-permute-done.3 = f32[32,512]{1,0:T(8,128)S(1)} collective-permute-done((f32[32,512]{1,0:T(8,128)S(1)}, f32[32,512]{1,0:T(8,128)S(1)}, u32[]{:S(2)}, u32[]{:S(2)}) %collective-permute-start.3) | collective-permute-done | bytes 65568 | tf_op jit(solution)/shard_map/ppermute | solution.py:124
  36.5 0.7 conditional.8
  36.5 0.3 fusion.37
  36.8 0.3 fusion.35
  37.2 0.7 collective-permute-start.4
  37.9 0.7 conditional.9
  37.9 0.3 fusion.76
  38.6 0.7 collective-permute-start.5
  39.3 0.7 conditional.10
  39.7 0.3 fusion.113
  40.0 0.7 collective-permute-start.6
  40.7 0.7 conditional.11
  40.7 0.3 fusion.154
  41.1 0.3 fusion.152
  41.4 0.7 collective-permute-start.7
  42.1 0.7 conditional.12
  42.1 0.3 fusion.193
  42.8 0.7 collective-permute-start.8
  43.5 0.7 conditional.13
  44.2 1.3 %collective-permute-start.9 = (f32[32,512]{1,0:T(8,128)S(1)}, f32[32,512]{1,0:T(8,128)S(1)}, u32[]{:S(2)}, u32[]{:S(2)}) collective-permute-start(f32[32,512]{1,0:T(8,128)S(1)} %get-tuple-element.311), channel_id=1, source_target_pairs={{24,28},{25,29},{26,30},{27,31},{4,0},{5,1},{6,2},{7,3}} | collective-permute-start | bytes 196616 | tf_op jit(solution)/shard_map/ppermute | solution.py:124
  45.5 26.9 %collective-permute-done.9 = f32[32,512]{1,0:T(8,128)S(1)} collective-permute-done((f32[32,512]{1,0:T(8,128)S(1)}, f32[32,512]{1,0:T(8,128)S(1)}, u32[]{:S(2)}, u32[]{:S(2)}) %collective-permute-start.9) | collective-permute-done | bytes 65568 | tf_op jit(solution)/shard_map/ppermute | solution.py:124
  72.8 0.3 fusion.271
  73.5 8.6 %all_to_all.5 = f32[4,2,2,32,128]{4,3,2,1,0:T(8,128)S(1)} all-to-all(f32[4,2,2,32,128]{4,3,2,1,0:T(8,128)S(1)} %maximum_bitcast_fusion), channel_id=1, replica_groups=mesh['tm'=8,'col'=4] {'col'}, dimensions={0} | all-to-all | bytes 524288 | tf_op jit(solution)/shard_map/all_to_all | solution.py:137
  82.1 0.7 add.356
  (91 shorter events, 4.0 us)
Async XLA Ops:
  4.1 17.9 %copy-start = (bf16[2,512,128]{2,1,0:T(8,128)(2,1)S(1)}, bf16[2,512,128]{2,1,0:T(8,128)(2,1)}, u32[]{:S(2)}) copy-start(bf16[2,512,128]{2,1,0:T(8,128)(2,1)} %param.22) | copy-start | bytes 786436
  4.1 9.9 %collective-permute-start = (bf16[1104,128]{1,0:T(8,128)(2,1)}, bf16[1104,128]{1,0:T(8,128)(2,1)S(1)}, u32[]{:S(2)}, u32[]{:S(2)}) collective-permute-start(bf16[1104,128]{1,0:T(8,128)(2,1)} %get-tuple-element.274), channel_id=1, source_target_pairs={{0,3},{1,0},{2,1},{3,2},{4,7},{5,4},{6,5},{7,6},{8,11},{9,8},{10,9... | collective-permute-start | bytes 847880 | tf_op jit(solution)/shard_map/ppermute | solution.py:65
  6.5 14.0 %collective-permute-start.1 = (bf16[1104,128]{1,0:T(8,128)(2,1)S(1)}, bf16[1104,128]{1,0:T(8,128)(2,1)S(1)}, u32[]{:S(2)}, u32[]{:S(2)}) collective-permute-start(bf16[1104,128]{1,0:T(8,128)(2,1)S(1)} %get-tuple-element.275), channel_id=1, source_target_pairs={{0,2},{1,3},{2,0},{3,1},{4,6},{5,7},{6,4},{7,5},{8,10},{9,11},{10,... | collective-permute-start | bytes 847880 | tf_op jit(solution)/shard_map/ppermute | solution.py:65
  7.0 14.2 %collective-permute-start.2 = (bf16[1104,128]{1,0:T(8,128)(2,1)S(1)}, bf16[1104,128]{1,0:T(8,128)(2,1)S(1)}, u32[]{:S(2)}, u32[]{:S(2)}) collective-permute-start(bf16[1104,128]{1,0:T(8,128)(2,1)S(1)} %get-tuple-element.273), channel_id=1, source_target_pairs={{0,1},{1,2},{2,3},{3,0},{4,5},{5,6},{6,7},{7,4},{8,9},{9,10},{10,1... | collective-permute-start | bytes 847880 | tf_op jit(solution)/shard_map/ppermute | solution.py:65
  30.8 5.7 %collective-permute-start.3 = (f32[32,512]{1,0:T(8,128)S(1)}, f32[32,512]{1,0:T(8,128)S(1)}, u32[]{:S(2)}, u32[]{:S(2)}) collective-permute-start(f32[32,512]{1,0:T(8,128)S(1)} %get-tuple-element.305), channel_id=1, source_target_pairs={{0,4},{1,5},{2,6},{3,7},{28,24},{29,25},{30,26},{31,27}} | collective-permute-start | bytes 196616 | tf_op jit(solution)/shard_map/ppermute | solution.py:124
  37.2 0.7 collective-permute-start.4
  38.6 0.7 collective-permute-start.5
  40.0 0.7 collective-permute-start.6
  41.4 0.7 collective-permute-start.7
  42.8 0.7 collective-permute-start.8
  44.2 28.2 %collective-permute-start.9 = (f32[32,512]{1,0:T(8,128)S(1)}, f32[32,512]{1,0:T(8,128)S(1)}, u32[]{:S(2)}, u32[]{:S(2)}) collective-permute-start(f32[32,512]{1,0:T(8,128)S(1)} %get-tuple-element.311), channel_id=1, source_target_pairs={{24,28},{25,29},{26,30},{27,31},{4,0},{5,1},{6,2},{7,3}} | collective-permute-start | bytes 196616 | tf_op jit(solution)/shard_map/ppermute | solution.py:124
  82.1 0.7 copy-start.1

commit v9 on v8

--- a/solution.py
+++ b/solution.py
@@ -64,8 +64,14 @@
             ]
             chunk = lax.ppermute(chunk, ("tm", "col"), pairs)
         chunks.append(chunk)
-    by_shift = jnp.stack(chunks[::-1] + chunks[::-1])
-    packet = lax.dynamic_slice_in_dim(by_shift, col_groups - 1 - col_pos, col_groups, 0)
+    def from_source(j):
+        which = (col_pos - j) % col_groups
+        out = chunks[0]
+        for shift in range(1, col_groups):
+            out = jnp.where(which == shift, chunks[shift], out)
+        return out
+
+    packet = jnp.stack([from_source(j) for j in range(col_groups)])
     n_coupling = step_count * state_width
     n_seen = step_count * own_rows
     mask = jnp.broadcast_to(

time: 83.3 us -> 75.8 us (0.910)
  local copies, waits for them, and re-layouts: 9.04 us -> 3.32 us
  other arithmetic: 7.78 us -> 4.66 us
  starting transfers between devices: 11.6 us -> 13.7 us
    unnamed x12 -> x8, local copies, waits for them, and re-layouts: 4.45 us -> 0.02 us
    ppermute x3, starting transfers between devices: 3.2 us -> 4.71 us  [local(): chunk = lax.ppermute(chunk, ('tm', 'col'), pairs)]
    slice x2 -> x1, local copies, waits for them, and re-layouts: 2.11 us -> 0.81 us  [local(): packet[:, :n_coupling].reshape(col_groups, step_count, state_width, cols)]
    convert_element_type x1, other arithmetic: 0.86 us -> 0.01 us  [local(): driven = gain[None, None, :] * seen.astype(jnp.float32)]
    another operation x26 -> x28, other arithmetic: 1.86 us -> 1.71 us
  transfers between devices with their start and end apart: 10 -> 10, of which waited for: 4 -> 5; matrix products, arithmetic and copies ran while one was open for 4% -> 1% of each run, Pallas kernels for 0% -> 0%
where the time goes in v9:
time: 75.8 us; the launch traced here: 75.5 us
  waiting for transfers between devices  39.2 us (52%)
  starting transfers between devices  13.7 us (18%)
  blocking collectives  8.56 us (11%)
  other arithmetic  4.66 us (6%)
  matrix products  4.43 us (6%)
  local copies, waits for them, and re-layouts  3.32 us (4%)
  between operations  1.19 us (2%)
    ppermute x7, waiting for transfers between devices, local(): got = lax.ppermute(send, ('tm', 'col'), pairs)  28.8 us
    ppermute x3, waiting for transfers between devices, local(): chunk = lax.ppermute(chunk, ('tm', 'col'), pairs)  10.4 us
    ppermute x7, starting transfers between devices, local(): got = lax.ppermute(send, ('tm', 'col'), pairs)  8.96 us
    all_to_all x1, blocking collectives, local(): got = lax.all_to_all(mine, 'col', split_axis=0, concat_axis=0, tiled=True)  8.56 us
    ppermute x3, starting transfers between devices, local(): chunk = lax.ppermute(chunk, ('tm', 'col'), pairs)  4.71 us
    dot_general x17, matrix products, split_dot(): lax.dot_general(both, weights, (((1,), (contract,)), ((), ())), preferred...  4.43 us
    concatenate x1, other arithmetic, local(): chunk = jnp.concatenate([coupling_rows, seen_d, small_pieces], axis=0)  1.78 us
  transfers between devices with their start and end apart: 10, of which 5 were waited for; matrix products, arithmetic and copies ran while one was open for 1% of the time, Pallas kernels for 0%

profile of v9, /device:TPU:0, one launch (start us, length us, event | category | flops | bytes accessed | tf_op | source)
XLA Modules:
  0.0 75.5 jit_solution(12297815662431102166)
XLA Ops:
  0.7 0.7 reduce-precision_convert_fusion.31
  1.4 0.8 %copy.31 = bf16[4,2,32,128]{3,2,1,0:T(8,128)(2,1)S(1)} copy(bf16[4,2,32,128]{3,2,0,1:T(8,128)(2,1)} %bitcast.332) | data formatting | bytes 131072 | tf_op jit(solution)/shard_map/transpose | solution.py:52
  2.3 1.8 %fusion.273 = (bf16[1104,128]{1,0:T(8,128)(2,1)}, bf16[1104,128]{1,0:T(8,128)(2,1)S(1)}, bf16[1104,128]{1,0:T(8,128)(2,1)S(1)}) fusion(bf16[9,128]{1,0:T(8,128)(2,1)S(1)} %convert_element_type.57, bf16[64,128]{1,0:T(8,128)(2,1)S(1)} %get-tuple-element.300, bf16[1024,128]{1,0:T(8,128)(2,1)} %bitcast.308, bf16[64,128]{1,0:T(8,128)(2,1)S(1)} %get-tuple-element.302, ...), kind=kLoop, calls=%fused_computation.370 | loop fusion | flops 2260992 | bytes 1161472 | tf_op jit(solution)/shard_map/concatenate | solution.py:58
  4.1 0.5 collective-permute-start.2
  4.6 1.9 %collective-permute-start = (bf16[1104,128]{1,0:T(8,128)(2,1)S(1)}, bf16[1104,128]{1,0:T(8,128)(2,1)S(1)}, u32[]{:S(2)}, u32[]{:S(2)}) collective-permute-start(bf16[1104,128]{1,0:T(8,128)(2,1)S(1)} %get-tuple-element.278), channel_id=1, source_target_pairs={{0,3},{1,0},{2,1},{3,2},{4,7},{5,4},{6,5},{7,6},{8,11},{9,8},{10,9... | collective-permute-start | bytes 847880 | tf_op jit(solution)/shard_map/ppermute | solution.py:65
  6.5 2.3 %collective-permute-start.1 = (bf16[1104,128]{1,0:T(8,128)(2,1)S(1)}, bf16[1104,128]{1,0:T(8,128)(2,1)S(1)}, u32[]{:S(2)}, u32[]{:S(2)}) collective-permute-start(bf16[1104,128]{1,0:T(8,128)(2,1)S(1)} %get-tuple-element.279), channel_id=1, source_target_pairs={{0,2},{1,3},{2,0},{3,1},{4,6},{5,7},{6,4},{7,5},{8,10},{9,11},{10,... | collective-permute-start | bytes 847880 | tf_op jit(solution)/shard_map/ppermute | solution.py:65
  8.8 0.2 broadcast_in_dim.15
  9.0 0.6 mul.324
  9.6 2.0 %collective-permute-done.2 = bf16[1104,128]{1,0:T(8,128)(2,1)S(1)} collective-permute-done((bf16[1104,128]{1,0:T(8,128)(2,1)}, bf16[1104,128]{1,0:T(8,128)(2,1)S(1)}, u32[]{:S(2)}, u32[]{:S(2)}) %collective-permute-start.2) | collective-permute-done | bytes 282656 | tf_op jit(solution)/shard_map/ppermute | solution.py:65
  11.6 1.8 %collective-permute-done = bf16[1104,128]{1,0:T(8,128)(2,1)S(1)} collective-permute-done((bf16[1104,128]{1,0:T(8,128)(2,1)S(1)}, bf16[1104,128]{1,0:T(8,128)(2,1)S(1)}, u32[]{:S(2)}, u32[]{:S(2)}) %collective-permute-start) | collective-permute-done | bytes 282656 | tf_op jit(solution)/shard_map/ppermute | solution.py:65
  13.4 6.6 %collective-permute-done.1 = bf16[1104,128]{1,0:T(8,128)(2,1)S(1)} collective-permute-done((bf16[1104,128]{1,0:T(8,128)(2,1)S(1)}, bf16[1104,128]{1,0:T(8,128)(2,1)S(1)}, u32[]{:S(2)}, u32[]{:S(2)}) %collective-permute-start.1) | collective-permute-done | bytes 282656 | tf_op jit(solution)/shard_map/ppermute | solution.py:65
  20.1 0.2 select_bitcast_fusion.2
  20.3 0.2 select_bitcast_fusion.3
  20.7 0.8 %copy.34 = bf16[4,1024,128]{2,0,1:T(4,128)(2,1)S(1)} copy(bf16[4,1024,128]{2,1,0:T(8,128)(2,1)S(1)} %pad_maximum_fusion) | data formatting | bytes 2097152 | tf_op jit(solution)/shard_map/slice | solution.py:82
  21.5 0.4 reshape.169
  22.3 0.6 conditional.7
  22.3 0.2 fusion.21
  22.9 4.3 %collective-permute-start.3 = (f32[32,512]{1,0:T(8,128)S(1)}, f32[32,512]{1,0:T(8,128)S(1)}, u32[]{:S(2)}, u32[]{:S(2)}) collective-permute-start(f32[32,512]{1,0:T(8,128)S(1)} %get-tuple-element.309), channel_id=1, source_target_pairs={{0,4},{1,5},{2,6},{3,7},{28,24},{29,25},{30,26},{31,27}} | collective-permute-start | bytes 196616 | tf_op jit(solution)/shard_map/ppermute | solution.py:130
  27.2 1.9 %collective-permute-done.3 = f32[32,512]{1,0:T(8,128)S(1)} collective-permute-done((f32[32,512]{1,0:T(8,128)S(1)}, f32[32,512]{1,0:T(8,128)S(1)}, u32[]{:S(2)}, u32[]{:S(2)}) %collective-permute-start.3) | collective-permute-done | bytes 65568 | tf_op jit(solution)/shard_map/ppermute | solution.py:130
  29.1 0.7 conditional.8
  29.2 0.3 fusion.37
  29.5 0.3 fusion.35
  29.8 0.7 collective-permute-start.4
  30.5 0.7 conditional.9
  30.6 0.3 fusion.76
  30.9 0.3 fusion.74
  31.2 0.7 collective-permute-start.5
  31.9 0.7 conditional.10
  32.0 0.3 fusion.115
  32.3 0.3 fusion.113
  32.6 0.7 collective-permute-start.6
  33.3 0.7 conditional.11
  33.4 0.3 fusion.154
  33.7 0.3 fusion.152
  34.0 0.7 collective-permute-start.7
  34.8 0.7 conditional.12
  34.8 0.3 fusion.193
  35.1 0.3 fusion.191
  35.4 0.7 collective-permute-start.8
  36.2 0.7 conditional.13
  36.2 0.3 fusion.232
  36.5 0.3 fusion.230
  36.9 1.3 %collective-permute-start.9 = (f32[32,512]{1,0:T(8,128)S(1)}, f32[32,512]{1,0:T(8,128)S(1)}, u32[]{:S(2)}, u32[]{:S(2)}) collective-permute-start(f32[32,512]{1,0:T(8,128)S(1)} %get-tuple-element.315), channel_id=1, source_target_pairs={{24,28},{25,29},{26,30},{27,31},{4,0},{5,1},{6,2},{7,3}} | collective-permute-start | bytes 196616 | tf_op jit(solution)/shard_map/ppermute | solution.py:130
  38.2 26.9 %collective-permute-done.9 = f32[32,512]{1,0:T(8,128)S(1)} collective-permute-done((f32[32,512]{1,0:T(8,128)S(1)}, f32[32,512]{1,0:T(8,128)S(1)}, u32[]{:S(2)}, u32[]{:S(2)}) %collective-permute-start.9) | collective-permute-done | bytes 65568 | tf_op jit(solution)/shard_map/ppermute | solution.py:130
  65.5 0.2 fusion.272
  65.7 0.3 fusion.271
  66.2 8.6 %all_to_all.5 = f32[4,2,2,32,128]{4,3,2,1,0:T(8,128)S(1)} all-to-all(f32[4,2,2,32,128]{4,3,2,1,0:T(8,128)S(1)} %maximum_bitcast_fusion), channel_id=1, replica_groups=mesh['tm'=8,'col'=4] {'col'}, dimensions={0} | all-to-all | bytes 524288 | tf_op jit(solution)/shard_map/all_to_all | solution.py:143
  74.8 0.7 add.367
  (87 shorter events, 1.8 us)
Async XLA Ops:
  0.6 8.2 %copy-start.2 = (s32[8,8]{1,0:T(8,128)S(1)}, s32[8,8]{1,0:T(8,128)}, u32[]{:S(2)}) copy-start(s32[8,8]{1,0:T(8,128)} %param.23) | copy-start | bytes 772
  4.1 7.5 %collective-permute-start.2 = (bf16[1104,128]{1,0:T(8,128)(2,1)}, bf16[1104,128]{1,0:T(8,128)(2,1)S(1)}, u32[]{:S(2)}, u32[]{:S(2)}) collective-permute-start(bf16[1104,128]{1,0:T(8,128)(2,1)} %get-tuple-element.277), channel_id=1, source_target_pairs={{0,1},{1,2},{2,3},{3,0},{4,5},{5,6},{6,7},{7,4},{8,9},{9,10},{10,1... | collective-permute-start | bytes 847880 | tf_op jit(solution)/shard_map/ppermute | solution.py:65
  4.6 8.9 %collective-permute-start = (bf16[1104,128]{1,0:T(8,128)(2,1)S(1)}, bf16[1104,128]{1,0:T(8,128)(2,1)S(1)}, u32[]{:S(2)}, u32[]{:S(2)}) collective-permute-start(bf16[1104,128]{1,0:T(8,128)(2,1)S(1)} %get-tuple-element.278), channel_id=1, source_target_pairs={{0,3},{1,0},{2,1},{3,2},{4,7},{5,4},{6,5},{7,6},{8,11},{9,8},{10,9... | collective-permute-start | bytes 847880 | tf_op jit(solution)/shard_map/ppermute | solution.py:65
  6.5 13.6 %collective-permute-start.1 = (bf16[1104,128]{1,0:T(8,128)(2,1)S(1)}, bf16[1104,128]{1,0:T(8,128)(2,1)S(1)}, u32[]{:S(2)}, u32[]{:S(2)}) collective-permute-start(bf16[1104,128]{1,0:T(8,128)(2,1)S(1)} %get-tuple-element.279), channel_id=1, source_target_pairs={{0,2},{1,3},{2,0},{3,1},{4,6},{5,7},{6,4},{7,5},{8,10},{9,11},{10,... | collective-permute-start | bytes 847880 | tf_op jit(solution)/shard_map/ppermute | solution.py:65
  9.0 11.0 %copy-start = (bf16[2,512,128]{2,1,0:T(8,128)(2,1)S(1)}, bf16[2,512,128]{2,1,0:T(8,128)(2,1)}, u32[]{:S(2)}) copy-start(bf16[2,512,128]{2,1,0:T(8,128)(2,1)} %param.22) | copy-start | bytes 786436
  22.9 6.2 %collective-permute-start.3 = (f32[32,512]{1,0:T(8,128)S(1)}, f32[32,512]{1,0:T(8,128)S(1)}, u32[]{:S(2)}, u32[]{:S(2)}) collective-permute-start(f32[32,512]{1,0:T(8,128)S(1)} %get-tuple-element.309), channel_id=1, source_target_pairs={{0,4},{1,5},{2,6},{3,7},{28,24},{29,25},{30,26},{31,27}} | collective-permute-start | bytes 196616 | tf_op jit(solution)/shard_map/ppermute | solution.py:130
  29.8 0.7 collective-permute-start.4
  31.2 0.7 collective-permute-start.5
  32.6 0.7 collective-permute-start.6
  34.0 0.7 collective-permute-start.7
  35.4 0.7 collective-permute-start.8
  36.9 28.2 %collective-permute-start.9 = (f32[32,512]{1,0:T(8,128)S(1)}, f32[32,512]{1,0:T(8,128)S(1)}, u32[]{:S(2)}, u32[]{:S(2)}) collective-permute-start(f32[32,512]{1,0:T(8,128)S(1)} %get-tuple-element.315), channel_id=1, source_target_pairs={{24,28},{25,29},{26,30},{27,31},{4,0},{5,1},{6,2},{7,3}} | collective-permute-start | bytes 196616 | tf_op jit(solution)/shard_map/ppermute | solution.py:130
  74.8 0.7 copy-start.1

commit v10 on v9

--- a/solution.py
+++ b/solution.py
@@ -138,12 +138,31 @@
         x_in, e_in = lax.fori_loop(0, time_groups - 1, stage, (x_in, e_in))
     xs = forward(x_in)
     es = backward(e_in)
-    mine = jnp.stack([jnp.stack(xs), jnp.stack([es[step_count - 2 - k] if k < step_count - 1 else e_in for k in range(step_count)])])
-    mine = mine.reshape(2, step_count, own_rows, col_groups, cols).transpose(3, 0, 1, 2, 4)
-    got = lax.all_to_all(mine, "col", split_axis=0, concat_axis=0, tiled=True)
-    got = got.transpose(1, 2, 0, 3, 4).reshape(2, step_count, rows, cols)
-    filtered = got[0]
-    return filtered, filtered + got[1]
+    filtered = jnp.stack(xs)
+    correction = jnp.stack([es[step_count - 2 - k] for k in range(step_count - 1)] + [e_in])
+    mine = jnp.stack([filtered, filtered + correction])
+    parts = [mine[:, :, :, j * cols : (j + 1) * cols] for j in range(col_groups)]
+
+    def pick(options, which):
+        out = options[0]
+        for j in range(1, col_groups):
+            out = jnp.where(which == j, options[j], out)
+        return out
+
+    arrived = []
+    for shift in range(col_groups):
+        piece = pick(parts, (col_pos + shift) % col_groups)
+        if shift:
+            pairs = [
+                (t * col_groups + c, t * col_groups + (c + shift) % col_groups)
+                for t in range(time_groups)
+                for c in range(col_groups)
+            ]
+            piece = lax.ppermute(piece, ("tm", "col"), pairs)
+        arrived.append(piece)
+    got = jnp.stack([pick(arrived, (col_pos - j) % col_groups) for j in range(col_groups)], axis=2)
+    got = got.reshape(2, step_count, rows, cols)
+    return got[0], got[1]
 
 
 def solution(mesh):

time: 75.8 us -> 73 us (0.963)
  blocking collectives: 8.56 us -> 0 us
  starting transfers between devices: 13.7 us -> 16.7 us
  waiting for transfers between devices: 39.2 us -> 41.1 us
  local copies, waits for them, and re-layouts: 3.32 us -> 4.5 us
    all_to_all x1 -> x0, blocking collectives: 8.56 us -> none  [local(): got = lax.all_to_all(mine, 'col', split_axis=0, concat_axis=0, tiled=True)]
    ppermute x0 -> x3, starting transfers between devices: none -> 3.06 us  [local(): piece = lax.ppermute(piece, ('tm', 'col'), pairs)]
    ppermute x0 -> x3, waiting for transfers between devices: none -> 1.9 us  [local(): piece = lax.ppermute(piece, ('tm', 'col'), pairs)]
    slice x1 -> x3, local copies, waits for them, and re-layouts: 0.02 us -> 1.35 us  [local(): return (got[0], got[1])]
  transfers between devices with their start and end apart: 10 -> 13, of which waited for: 5 -> 8; matrix products, arithmetic and copies ran while one was open for 1% -> 1% of each run, Pallas kernels for 0% -> 0%
where the time goes in v10:
time: 73 us; the launch traced here: 72.5 us
  waiting for transfers between devices  41.1 us (56%)
  starting transfers between devices  16.7 us (23%)
  local copies, waits for them, and re-layouts  4.5 us (6%)
  matrix products  4.43 us (6%)
  other arithmetic  4.11 us (6%)
  between operations  1.21 us (2%)
    ppermute x7, waiting for transfers between devices, local(): got = lax.ppermute(send, ('tm', 'col'), pairs)  28.8 us
    ppermute x3, waiting for transfers between devices, local(): chunk = lax.ppermute(chunk, ('tm', 'col'), pairs)  10.4 us
    ppermute x7, starting transfers between devices, local(): got = lax.ppermute(send, ('tm', 'col'), pairs)  8.96 us
    ppermute x3, starting transfers between devices, local(): chunk = lax.ppermute(chunk, ('tm', 'col'), pairs)  4.71 us
    dot_general x17, matrix products, split_dot(): lax.dot_general(both, weights, (((1,), (contract,)), ((), ())), preferred...  4.43 us
    ppermute x3, starting transfers between devices, local(): piece = lax.ppermute(piece, ('tm', 'col'), pairs)  3.06 us
    ppermute x3, waiting for transfers between devices, local(): piece = lax.ppermute(piece, ('tm', 'col'), pairs)  1.9 us
    concatenate x1, other arithmetic, local(): chunk = jnp.concatenate([coupling_rows, seen_d, small_pieces], axis=0)  1.76 us
  transfers between devices with their start and end apart: 13, of which 8 were waited for; matrix products, arithmetic and copies ran while one was open for 1% of the time, Pallas kernels for 0%

profile of v10, /device:TPU:0, one launch (start us, length us, event | category | flops | bytes accessed | tf_op | source)
XLA Modules:
  0.0 72.5 jit_solution(14665489372466490781)
XLA Ops:
  0.7 0.7 reduce-precision_convert_fusion.31
  1.4 0.8 %copy.15 = bf16[4,2,32,128]{3,2,1,0:T(8,128)(2,1)S(1)} copy(bf16[4,2,32,128]{3,2,0,1:T(8,128)(2,1)} %bitcast.342) | data formatting | bytes 131072 | tf_op jit(solution)/shard_map/transpose | solution.py:52
  2.3 1.8 %fusion.273 = (bf16[1104,128]{1,0:T(8,128)(2,1)}, bf16[1104,128]{1,0:T(8,128)(2,1)S(1)}, bf16[1104,128]{1,0:T(8,128)(2,1)S(1)}) fusion(bf16[9,128]{1,0:T(8,128)(2,1)S(1)} %convert_element_type.57, bf16[64,128]{1,0:T(8,128)(2,1)S(1)} %get-tuple-element.309, bf16[1024,128]{1,0:T(8,128)(2,1)} %bitcast.316, bf16[64,128]{1,0:T(8,128)(2,1)S(1)} %get-tuple-element.311, ...), kind=kLoop, calls=%fused_computation.376 | loop fusion | flops 2260992 | bytes 1161472 | tf_op jit(solution)/shard_map/concatenate | solution.py:58
  4.1 0.5 collective-permute-start.2
  4.5 1.9 %collective-permute-start = (bf16[1104,128]{1,0:T(8,128)(2,1)S(1)}, bf16[1104,128]{1,0:T(8,128)(2,1)S(1)}, u32[]{:S(2)}, u32[]{:S(2)}) collective-permute-start(bf16[1104,128]{1,0:T(8,128)(2,1)S(1)} %get-tuple-element.285), channel_id=1, source_target_pairs={{0,3},{1,0},{2,1},{3,2},{4,7},{5,4},{6,5},{7,6},{8,11},{9,8},{10,9... | collective-permute-start | bytes 847880 | tf_op jit(solution)/shard_map/ppermute | solution.py:65
  6.5 2.3 %collective-permute-start.1 = (bf16[1104,128]{1,0:T(8,128)(2,1)S(1)}, bf16[1104,128]{1,0:T(8,128)(2,1)S(1)}, u32[]{:S(2)}, u32[]{:S(2)}) collective-permute-start(bf16[1104,128]{1,0:T(8,128)(2,1)S(1)} %get-tuple-element.286), channel_id=1, source_target_pairs={{0,2},{1,3},{2,0},{3,1},{4,6},{5,7},{6,4},{7,5},{8,10},{9,11},{10,... | collective-permute-start | bytes 847880 | tf_op jit(solution)/shard_map/ppermute | solution.py:65
  9.0 0.6 mul.324
  9.6 2.0 %collective-permute-done.2 = bf16[1104,128]{1,0:T(8,128)(2,1)S(1)} collective-permute-done((bf16[1104,128]{1,0:T(8,128)(2,1)}, bf16[1104,128]{1,0:T(8,128)(2,1)S(1)}, u32[]{:S(2)}, u32[]{:S(2)}) %collective-permute-start.2) | collective-permute-done | bytes 282656 | tf_op jit(solution)/shard_map/ppermute | solution.py:65
  11.6 1.8 %collective-permute-done = bf16[1104,128]{1,0:T(8,128)(2,1)S(1)} collective-permute-done((bf16[1104,128]{1,0:T(8,128)(2,1)S(1)}, bf16[1104,128]{1,0:T(8,128)(2,1)S(1)}, u32[]{:S(2)}, u32[]{:S(2)}) %collective-permute-start) | collective-permute-done | bytes 282656 | tf_op jit(solution)/shard_map/ppermute | solution.py:65
  13.4 6.6 %collective-permute-done.1 = bf16[1104,128]{1,0:T(8,128)(2,1)S(1)} collective-permute-done((bf16[1104,128]{1,0:T(8,128)(2,1)S(1)}, bf16[1104,128]{1,0:T(8,128)(2,1)S(1)}, u32[]{:S(2)}, u32[]{:S(2)}) %collective-permute-start.1) | collective-permute-done | bytes 282656 | tf_op jit(solution)/shard_map/ppermute | solution.py:65
  20.7 0.8 %copy.18 = bf16[4,1024,128]{2,0,1:T(4,128)(2,1)S(1)} copy(bf16[4,1024,128]{2,1,0:T(8,128)(2,1)S(1)} %pad_maximum_fusion) | data formatting | bytes 2097152 | tf_op jit(solution)/shard_map/slice | solution.py:82
  21.5 0.4 reshape.215
  22.3 0.6 conditional.7
  22.8 4.3 %collective-permute-start.3 = (f32[32,512]{1,0:T(8,128)S(1)}, f32[32,512]{1,0:T(8,128)S(1)}, u32[]{:S(2)}, u32[]{:S(2)}) collective-permute-start(f32[32,512]{1,0:T(8,128)S(1)} %get-tuple-element.318), channel_id=1, source_target_pairs={{0,4},{1,5},{2,6},{3,7},{28,24},{29,25},{30,26},{31,27}} | collective-permute-start | bytes 196616 | tf_op jit(solution)/shard_map/ppermute | solution.py:130
  27.2 1.9 %collective-permute-done.3 = f32[32,512]{1,0:T(8,128)S(1)} collective-permute-done((f32[32,512]{1,0:T(8,128)S(1)}, f32[32,512]{1,0:T(8,128)S(1)}, u32[]{:S(2)}, u32[]{:S(2)}) %collective-permute-start.3) | collective-permute-done | bytes 65568 | tf_op jit(solution)/shard_map/ppermute | solution.py:130
  29.1 0.7 conditional.8
  29.1 0.3 fusion.37
  29.5 0.3 fusion.35
  29.8 0.7 collective-permute-start.4
  30.5 0.7 conditional.9
  30.6 0.3 fusion.76
  30.9 0.3 fusion.74
  31.2 0.7 collective-permute-start.5
  31.9 0.7 conditional.10
  32.0 0.3 fusion.115
  32.3 0.3 fusion.113
  32.6 0.7 collective-permute-start.6
  33.3 0.7 conditional.11
  33.4 0.3 fusion.154
  33.7 0.3 fusion.152
  34.0 0.7 collective-permute-start.7
  34.7 0.7 conditional.12
  34.8 0.3 fusion.193
  35.1 0.3 fusion.191
  35.4 0.7 collective-permute-start.8
  36.1 0.7 conditional.13
  36.2 0.3 fusion.232
  36.5 0.3 fusion.230
  36.8 1.3 %collective-permute-start.9 = (f32[32,512]{1,0:T(8,128)S(1)}, f32[32,512]{1,0:T(8,128)S(1)}, u32[]{:S(2)}, u32[]{:S(2)}) collective-permute-start(f32[32,512]{1,0:T(8,128)S(1)} %get-tuple-element.324), channel_id=1, source_target_pairs={{24,28},{25,29},{26,30},{27,31},{4,0},{5,1},{6,2},{7,3}} | collective-permute-start | bytes 196616 | tf_op jit(solution)/shard_map/ppermute | solution.py:130
  38.2 26.9 %collective-permute-done.9 = f32[32,512]{1,0:T(8,128)S(1)} collective-permute-done((f32[32,512]{1,0:T(8,128)S(1)}, f32[32,512]{1,0:T(8,128)S(1)}, u32[]{:S(2)}, u32[]{:S(2)}) %collective-permute-start.9) | collective-permute-done | bytes 65568 | tf_op jit(solution)/shard_map/ppermute | solution.py:130
  65.6 0.3 fusion.271
  66.1 1.6 %collective-permute-start.11 = (f32[2,2,32,128]{3,2,1,0:T(8,128)S(1)}, f32[2,2,32,128]{3,2,1,0:T(8,128)S(1)}, u32[]{:S(2)}, u32[]{:S(2)}) collective-permute-start(f32[2,2,32,128]{3,2,1,0:T(8,128)S(1)} %get-tuple-element.292), channel_id=1, source_target_pairs={{0,2},{1,3},{2,0},{3,1},{4,6},{5,7},{6,4},{7,5},{8,10},{9,11},{10,... | collective-permute-start | bytes 196616 | tf_op jit(solution)/shard_map/ppermute | solution.py:161
  67.7 1.4 %collective-permute-start.10 = (f32[2,2,32,128]{3,2,1,0:T(8,128)S(1)}, f32[2,2,32,128]{3,2,1,0:T(8,128)S(1)}, u32[]{:S(2)}, u32[]{:S(2)}) collective-permute-start(f32[2,2,32,128]{3,2,1,0:T(8,128)S(1)} %get-tuple-element.293), channel_id=1, source_target_pairs={{0,3},{1,0},{2,1},{3,2},{4,7},{5,4},{6,5},{7,6},{8,11},{9,8},{10,9... | collective-permute-start | bytes 196616 | tf_op jit(solution)/shard_map/ppermute | solution.py:161
  69.1 0.7 collective-permute-done.12
  69.8 0.8 %collective-permute-done.11 = f32[2,2,32,128]{3,2,1,0:T(8,128)S(1)} collective-permute-done((f32[2,2,32,128]{3,2,1,0:T(8,128)S(1)}, f32[2,2,32,128]{3,2,1,0:T(8,128)S(1)}, u32[]{:S(2)}, u32[]{:S(2)}) %collective-permute-start.11) | collective-permute-done | bytes 65568 | tf_op jit(solution)/shard_map/ppermute | solution.py:161
  70.6 0.5 collective-permute-done.10
  71.2 0.7 copy.20
  71.8 0.7 copy.19
  (90 shorter events, 3.0 us)
Async XLA Ops:
  0.6 8.1 %copy-start.1 = (s32[8,8]{1,0:T(8,128)S(1)}, s32[8,8]{1,0:T(8,128)}, u32[]{:S(2)}) copy-start(s32[8,8]{1,0:T(8,128)} %param.23) | copy-start | bytes 772
  4.1 7.5 %collective-permute-start.2 = (bf16[1104,128]{1,0:T(8,128)(2,1)}, bf16[1104,128]{1,0:T(8,128)(2,1)S(1)}, u32[]{:S(2)}, u32[]{:S(2)}) collective-permute-start(bf16[1104,128]{1,0:T(8,128)(2,1)} %get-tuple-element.284), channel_id=1, source_target_pairs={{0,1},{1,2},{2,3},{3,0},{4,5},{5,6},{6,7},{7,4},{8,9},{9,10},{10,1... | collective-permute-start | bytes 847880 | tf_op jit(solution)/shard_map/ppermute | solution.py:65
  4.5 8.9 %collective-permute-start = (bf16[1104,128]{1,0:T(8,128)(2,1)S(1)}, bf16[1104,128]{1,0:T(8,128)(2,1)S(1)}, u32[]{:S(2)}, u32[]{:S(2)}) collective-permute-start(bf16[1104,128]{1,0:T(8,128)(2,1)S(1)} %get-tuple-element.285), channel_id=1, source_target_pairs={{0,3},{1,0},{2,1},{3,2},{4,7},{5,4},{6,5},{7,6},{8,11},{9,8},{10,9... | collective-permute-start | bytes 847880 | tf_op jit(solution)/shard_map/ppermute | solution.py:65
  6.5 13.6 %collective-permute-start.1 = (bf16[1104,128]{1,0:T(8,128)(2,1)S(1)}, bf16[1104,128]{1,0:T(8,128)(2,1)S(1)}, u32[]{:S(2)}, u32[]{:S(2)}) collective-permute-start(bf16[1104,128]{1,0:T(8,128)(2,1)S(1)} %get-tuple-element.286), channel_id=1, source_target_pairs={{0,2},{1,3},{2,0},{3,1},{4,6},{5,7},{6,4},{7,5},{8,10},{9,11},{10,... | collective-permute-start | bytes 847880 | tf_op jit(solution)/shard_map/ppermute | solution.py:65
  9.0 11.0 %copy-start = (bf16[2,512,128]{2,1,0:T(8,128)(2,1)S(1)}, bf16[2,512,128]{2,1,0:T(8,128)(2,1)}, u32[]{:S(2)}) copy-start(bf16[2,512,128]{2,1,0:T(8,128)(2,1)} %param.22) | copy-start | bytes 786436
  22.8 6.2 %collective-permute-start.3 = (f32[32,512]{1,0:T(8,128)S(1)}, f32[32,512]{1,0:T(8,128)S(1)}, u32[]{:S(2)}, u32[]{:S(2)}) collective-permute-start(f32[32,512]{1,0:T(8,128)S(1)} %get-tuple-element.318), channel_id=1, source_target_pairs={{0,4},{1,5},{2,6},{3,7},{28,24},{29,25},{30,26},{31,27}} | collective-permute-start | bytes 196616 | tf_op jit(solution)/shard_map/ppermute | solution.py:130
  29.8 0.7 collective-permute-start.4
  31.2 0.7 collective-permute-start.5
  32.6 0.7 collective-permute-start.6
  34.0 0.7 collective-permute-start.7
  35.4 0.7 collective-permute-start.8
  36.8 28.2 %collective-permute-start.9 = (f32[32,512]{1,0:T(8,128)S(1)}, f32[32,512]{1,0:T(8,128)S(1)}, u32[]{:S(2)}, u32[]{:S(2)}) collective-permute-start(f32[32,512]{1,0:T(8,128)S(1)} %get-tuple-element.324), channel_id=1, source_target_pairs={{24,28},{25,29},{26,30},{27,31},{4,0},{5,1},{6,2},{7,3}} | collective-permute-start | bytes 196616 | tf_op jit(solution)/shard_map/ppermute | solution.py:130
  66.0 3.8 %collective-permute-start.12 = (f32[2,2,32,128]{3,2,1,0:T(8,128)S(1)}, f32[2,2,32,128]{3,2,1,0:T(8,128)S(1)}, u32[]{:S(2)}, u32[]{:S(2)}) collective-permute-start(f32[2,2,32,128]{3,2,1,0:T(8,128)S(1)} %get-tuple-element.215), channel_id=1, source_target_pairs={{0,1},{1,2},{2,3},{3,0},{4,5},{5,6},{6,7},{7,4},{8,9},{9,10},{10,1... | collective-permute-start | bytes 196616 | tf_op jit(solution)/shard_map/ppermute | solution.py:161
  66.1 4.5 %collective-permute-start.11 = (f32[2,2,32,128]{3,2,1,0:T(8,128)S(1)}, f32[2,2,32,128]{3,2,1,0:T(8,128)S(1)}, u32[]{:S(2)}, u32[]{:S(2)}) collective-permute-start(f32[2,2,32,128]{3,2,1,0:T(8,128)S(1)} %get-tuple-element.292), channel_id=1, source_target_pairs={{0,2},{1,3},{2,0},{3,1},{4,6},{5,7},{6,4},{7,5},{8,10},{9,11},{10,... | collective-permute-start | bytes 196616 | tf_op jit(solution)/shard_map/ppermute | solution.py:161
  67.7 3.4 %collective-permute-start.10 = (f32[2,2,32,128]{3,2,1,0:T(8,128)S(1)}, f32[2,2,32,128]{3,2,1,0:T(8,128)S(1)}, u32[]{:S(2)}, u32[]{:S(2)}) collective-permute-start(f32[2,2,32,128]{3,2,1,0:T(8,128)S(1)} %get-tuple-element.293), channel_id=1, source_target_pairs={{0,3},{1,0},{2,1},{3,2},{4,7},{5,4},{6,5},{7,6},{8,11},{9,8},{10,9... | collective-permute-start | bytes 196616 | tf_op jit(solution)/shard_map/ppermute | solution.py:161

commit v11 on v10

--- a/solution.py
+++ b/solution.py
@@ -160,9 +160,13 @@
             ]
             piece = lax.ppermute(piece, ("tm", "col"), pairs)
         arrived.append(piece)
-    got = jnp.stack([pick(arrived, (col_pos - j) % col_groups) for j in range(col_groups)], axis=2)
-    got = got.reshape(2, step_count, rows, cols)
-    return got[0], got[1]
+    outputs = []
+    for kind in range(2):
+        mine_kind = [piece[kind] for piece in arrived]
+        outputs.append(
+            jnp.concatenate([pick(mine_kind, (col_pos - j) % col_groups) for j in range(col_groups)], axis=1)
+        )
+    return outputs[0], outputs[1]
 
 
 def solution(mesh):

time: 73 us -> 73 us (level)
  waiting for transfers between devices: 41.1 us -> 43.2 us
  local copies, waits for them, and re-layouts: 4.5 us -> 3.15 us
  starting transfers between devices: 16.7 us -> 15.5 us
    ppermute x3, waiting for transfers between devices: 1.9 us -> 4.02 us  [local(): piece = lax.ppermute(piece, ('tm', 'col'), pairs)]
    slice x3 -> x0, local copies, waits for them, and re-layouts: 1.35 us -> none  [local(): return (got[0], got[1])]
    ppermute x3, starting transfers between devices: 3.06 us -> 1.83 us  [local(): piece = lax.ppermute(piece, ('tm', 'col'), pairs)]
where the time goes in v11:
time: 73 us; the launch traced here: 72.7 us
  waiting for transfers between devices  43.2 us (59%)
  starting transfers between devices  15.5 us (21%)
  other arithmetic  4.82 us (7%)
  matrix products  4.43 us (6%)
  local copies, waits for them, and re-layouts  3.15 us (4%)
  between operations  1.2 us (2%)
    ppermute x7, waiting for transfers between devices, local(): got = lax.ppermute(send, ('tm', 'col'), pairs)  28.8 us
    ppermute x3, waiting for transfers between devices, local(): chunk = lax.ppermute(chunk, ('tm', 'col'), pairs)  10.4 us
    ppermute x7, starting transfers between devices, local(): got = lax.ppermute(send, ('tm', 'col'), pairs)  8.96 us
    ppermute x3, starting transfers between devices, local(): chunk = lax.ppermute(chunk, ('tm', 'col'), pairs)  4.71 us
    dot_general x17, matrix products, split_dot(): lax.dot_general(both, weights, (((1,), (contract,)), ((), ())), preferred...  4.43 us
    ppermute x3, waiting for transfers between devices, local(): piece = lax.ppermute(piece, ('tm', 'col'), pairs)  4.02 us
    ppermute x3, starting transfers between devices, local(): piece = lax.ppermute(piece, ('tm', 'col'), pairs)  1.83 us
    concatenate x1, other arithmetic, local(): chunk = jnp.concatenate([coupling_rows, seen_d, small_pieces], axis=0)  1.76 us
  transfers between devices with their start and end apart: 13, of which 8 were waited for; matrix products, arithmetic and copies ran while one was open for 1% of the time, Pallas kernels for 0%

profile of v11, /device:TPU:0, one launch (start us, length us, event | category | flops | bytes accessed | tf_op | source)
XLA Modules:
  0.0 72.7 jit_solution(2892230096478947753)
XLA Ops:
  0.7 0.7 reduce-precision_convert_fusion.31
  1.4 0.8 %copy.13 = bf16[4,2,32,128]{3,2,1,0:T(8,128)(2,1)S(1)} copy(bf16[4,2,32,128]{3,2,0,1:T(8,128)(2,1)} %bitcast.346) | data formatting | bytes 131072 | tf_op jit(solution)/shard_map/transpose | solution.py:52
  2.3 1.8 %fusion.273 = (bf16[1104,128]{1,0:T(8,128)(2,1)}, bf16[1104,128]{1,0:T(8,128)(2,1)S(1)}, bf16[1104,128]{1,0:T(8,128)(2,1)S(1)}) fusion(bf16[9,128]{1,0:T(8,128)(2,1)S(1)} %convert_element_type.57, bf16[64,128]{1,0:T(8,128)(2,1)S(1)} %get-tuple-element.311, bf16[1024,128]{1,0:T(8,128)(2,1)} %bitcast.322, bf16[64,128]{1,0:T(8,128)(2,1)S(1)} %get-tuple-element.313, ...), kind=kLoop, calls=%fused_computation.376 | loop fusion | flops 2260992 | bytes 1161472 | tf_op jit(solution)/shard_map/concatenate | solution.py:58
  4.1 0.5 collective-permute-start.2
  4.5 1.9 %collective-permute-start = (bf16[1104,128]{1,0:T(8,128)(2,1)S(1)}, bf16[1104,128]{1,0:T(8,128)(2,1)S(1)}, u32[]{:S(2)}, u32[]{:S(2)}) collective-permute-start(bf16[1104,128]{1,0:T(8,128)(2,1)S(1)} %get-tuple-element.283), channel_id=1, source_target_pairs={{0,3},{1,0},{2,1},{3,2},{4,7},{5,4},{6,5},{7,6},{8,11},{9,8},{10,9... | collective-permute-start | bytes 847880 | tf_op jit(solution)/shard_map/ppermute | solution.py:65
  6.5 2.3 %collective-permute-start.1 = (bf16[1104,128]{1,0:T(8,128)(2,1)S(1)}, bf16[1104,128]{1,0:T(8,128)(2,1)S(1)}, u32[]{:S(2)}, u32[]{:S(2)}) collective-permute-start(bf16[1104,128]{1,0:T(8,128)(2,1)S(1)} %get-tuple-element.284), channel_id=1, source_target_pairs={{0,2},{1,3},{2,0},{3,1},{4,6},{5,7},{6,4},{7,5},{8,10},{9,11},{10,... | collective-permute-start | bytes 847880 | tf_op jit(solution)/shard_map/ppermute | solution.py:65
  9.0 0.6 mul.324
  9.6 2.0 %collective-permute-done.2 = bf16[1104,128]{1,0:T(8,128)(2,1)S(1)} collective-permute-done((bf16[1104,128]{1,0:T(8,128)(2,1)}, bf16[1104,128]{1,0:T(8,128)(2,1)S(1)}, u32[]{:S(2)}, u32[]{:S(2)}) %collective-permute-start.2) | collective-permute-done | bytes 282656 | tf_op jit(solution)/shard_map/ppermute | solution.py:65
  11.6 1.8 %collective-permute-done = bf16[1104,128]{1,0:T(8,128)(2,1)S(1)} collective-permute-done((bf16[1104,128]{1,0:T(8,128)(2,1)S(1)}, bf16[1104,128]{1,0:T(8,128)(2,1)S(1)}, u32[]{:S(2)}, u32[]{:S(2)}) %collective-permute-start) | collective-permute-done | bytes 282656 | tf_op jit(solution)/shard_map/ppermute | solution.py:65
  13.4 6.6 %collective-permute-done.1 = bf16[1104,128]{1,0:T(8,128)(2,1)S(1)} collective-permute-done((bf16[1104,128]{1,0:T(8,128)(2,1)S(1)}, bf16[1104,128]{1,0:T(8,128)(2,1)S(1)}, u32[]{:S(2)}, u32[]{:S(2)}) %collective-permute-start.1) | collective-permute-done | bytes 282656 | tf_op jit(solution)/shard_map/ppermute | solution.py:65
  20.0 0.2 select_bitcast_fusion.2
  20.3 0.2 select_bitcast_fusion.3
  20.7 0.8 %copy.16 = bf16[4,1024,128]{2,0,1:T(4,128)(2,1)S(1)} copy(bf16[4,1024,128]{2,1,0:T(8,128)(2,1)S(1)} %pad_maximum_fusion) | data formatting | bytes 2097152 | tf_op jit(solution)/shard_map/slice | solution.py:82
  21.5 0.4 reshape.258
  22.3 0.6 conditional.7
  22.3 0.2 fusion.21
  22.8 4.3 %collective-permute-start.3 = (f32[32,512]{1,0:T(8,128)S(1)}, f32[32,512]{1,0:T(8,128)S(1)}, u32[]{:S(2)}, u32[]{:S(2)}) collective-permute-start(f32[32,512]{1,0:T(8,128)S(1)} %get-tuple-element.322), channel_id=1, source_target_pairs={{0,4},{1,5},{2,6},{3,7},{28,24},{29,25},{30,26},{31,27}} | collective-permute-start | bytes 196616 | tf_op jit(solution)/shard_map/ppermute | solution.py:130
  27.2 1.9 %collective-permute-done.3 = f32[32,512]{1,0:T(8,128)S(1)} collective-permute-done((f32[32,512]{1,0:T(8,128)S(1)}, f32[32,512]{1,0:T(8,128)S(1)}, u32[]{:S(2)}, u32[]{:S(2)}) %collective-permute-start.3) | collective-permute-done | bytes 65568 | tf_op jit(solution)/shard_map/ppermute | solution.py:130
  29.1 0.7 conditional.8
  29.1 0.3 fusion.37
  29.5 0.3 fusion.35
  29.8 0.7 collective-permute-start.4
  30.5 0.7 conditional.9
  30.6 0.3 fusion.76
  30.9 0.3 fusion.74
  31.2 0.7 collective-permute-start.5
  31.9 0.7 conditional.10
  32.0 0.3 fusion.115
  32.3 0.3 fusion.113
  32.6 0.7 collective-permute-start.6
  33.3 0.7 conditional.11
  33.4 0.3 fusion.154
  33.7 0.3 fusion.152
  34.0 0.7 collective-permute-start.7
  34.7 0.7 conditional.12
  34.8 0.3 fusion.193
  35.1 0.3 fusion.191
  35.4 0.7 collective-permute-start.8
  36.1 0.7 conditional.13
  36.2 0.3 fusion.232
  36.5 0.3 fusion.230
  36.8 1.3 %collective-permute-start.9 = (f32[32,512]{1,0:T(8,128)S(1)}, f32[32,512]{1,0:T(8,128)S(1)}, u32[]{:S(2)}, u32[]{:S(2)}) collective-permute-start(f32[32,512]{1,0:T(8,128)S(1)} %get-tuple-element.328), channel_id=1, source_target_pairs={{24,28},{25,29},{26,30},{27,31},{4,0},{5,1},{6,2},{7,3}} | collective-permute-start | bytes 196616 | tf_op jit(solution)/shard_map/ppermute | solution.py:130
  38.2 26.9 %collective-permute-done.9 = f32[32,512]{1,0:T(8,128)S(1)} collective-permute-done((f32[32,512]{1,0:T(8,128)S(1)}, f32[32,512]{1,0:T(8,128)S(1)}, u32[]{:S(2)}, u32[]{:S(2)}) %collective-permute-start.9) | collective-permute-done | bytes 65568 | tf_op jit(solution)/shard_map/ppermute | solution.py:130
  65.6 0.3 fusion.271
  66.1 1.6 %collective-permute-start.11 = (f32[2,2,32,128]{3,2,1,0:T(8,128)S(1)}, f32[2,2,32,128]{3,2,1,0:T(8,128)S(1)}, u32[]{:S(2)}, u32[]{:S(2)}) collective-permute-start(f32[2,2,32,128]{3,2,1,0:T(8,128)S(1)} %get-tuple-element.293), channel_id=1, source_target_pairs={{0,2},{1,3},{2,0},{3,1},{4,6},{5,7},{6,4},{7,5},{8,10},{9,11},{10,... | collective-permute-start | bytes 196616 | tf_op jit(solution)/shard_map/ppermute | solution.py:161
  67.7 0.2 collective-permute-start.12
  68.0 3.8 %collective-permute-done.11 = f32[2,2,32,128]{3,2,1,0:T(8,128)S(1)} collective-permute-done((f32[2,2,32,128]{3,2,1,0:T(8,128)S(1)}, f32[2,2,32,128]{3,2,1,0:T(8,128)S(1)}, u32[]{:S(2)}, u32[]{:S(2)}) %collective-permute-start.11) | collective-permute-done | bytes 65568 | tf_op jit(solution)/shard_map/ppermute | solution.py:161
  72.0 0.7 pad_maximum_fusion.3
  (88 shorter events, 2.5 us)
Async XLA Ops:
  0.6 8.1 %copy-start.1 = (s32[8,8]{1,0:T(8,128)S(1)}, s32[8,8]{1,0:T(8,128)}, u32[]{:S(2)}) copy-start(s32[8,8]{1,0:T(8,128)} %param.23) | copy-start | bytes 772
  4.1 7.5 %collective-permute-start.2 = (bf16[1104,128]{1,0:T(8,128)(2,1)}, bf16[1104,128]{1,0:T(8,128)(2,1)S(1)}, u32[]{:S(2)}, u32[]{:S(2)}) collective-permute-start(bf16[1104,128]{1,0:T(8,128)(2,1)} %get-tuple-element.282), channel_id=1, source_target_pairs={{0,1},{1,2},{2,3},{3,0},{4,5},{5,6},{6,7},{7,4},{8,9},{9,10},{10,1... | collective-permute-start | bytes 847880 | tf_op jit(solution)/shard_map/ppermute | solution.py:65
  4.5 8.9 %collective-permute-start = (bf16[1104,128]{1,0:T(8,128)(2,1)S(1)}, bf16[1104,128]{1,0:T(8,128)(2,1)S(1)}, u32[]{:S(2)}, u32[]{:S(2)}) collective-permute-start(bf16[1104,128]{1,0:T(8,128)(2,1)S(1)} %get-tuple-element.283), channel_id=1, source_target_pairs={{0,3},{1,0},{2,1},{3,2},{4,7},{5,4},{6,5},{7,6},{8,11},{9,8},{10,9... | collective-permute-start | bytes 847880 | tf_op jit(solution)/shard_map/ppermute | solution.py:65
  6.5 13.6 %collective-permute-start.1 = (bf16[1104,128]{1,0:T(8,128)(2,1)S(1)}, bf16[1104,128]{1,0:T(8,128)(2,1)S(1)}, u32[]{:S(2)}, u32[]{:S(2)}) collective-permute-start(bf16[1104,128]{1,0:T(8,128)(2,1)S(1)} %get-tuple-element.284), channel_id=1, source_target_pairs={{0,2},{1,3},{2,0},{3,1},{4,6},{5,7},{6,4},{7,5},{8,10},{9,11},{10,... | collective-permute-start | bytes 847880 | tf_op jit(solution)/shard_map/ppermute | solution.py:65
  9.0 11.0 %copy-start = (bf16[2,512,128]{2,1,0:T(8,128)(2,1)S(1)}, bf16[2,512,128]{2,1,0:T(8,128)(2,1)}, u32[]{:S(2)}) copy-start(bf16[2,512,128]{2,1,0:T(8,128)(2,1)} %param.22) | copy-start | bytes 786436
  22.8 6.2 %collective-permute-start.3 = (f32[32,512]{1,0:T(8,128)S(1)}, f32[32,512]{1,0:T(8,128)S(1)}, u32[]{:S(2)}, u32[]{:S(2)}) collective-permute-start(f32[32,512]{1,0:T(8,128)S(1)} %get-tuple-element.322), channel_id=1, source_target_pairs={{0,4},{1,5},{2,6},{3,7},{28,24},{29,25},{30,26},{31,27}} | collective-permute-start | bytes 196616 | tf_op jit(solution)/shard_map/ppermute | solution.py:130
  29.8 0.7 collective-permute-start.4
  31.2 0.7 collective-permute-start.5
  32.6 0.7 collective-permute-start.6
  34.0 0.7 collective-permute-start.7
  35.4 0.7 collective-permute-start.8
  36.8 28.2 %collective-permute-start.9 = (f32[32,512]{1,0:T(8,128)S(1)}, f32[32,512]{1,0:T(8,128)S(1)}, u32[]{:S(2)}, u32[]{:S(2)}) collective-permute-start(f32[32,512]{1,0:T(8,128)S(1)} %get-tuple-element.328), channel_id=1, source_target_pairs={{24,28},{25,29},{26,30},{27,31},{4,0},{5,1},{6,2},{7,3}} | collective-permute-start | bytes 196616 | tf_op jit(solution)/shard_map/ppermute | solution.py:130
  66.0 2.0 %collective-permute-start.10 = (f32[2,2,32,128]{3,2,1,0:T(8,128)S(1)}, f32[2,2,32,128]{3,2,1,0:T(8,128)S(1)}, u32[]{:S(2)}, u32[]{:S(2)}) collective-permute-start(f32[2,2,32,128]{3,2,1,0:T(8,128)S(1)} %get-tuple-element.213), channel_id=1, source_target_pairs={{0,3},{1,0},{2,1},{3,2},{4,7},{5,4},{6,5},{7,6},{8,11},{9,8},{10,9... | collective-permute-start | bytes 196616 | tf_op jit(solution)/shard_map/ppermute | solution.py:161
  66.1 5.6 %collective-permute-start.11 = (f32[2,2,32,128]{3,2,1,0:T(8,128)S(1)}, f32[2,2,32,128]{3,2,1,0:T(8,128)S(1)}, u32[]{:S(2)}, u32[]{:S(2)}) collective-permute-start(f32[2,2,32,128]{3,2,1,0:T(8,128)S(1)} %get-tuple-element.293), channel_id=1, source_target_pairs={{0,2},{1,3},{2,0},{3,1},{4,6},{5,7},{6,4},{7,5},{8,10},{9,11},{10,... | collective-permute-start | bytes 196616 | tf_op jit(solution)/shard_map/ppermute | solution.py:161
  67.7 4.2 %collective-permute-start.12 = (f32[2,2,32,128]{3,2,1,0:T(8,128)S(1)}, f32[2,2,32,128]{3,2,1,0:T(8,128)S(1)}, u32[]{:S(2)}, u32[]{:S(2)}) collective-permute-start(f32[2,2,32,128]{3,2,1,0:T(8,128)S(1)} %get-tuple-element.294), channel_id=1, source_target_pairs={{0,1},{1,2},{2,3},{3,0},{4,5},{5,6},{6,7},{7,4},{8,9},{9,10},{10,1... | collective-permute-start | bytes 196616 | tf_op jit(solution)/shard_map/ppermute | solution.py:161

commit v12 on v11

--- a/solution.py
+++ b/solution.py
@@ -2,6 +2,8 @@
 import jax.numpy as jnp
 from jax import lax
 from jax.sharding import PartitionSpec as P
+from jax.experimental import pallas as pl
+from jax.experimental.pallas import tpu as pltpu
 
 
 def bf16_part(value):
@@ -25,6 +27,49 @@
     rest = value - high
     mid = bf16_part(rest)
     return jnp.stack([high, mid, rest - mid]).astype(jnp.bfloat16)
+
+
+def stage_kernel(flag_ref, x_ref, e_ref, w_ref, diag_ref, drive_ref, out_ref):
+    step_count = w_ref.shape[0]
+
+    def halves(value):
+        high = value.astype(jnp.bfloat16)
+        low = (value - high.astype(jnp.float32)).astype(jnp.bfloat16)
+        return high, low
+
+    @pl.when(flag_ref[0] == 1)
+    def _():
+        x = x_ref[...]
+        for k in range(step_count):
+            high, low = halves(x)
+            w = w_ref[k]
+            prod = jnp.dot(high, w, preferred_element_type=jnp.float32)
+            prod = prod + jnp.dot(low, w, preferred_element_type=jnp.float32)
+            x = prod + x * diag_ref[k : k + 1, :] + drive_ref[k]
+            out_ref[k] = x
+
+    @pl.when(flag_ref[0] != 1)
+    def _():
+        e = e_ref[...]
+        for j, k in enumerate(range(step_count - 1, -1, -1)):
+            z = e + drive_ref[k]
+            high, low = halves(z)
+            w = w_ref[k]
+            dims = (((1,), (1,)), ((), ()))
+            prod = lax.dot_general(high, w, dims, preferred_element_type=jnp.float32)
+            prod = prod + lax.dot_general(low, w, dims, preferred_element_type=jnp.float32)
+            e = prod + z * diag_ref[k : k + 1, :]
+            out_ref[j] = e
+
+
+def run_stage(flag, x, e, weights, diag, driven):
+    vmem = pl.BlockSpec(memory_space=pltpu.VMEM)
+    return pl.pallas_call(
+        stage_kernel,
+        out_shape=jax.ShapeDtypeStruct(driven.shape, jnp.float32),
+        in_specs=[pl.BlockSpec(memory_space=pltpu.SMEM)] + [vmem] * 5,
+        out_specs=vmem,
+    )(flag, x, e, weights, diag, driven)
 
 
 def passed_along(shard, axis, by):
@@ -118,13 +163,8 @@
     if time_groups <= 8 and time_groups % 2 == 0:
         last = time_groups - 1
         for k in range(last):
-            send = lax.cond(
-                tm_pos == k,
-                lambda x, e: forward(x)[-1],
-                lambda x, e: backward(e)[-1],
-                x_in,
-                e_in,
-            )
+            flag = (tm_pos == k).astype(jnp.int32).reshape(1)
+            send = run_stage(flag, x_in, e_in, weights, diag, driven)[-1]
             pairs = [(k * col_groups + c, (k + 1) * col_groups + c) for c in range(col_groups)]
             pairs += [((last - k) * col_groups + c, (last - k - 1) * col_groups + c) for c in range(col_groups)]
             got = lax.ppermute(send, ("tm", "col"), pairs)

time: 73 us -> 100 us (1.37)
  Pallas kernels: 0 us -> 19.1 us
  local copies, waits for them, and re-layouts: 3.15 us -> 10.3 us
  other arithmetic: 4.82 us -> 9.18 us
  matrix products: 4.43 us -> 0.67 us
    pallas_call x0 -> x7, Pallas kernels: none -> 19.1 us  [run_stage(): pl.pallas_call(stage_kernel, out_shape=jax.ShapeDtypeStruct(driven.shape,...]
    squeeze x0 -> x7, local copies, waits for them, and re-layouts: none -> 5.91 us  [local(): send = run_stage(flag, x_in, e_in, weights, diag, driven)[-1]]
    select_n x6, other arithmetic: 0.1 us -> 3.99 us  [local(): e_in = jnp.where(tm_pos == last - k - 1, got, e_in)]
    dot_general x17 -> x3, matrix products: 4.43 us -> 0.67 us  [split_dot(): lax.dot_general(both, weights, (((1,), (contract,)), ((), ())), preferred...]
    mul x1, other arithmetic: 0.11 us -> 1.11 us  [local(): packet[:, :n_coupling].reshape(col_groups, step_count, state_width, cols)...]
where the time goes in v12:
time: 100 us; the launch traced here: 99.2 us
  waiting for transfers between devices  43 us (43%)
  Pallas kernels  19.1 us (19%)
  starting transfers between devices  15.7 us (16%)
  local copies, waits for them, and re-layouts  10.3 us (10%)
  other arithmetic  9.18 us (9%)
  between operations  1.22 us (1%)
    ppermute x7, waiting for transfers between devices, local(): got = lax.ppermute(send, ('tm', 'col'), pairs)  28.7 us
    pallas_call x7, Pallas kernels, run_stage(): pl.pallas_call(stage_kernel, out_shape=jax.ShapeDtypeStruct(driven.shape,...  19.1 us
    ppermute x3, waiting for transfers between devices, local(): chunk = lax.ppermute(chunk, ('tm', 'col'), pairs)  10.2 us
    ppermute x7, starting transfers between devices, local(): got = lax.ppermute(send, ('tm', 'col'), pairs)  9.14 us
    squeeze x7, local copies, waits for them, and re-layouts, local(): send = run_stage(flag, x_in, e_in, weights, diag, driven)[-1]  5.91 us
    ppermute x3, starting transfers between devices, local(): chunk = lax.ppermute(chunk, ('tm', 'col'), pairs)  4.76 us
    ppermute x3, waiting for transfers between devices, local(): piece = lax.ppermute(piece, ('tm', 'col'), pairs)  4.02 us
    select_n x6, other arithmetic, local(): e_in = jnp.where(tm_pos == last - k - 1, got, e_in)  3.99 us
  transfers between devices with their start and end apart: 13, of which 8 were waited for; matrix products, arithmetic and copies ran while one was open for 1% of the time, Pallas kernels for 0%

profile of v12, /device:TPU:0, one launch (start us, length us, event | category | flops | bytes accessed | tf_op | source)
XLA Modules:
  0.0 99.2 jit_solution(5632776030263965027)
XLA Ops:
  0.7 0.7 reduce-precision_convert_fusion.4
  1.4 0.8 copy.13
  2.3 1.1 %fusion.4 = (bf16[1104,128]{1,0:T(8,128)(2,1)S(1)}, bf16[1104,128]{1,0:T(8,128)(2,1)S(1)}, bf16[1104,128]{1,0:T(8,128)(2,1)S(1)}) fusion(bf16[9,128]{1,0:T(8,128)(2,1)S(1)} %convert_element_type.33, bf16[64,128]{1,0:T(8,128)(2,1)S(1)} %get-tuple-element.46, bf16[1024,128]{1,0:T(8,128)(2,1)} %bitcast.114, bf16[64,128]{1,0:T(8,128)(2,1)S(1)} %get-tuple-element.48, ...), kind=kLoop, calls=%fused_computation.15 | loop fusion | flops 2260992 | bytes 1161472 | tf_op jit(solution)/shard_map/concatenate | solution.py:103
  3.4 0.5 collective-permute-start.2
  3.9 2.0 %collective-permute-start = (bf16[1104,128]{1,0:T(8,128)(2,1)S(1)}, bf16[1104,128]{1,0:T(8,128)(2,1)S(1)}, u32[]{:S(2)}, u32[]{:S(2)}) collective-permute-start(bf16[1104,128]{1,0:T(8,128)(2,1)S(1)} %get-tuple-element.18), channel_id=1, source_target_pairs={{0,3},{1,0},{2,1},{3,2},{4,7},{5,4},{6,5},{7,6},{8,11},{9,8},{10,9... | collective-permute-start | bytes 847880 | tf_op jit(solution)/shard_map/ppermute | solution.py:110
  5.9 2.2 %collective-permute-start.1 = (bf16[1104,128]{1,0:T(8,128)(2,1)S(1)}, bf16[1104,128]{1,0:T(8,128)(2,1)S(1)}, u32[]{:S(2)}, u32[]{:S(2)}) collective-permute-start(bf16[1104,128]{1,0:T(8,128)(2,1)S(1)} %get-tuple-element.19), channel_id=1, source_target_pairs={{0,2},{1,3},{2,0},{3,1},{4,6},{5,7},{6,4},{7,5},{8,10},{9,11},{10,... | collective-permute-start | bytes 847880 | tf_op jit(solution)/shard_map/ppermute | solution.py:110
  8.3 0.6 mul.46
  9.0 1.6 %collective-permute-done.2 = bf16[1104,128]{1,0:T(8,128)(2,1)S(1)} collective-permute-done((bf16[1104,128]{1,0:T(8,128)(2,1)S(1)}, bf16[1104,128]{1,0:T(8,128)(2,1)S(1)}, u32[]{:S(2)}, u32[]{:S(2)}) %collective-permute-start.2) | collective-permute-done | bytes 282656 | tf_op jit(solution)/shard_map/ppermute | solution.py:110
  10.5 2.5 %collective-permute-done = bf16[1104,128]{1,0:T(8,128)(2,1)S(1)} collective-permute-done((bf16[1104,128]{1,0:T(8,128)(2,1)S(1)}, bf16[1104,128]{1,0:T(8,128)(2,1)S(1)}, u32[]{:S(2)}, u32[]{:S(2)}) %collective-permute-start) | collective-permute-done | bytes 282656 | tf_op jit(solution)/shard_map/ppermute | solution.py:110
  13.0 6.2 %collective-permute-done.1 = bf16[1104,128]{1,0:T(8,128)(2,1)S(1)} collective-permute-done((bf16[1104,128]{1,0:T(8,128)(2,1)S(1)}, bf16[1104,128]{1,0:T(8,128)(2,1)S(1)}, u32[]{:S(2)}, u32[]{:S(2)}) %collective-permute-start.1) | collective-permute-done | bytes 282656 | tf_op jit(solution)/shard_map/ppermute | solution.py:110
  19.9 0.6 copy.19
  20.5 0.8 copy.14
  21.4 0.4 reshape.303
  22.0 0.7 broadcast_multiply_fusion.1.drive_ref
  22.6 1.1 %broadcast_multiply_fusion.w_ref = bf16[2,512,512]{2,1,0:T(8,128)(2,1)} fusion(bf16[2,512,512]{2,1,0:T(8,128)(2,1)S(1)} %reshape.303, bf16[512,512]{1,0:T(8,128)(2,1)S(1)} %mul.46), kind=kLoop, calls=%fused_computation.6 | loop fusion | flops 524288 | bytes 2621440 | tf_op jit(solution)/shard_map/mul | solution.py:126
  23.7 0.6 broadcast_in_dim.4.x_ref.e_ref
  24.4 2.5 %shard_map.68 = f32[2,32,512]{2,1,0:T(8,128)} custom-call(s32[1]{0:T(128)} %bitcast.6.flag_ref, f32[32,512]{1,0:T(8,128)} %broadcast_in_dim.4.x_ref.e_ref, f32[32,512]{1,0:T(8,128)} %broadcast_in_dim.4.x_ref.e_ref, bf16[2,512,512]{2,1,0:T(8,128)(2,1)} %broadcast_multiply_fusion.w_ref, f32[2,512]{1,0:T(2,128)} %bitcast.122, ...), custom_call_target="tpu_custom_call" | custom-call | tf_op jit(solution)/shard_map/pallas_call | solution.py:67
  26.9 0.8 slice_bitcast_fusion.13
  27.7 4.5 %collective-permute-start.3 = (f32[32,512]{1,0:T(8,128)S(1)}, f32[32,512]{1,0:T(8,128)S(1)}, u32[]{:S(2)}, u32[]{:S(2)}) collective-permute-start(f32[32,512]{1,0:T(8,128)S(1)} %slice_bitcast_fusion.13), channel_id=1, source_target_pairs={{0,4},{1,5},{2,6},{3,7},{28,24},{29,25},{30,26},{31,27}} | collective-permute-start | bytes 196616 | tf_op jit(solution)/shard_map/ppermute | solution.py:170
  32.2 1.9 %collective-permute-done.3 = f32[32,512]{1,0:T(8,128)S(1)} collective-permute-done((f32[32,512]{1,0:T(8,128)S(1)}, f32[32,512]{1,0:T(8,128)S(1)}, u32[]{:S(2)}, u32[]{:S(2)}) %collective-permute-start.3) | collective-permute-done | bytes 65568 | tf_op jit(solution)/shard_map/ppermute | solution.py:170
  34.1 0.7 broadcast_select_fusion
  34.7 2.8 %shard_map.69 = f32[2,32,512]{2,1,0:T(8,128)} custom-call(s32[1]{0:T(128)} %bitcast.5.flag_ref, f32[32,512]{1,0:T(8,128)} %get-tuple-element.44.x_ref, f32[32,512]{1,0:T(8,128)} %get-tuple-element.43.e_ref, bf16[2,512,512]{2,1,0:T(8,128)(2,1)} %broadcast_multiply_fusion.w_ref, f32[2,512]{1,0:T(2,128)} %bitcast.123, ...), custom_call_target="tpu_custom_call" | custom-call | tf_op jit(solution)/shard_map/pallas_call | solution.py:67
  37.5 0.8 slice_bitcast_fusion.12
  38.3 0.7 collective-permute-start.4
  39.0 0.7 broadcast_select_fusion.11
  39.7 2.8 %shard_map.70 = f32[2,32,512]{2,1,0:T(8,128)} custom-call(s32[1]{0:T(128)} %bitcast.4.flag_ref, f32[32,512]{1,0:T(8,128)} %get-tuple-element.42.x_ref, f32[32,512]{1,0:T(8,128)} %get-tuple-element.41.e_ref, bf16[2,512,512]{2,1,0:T(8,128)(2,1)} %broadcast_multiply_fusion.w_ref, f32[2,512]{1,0:T(2,128)} %bitcast.124, ...), custom_call_target="tpu_custom_call" | custom-call | tf_op jit(solution)/shard_map/pallas_call | solution.py:67
  42.5 0.8 slice_bitcast_fusion.11
  43.3 0.7 collective-permute-start.5
  44.0 0.7 broadcast_select_fusion.9
  44.7 2.8 %shard_map.71 = f32[2,32,512]{2,1,0:T(8,128)} custom-call(s32[1]{0:T(128)} %bitcast.3.flag_ref, f32[32,512]{1,0:T(8,128)} %get-tuple-element.40.x_ref, f32[32,512]{1,0:T(8,128)} %get-tuple-element.39.e_ref, bf16[2,512,512]{2,1,0:T(8,128)(2,1)} %broadcast_multiply_fusion.w_ref, f32[2,512]{1,0:T(2,128)} %bitcast.125, ...), custom_call_target="tpu_custom_call" | custom-call | tf_op jit(solution)/shard_map/pallas_call | solution.py:67
  47.5 0.8 slice_bitcast_fusion.10
  48.3 0.7 collective-permute-start.6
  49.0 0.7 broadcast_select_fusion.6
  49.7 2.8 %shard_map.72 = f32[2,32,512]{2,1,0:T(8,128)} custom-call(s32[1]{0:T(128)} %bitcast.2.flag_ref, f32[32,512]{1,0:T(8,128)} %get-tuple-element.38.x_ref, f32[32,512]{1,0:T(8,128)} %get-tuple-element.37.e_ref, bf16[2,512,512]{2,1,0:T(8,128)(2,1)} %broadcast_multiply_fusion.w_ref, f32[2,512]{1,0:T(2,128)} %bitcast.126, ...), custom_call_target="tpu_custom_call" | custom-call | tf_op jit(solution)/shard_map/pallas_call | solution.py:67
  52.4 0.8 slice_bitcast_fusion.9
  53.3 0.7 collective-permute-start.7
  54.0 0.7 broadcast_select_fusion.4
  54.6 2.8 %shard_map.73 = f32[2,32,512]{2,1,0:T(8,128)} custom-call(s32[1]{0:T(128)} %bitcast.1.flag_ref, f32[32,512]{1,0:T(8,128)} %get-tuple-element.36.x_ref, f32[32,512]{1,0:T(8,128)} %get-tuple-element.35.e_ref, bf16[2,512,512]{2,1,0:T(8,128)(2,1)} %broadcast_multiply_fusion.w_ref, f32[2,512]{1,0:T(2,128)} %bitcast.127, ...), custom_call_target="tpu_custom_call" | custom-call | tf_op jit(solution)/shard_map/pallas_call | solution.py:67
  57.4 0.8 slice_bitcast_fusion.8
  58.3 0.7 collective-permute-start.8
  59.0 0.7 broadcast_select_fusion.3
  59.6 2.8 %shard_map.74 = f32[2,32,512]{2,1,0:T(8,128)} custom-call(s32[1]{0:T(128)} %bitcast.flag_ref, f32[32,512]{1,0:T(8,128)} %get-tuple-element.34.x_ref, f32[32,512]{1,0:T(8,128)} %get-tuple-element.33.e_ref, bf16[2,512,512]{2,1,0:T(8,128)(2,1)} %broadcast_multiply_fusion.w_ref, f32[2,512]{1,0:T(2,128)} %bitcast.128, ...), custom_call_target="tpu_custom_call" | custom-call | tf_op jit(solution)/shard_map/pallas_call | solution.py:67
  62.4 0.8 slice_bitcast_fusion.7
  63.2 1.4 %collective-permute-start.9 = (f32[32,512]{1,0:T(8,128)S(1)}, f32[32,512]{1,0:T(8,128)S(1)}, u32[]{:S(2)}, u32[]{:S(2)}) collective-permute-start(f32[32,512]{1,0:T(8,128)S(1)} %slice_bitcast_fusion.7), channel_id=1, source_target_pairs={{24,28},{25,29},{26,30},{27,31},{4,0},{5,1},{6,2},{7,3}} | collective-permute-start | bytes 196616 | tf_op jit(solution)/shard_map/ppermute | solution.py:170
  64.7 26.9 %collective-permute-done.9 = f32[32,512]{1,0:T(8,128)S(1)} collective-permute-done((f32[32,512]{1,0:T(8,128)S(1)}, f32[32,512]{1,0:T(8,128)S(1)}, u32[]{:S(2)}, u32[]{:S(2)}) %collective-permute-start.9) | collective-permute-done | bytes 65568 | tf_op jit(solution)/shard_map/ppermute | solution.py:170
  92.6 1.6 %collective-permute-start.11 = (f32[2,2,32,128]{3,2,1,0:T(8,128)S(1)}, f32[2,2,32,128]{3,2,1,0:T(8,128)S(1)}, u32[]{:S(2)}, u32[]{:S(2)}) collective-permute-start(f32[2,2,32,128]{3,2,1,0:T(8,128)S(1)} %get-tuple-element.28), channel_id=1, source_target_pairs={{0,2},{1,3},{2,0},{3,1},{4,6},{5,7},{6,4},{7,5},{8,10},{9,11},{10,... | collective-permute-start | bytes 196616 | tf_op jit(solution)/shard_map/ppermute | solution.py:201
  94.5 3.8 %collective-permute-done.11 = f32[2,2,32,128]{3,2,1,0:T(8,128)S(1)} collective-permute-done((f32[2,2,32,128]{3,2,1,0:T(8,128)S(1)}, f32[2,2,32,128]{3,2,1,0:T(8,128)S(1)}, u32[]{:S(2)}, u32[]{:S(2)}) %collective-permute-start.11) | collective-permute-done | bytes 65568 | tf_op jit(solution)/shard_map/ppermute | solution.py:201
  98.5 0.7 pad_maximum_fusion.1
  (75 shorter events, 2.7 us)
Async XLA Ops:
  0.6 7.5 %copy-start.15 = (s32[8,8]{1,0:T(8,128)S(1)}, s32[8,8]{1,0:T(8,128)}, u32[]{:S(2)}) copy-start(s32[8,8]{1,0:T(8,128)} %param.9) | copy-start | bytes 772
  3.4 7.2 %collective-permute-start.2 = (bf16[1104,128]{1,0:T(8,128)(2,1)S(1)}, bf16[1104,128]{1,0:T(8,128)(2,1)S(1)}, u32[]{:S(2)}, u32[]{:S(2)}) collective-permute-start(bf16[1104,128]{1,0:T(8,128)(2,1)S(1)} %get-tuple-element.17), channel_id=1, source_target_pairs={{0,1},{1,2},{2,3},{3,0},{4,5},{5,6},{6,7},{7,4},{8,9},{9,10},{10,1... | collective-permute-start | bytes 847880 | tf_op jit(solution)/shard_map/ppermute | solution.py:110
  3.9 9.1 %collective-permute-start = (bf16[1104,128]{1,0:T(8,128)(2,1)S(1)}, bf16[1104,128]{1,0:T(8,128)(2,1)S(1)}, u32[]{:S(2)}, u32[]{:S(2)}) collective-permute-start(bf16[1104,128]{1,0:T(8,128)(2,1)S(1)} %get-tuple-element.18), channel_id=1, source_target_pairs={{0,3},{1,0},{2,1},{3,2},{4,7},{5,4},{6,5},{7,6},{8,11},{9,8},{10,9... | collective-permute-start | bytes 847880 | tf_op jit(solution)/shard_map/ppermute | solution.py:110
  5.9 13.3 %collective-permute-start.1 = (bf16[1104,128]{1,0:T(8,128)(2,1)S(1)}, bf16[1104,128]{1,0:T(8,128)(2,1)S(1)}, u32[]{:S(2)}, u32[]{:S(2)}) collective-permute-start(bf16[1104,128]{1,0:T(8,128)(2,1)S(1)} %get-tuple-element.19), channel_id=1, source_target_pairs={{0,2},{1,3},{2,0},{3,1},{4,6},{5,7},{6,4},{7,5},{8,10},{9,11},{10,... | collective-permute-start | bytes 847880 | tf_op jit(solution)/shard_map/ppermute | solution.py:110
  8.1 11.0 %copy-start.2 = (bf16[2,512,128]{2,1,0:T(8,128)(2,1)S(1)}, bf16[2,512,128]{2,1,0:T(8,128)(2,1)}, u32[]{:S(2)}) copy-start(bf16[2,512,128]{2,1,0:T(8,128)(2,1)} %param.8) | copy-start | bytes 786436
  27.7 6.4 %collective-permute-start.3 = (f32[32,512]{1,0:T(8,128)S(1)}, f32[32,512]{1,0:T(8,128)S(1)}, u32[]{:S(2)}, u32[]{:S(2)}) collective-permute-start(f32[32,512]{1,0:T(8,128)S(1)} %slice_bitcast_fusion.13), channel_id=1, source_target_pairs={{0,4},{1,5},{2,6},{3,7},{28,24},{29,25},{30,26},{31,27}} | collective-permute-start | bytes 196616 | tf_op jit(solution)/shard_map/ppermute | solution.py:170
  34.7 4.3 %copy-start.12 = (f32[32,512]{1,0:T(8,128)S(1)}, f32[32,512]{1,0:T(8,128)}, u32[]{:S(2)}) copy-start(f32[32,512]{1,0:T(8,128)} %get-tuple-element.43.e_ref) | copy-start | bytes 196612
  34.7 4.3 %copy-start.13 = (f32[32,512]{1,0:T(8,128)S(1)}, f32[32,512]{1,0:T(8,128)}, u32[]{:S(2)}) copy-start(f32[32,512]{1,0:T(8,128)} %get-tuple-element.44.x_ref) | copy-start | bytes 196612
  38.3 0.7 collective-permute-start.4
  39.7 4.3 %copy-start.8 = (f32[32,512]{1,0:T(8,128)S(1)}, f32[32,512]{1,0:T(8,128)}, u32[]{:S(2)}) copy-start(f32[32,512]{1,0:T(8,128)} %get-tuple-element.41.e_ref) | copy-start | bytes 196612
  39.7 4.3 %copy-start.9 = (f32[32,512]{1,0:T(8,128)S(1)}, f32[32,512]{1,0:T(8,128)}, u32[]{:S(2)}) copy-start(f32[32,512]{1,0:T(8,128)} %get-tuple-element.42.x_ref) | copy-start | bytes 196612
  43.3 0.7 collective-permute-start.5
  44.7 4.3 %copy-start.10 = (f32[32,512]{1,0:T(8,128)S(1)}, f32[32,512]{1,0:T(8,128)}, u32[]{:S(2)}) copy-start(f32[32,512]{1,0:T(8,128)} %get-tuple-element.39.e_ref) | copy-start | bytes 196612
  44.7 4.3 %copy-start.11 = (f32[32,512]{1,0:T(8,128)S(1)}, f32[32,512]{1,0:T(8,128)}, u32[]{:S(2)}) copy-start(f32[32,512]{1,0:T(8,128)} %get-tuple-element.40.x_ref) | copy-start | bytes 196612
  48.3 0.7 collective-permute-start.6
  49.7 4.3 %copy-start.4 = (f32[32,512]{1,0:T(8,128)S(1)}, f32[32,512]{1,0:T(8,128)}, u32[]{:S(2)}) copy-start(f32[32,512]{1,0:T(8,128)} %get-tuple-element.37.e_ref) | copy-start | bytes 196612
  49.7 4.3 %copy-start.5 = (f32[32,512]{1,0:T(8,128)S(1)}, f32[32,512]{1,0:T(8,128)}, u32[]{:S(2)}) copy-start(f32[32,512]{1,0:T(8,128)} %get-tuple-element.38.x_ref) | copy-start | bytes 196612
  53.3 0.7 collective-permute-start.7
  54.6 4.3 %copy-start.6 = (f32[32,512]{1,0:T(8,128)S(1)}, f32[32,512]{1,0:T(8,128)}, u32[]{:S(2)}) copy-start(f32[32,512]{1,0:T(8,128)} %get-tuple-element.35.e_ref) | copy-start | bytes 196612
  54.6 4.3 %copy-start.7 = (f32[32,512]{1,0:T(8,128)S(1)}, f32[32,512]{1,0:T(8,128)}, u32[]{:S(2)}) copy-start(f32[32,512]{1,0:T(8,128)} %get-tuple-element.36.x_ref) | copy-start | bytes 196612
  58.3 0.7 collective-permute-start.8
  58.9 32.7 %copy-start = (bf16[2,512,512]{2,1,0:T(8,128)(2,1)S(1)}, bf16[2,512,512]{2,1,0:T(8,128)(2,1)}, u32[]{:S(2)}) copy-start(bf16[2,512,512]{2,1,0:T(8,128)(2,1)} %broadcast_multiply_fusion.w_ref) | copy-start | bytes 3145732
  59.6 31.9 %copy-start.3 = (f32[32,512]{1,0:T(8,128)S(1)}, f32[32,512]{1,0:T(8,128)}, u32[]{:S(2)}) copy-start(f32[32,512]{1,0:T(8,128)} %get-tuple-element.34.x_ref) | copy-start | bytes 196612
  59.6 32.2 %copy-start.1 = (f32[2,32,512]{2,1,0:T(8,128)S(1)}, f32[2,32,512]{2,1,0:T(8,128)}, u32[]{:S(2)}) copy-start(f32[2,32,512]{2,1,0:T(8,128)} %broadcast_multiply_fusion.1.drive_ref) | copy-start | bytes 393220
  63.2 28.8 %copy-start.14 = (f32[32,512]{1,0:T(8,128)S(1)}, f32[32,512]{1,0:T(8,128)}, u32[]{:S(2)}) copy-start(f32[32,512]{1,0:T(8,128)} %get-tuple-element.33.e_ref) | copy-start | bytes 196612
  63.2 28.3 %collective-permute-start.9 = (f32[32,512]{1,0:T(8,128)S(1)}, f32[32,512]{1,0:T(8,128)S(1)}, u32[]{:S(2)}, u32[]{:S(2)}) collective-permute-start(f32[32,512]{1,0:T(8,128)S(1)} %slice_bitcast_fusion.7), channel_id=1, source_target_pairs={{24,28},{25,29},{26,30},{27,31},{4,0},{5,1},{6,2},{7,3}} | collective-permute-start | bytes 196616 | tf_op jit(solution)/shard_map/ppermute | solution.py:170
  92.5 2.0 %collective-permute-start.10 = (f32[2,2,32,128]{3,2,1,0:T(8,128)S(1)}, f32[2,2,32,128]{3,2,1,0:T(8,128)S(1)}, u32[]{:S(2)}, u32[]{:S(2)}) collective-permute-start(f32[2,2,32,128]{3,2,1,0:T(8,128)S(1)} %get-tuple-element.2), channel_id=1, source_target_pairs={{0,3},{1,0},{2,1},{3,2},{4,7},{5,4},{6,5},{7,6},{8,11},{9,8},{10,9... | collective-permute-start | bytes 196616 | tf_op jit(solution)/shard_map/ppermute | solution.py:201
  92.6 5.6 %collective-permute-start.11 = (f32[2,2,32,128]{3,2,1,0:T(8,128)S(1)}, f32[2,2,32,128]{3,2,1,0:T(8,128)S(1)}, u32[]{:S(2)}, u32[]{:S(2)}) collective-permute-start(f32[2,2,32,128]{3,2,1,0:T(8,128)S(1)} %get-tuple-element.28), channel_id=1, source_target_pairs={{0,2},{1,3},{2,0},{3,1},{4,6},{5,7},{6,4},{7,5},{8,10},{9,11},{10,... | collective-permute-start | bytes 196616 | tf_op jit(solution)/shard_map/ppermute | solution.py:201
  94.2 4.2 %collective-permute-start.12 = (f32[2,2,32,128]{3,2,1,0:T(8,128)S(1)}, f32[2,2,32,128]{3,2,1,0:T(8,128)S(1)}, u32[]{:S(2)}, u32[]{:S(2)}) collective-permute-start(f32[2,2,32,128]{3,2,1,0:T(8,128)S(1)} %get-tuple-element.29), channel_id=1, source_target_pairs={{0,1},{1,2},{2,3},{3,0},{4,5},{5,6},{6,7},{7,4},{8,9},{9,10},{10,1... | collective-permute-start | bytes 196616 | tf_op jit(solution)/shard_map/ppermute | solution.py:201

commit v13 on v10

--- a/solution.py
+++ b/solution.py
@@ -71,18 +71,16 @@
             out = jnp.where(which == shift, chunks[shift], out)
         return out
 
-    packet = jnp.stack([from_source(j) for j in range(col_groups)])
+    sourced = [from_source(j) for j in range(col_groups)]
+    packet = jnp.stack(sourced)
     n_coupling = step_count * state_width
     n_seen = step_count * own_rows
     mask = jnp.broadcast_to(
         pattern.astype(jnp.bfloat16)[:, None, :, None],
         (block_count, block_size, block_count, block_size),
     ).reshape(state_width, state_width)
-    weights = (
-        packet[:, :n_coupling]
-        .reshape(col_groups, step_count, state_width, cols)
-        .transpose(1, 2, 0, 3)
-        .reshape(step_count, state_width, state_width)
+    weights = jnp.concatenate(
+        [part[:n_coupling].reshape(step_count, state_width, cols) for part in sourced], axis=2
     ) * mask[None]
     seen = (
         packet[:, n_coupling : n_coupling + n_seen]

time: 73 us -> 71.1 us (0.974)
  local copies, waits for them, and re-layouts: 4.5 us -> 3.33 us
    slice x1 -> x4, local copies, waits for them, and re-layouts: 0.81 us -> 0.08 us  [local(): part[:n_coupling].reshape(step_count, state_width, cols)]
    another operation x30 -> x27, other arithmetic: 1.74 us -> 1.18 us
where the time goes in v13:
time: 71.1 us; the launch traced here: 70.6 us
  waiting for transfers between devices  40.9 us (58%)
  starting transfers between devices  16.8 us (24%)
  matrix products  4.43 us (6%)
  other arithmetic  3.52 us (5%)
  local copies, waits for them, and re-layouts  3.33 us (5%)
  between operations  1.22 us (2%)
    ppermute x7, waiting for transfers between devices, local(): got = lax.ppermute(send, ('tm', 'col'), pairs)  28.8 us
    ppermute x3, waiting for transfers between devices, local(): chunk = lax.ppermute(chunk, ('tm', 'col'), pairs)  10.2 us
    ppermute x7, starting transfers between devices, local(): got = lax.ppermute(send, ('tm', 'col'), pairs)  8.96 us
    ppermute x3, starting transfers between devices, local(): chunk = lax.ppermute(chunk, ('tm', 'col'), pairs)  4.76 us
    dot_general x17, matrix products, split_dot(): lax.dot_general(both, weights, (((1,), (contract,)), ((), ())), preferred...  4.43 us
    ppermute x3, starting transfers between devices, local(): piece = lax.ppermute(piece, ('tm', 'col'), pairs)  3.06 us
    ppermute x3, waiting for transfers between devices, local(): piece = lax.ppermute(piece, ('tm', 'col'), pairs)  1.9 us
  transfers between devices with their start and end apart: 13, of which 8 were waited for; matrix products, arithmetic and copies ran while one was open for 1% of the time, Pallas kernels for 0%

profile of v13, /device:TPU:0, one launch (start us, length us, event | category | flops | bytes accessed | tf_op | source)
XLA Modules:
  0.0 70.6 jit_solution(12111205060384783072)
XLA Ops:
  0.7 0.7 %reduce-precision_convert_fusion.31 = (bf16[1,3,128]{2,1,0:T(4,128)(2,1)S(1)}, bf16[1,3,128]{2,1,0:T(4,128)(2,1)S(1)}, bf16[1,3,128]{2,1,0:T(4,128)(2,1)S(1)}) fusion(f32[1,1,128]{2,1,0:T(1,128)} %bitcast.380, f32[1,2,128]{2,1,0:T(2,128)} %bitcast.379), kind=kLoop, calls=%fused_computation.460 | loop fusion | flops 3072 | bytes 3840 | tf_op jit(solution)/shard_map/convert.66
  1.4 0.8 %copy.13 = bf16[4,2,32,128]{3,2,1,0:T(8,128)(2,1)S(1)} copy(bf16[4,2,32,128]{3,2,0,1:T(8,128)(2,1)} %bitcast.350) | data formatting | bytes 131072 | tf_op jit(solution)/shard_map/transpose | solution.py:52
  2.3 1.1 %fusion.273 = (bf16[1104,128]{1,0:T(8,128)(2,1)S(1)}, bf16[1104,128]{1,0:T(8,128)(2,1)S(1)}, bf16[1104,128]{1,0:T(8,128)(2,1)S(1)}) fusion(bf16[9,128]{1,0:T(8,128)(2,1)S(1)} %convert_element_type.57, bf16[64,128]{1,0:T(8,128)(2,1)S(1)} %get-tuple-element.309, bf16[1024,128]{1,0:T(8,128)(2,1)} %bitcast.320, bf16[64,128]{1,0:T(8,128)(2,1)S(1)} %get-tuple-element.311, ...), kind=kLoop, calls=%fused_computation.373 | loop fusion | flops 2260992 | bytes 1161472 | tf_op jit(solution)/shard_map/concatenate | solution.py:58
  3.4 0.5 collective-permute-start.2
  3.9 2.0 %collective-permute-start = (bf16[1104,128]{1,0:T(8,128)(2,1)S(1)}, bf16[1104,128]{1,0:T(8,128)(2,1)S(1)}, u32[]{:S(2)}, u32[]{:S(2)}) collective-permute-start(bf16[1104,128]{1,0:T(8,128)(2,1)S(1)} %get-tuple-element.285), channel_id=1, source_target_pairs={{0,3},{1,0},{2,1},{3,2},{4,7},{5,4},{6,5},{7,6},{8,11},{9,8},{10,9... | collective-permute-start | bytes 847880 | tf_op jit(solution)/shard_map/ppermute | solution.py:65
  5.9 2.2 %collective-permute-start.1 = (bf16[1104,128]{1,0:T(8,128)(2,1)S(1)}, bf16[1104,128]{1,0:T(8,128)(2,1)S(1)}, u32[]{:S(2)}, u32[]{:S(2)}) collective-permute-start(bf16[1104,128]{1,0:T(8,128)(2,1)S(1)} %get-tuple-element.286), channel_id=1, source_target_pairs={{0,2},{1,3},{2,0},{3,1},{4,6},{5,7},{6,4},{7,5},{8,10},{9,11},{10,... | collective-permute-start | bytes 847880 | tf_op jit(solution)/shard_map/ppermute | solution.py:65
  8.3 0.6 mul.324
  9.0 1.5 %collective-permute-done.2 = bf16[1104,128]{1,0:T(8,128)(2,1)S(1)} collective-permute-done((bf16[1104,128]{1,0:T(8,128)(2,1)S(1)}, bf16[1104,128]{1,0:T(8,128)(2,1)S(1)}, u32[]{:S(2)}, u32[]{:S(2)}) %collective-permute-start.2) | collective-permute-done | bytes 282656 | tf_op jit(solution)/shard_map/ppermute | solution.py:65
  10.5 2.5 %collective-permute-done = bf16[1104,128]{1,0:T(8,128)(2,1)S(1)} collective-permute-done((bf16[1104,128]{1,0:T(8,128)(2,1)S(1)}, bf16[1104,128]{1,0:T(8,128)(2,1)S(1)}, u32[]{:S(2)}, u32[]{:S(2)}) %collective-permute-start) | collective-permute-done | bytes 282656 | tf_op jit(solution)/shard_map/ppermute | solution.py:65
  13.0 6.2 %collective-permute-done.1 = bf16[1104,128]{1,0:T(8,128)(2,1)S(1)} collective-permute-done((bf16[1104,128]{1,0:T(8,128)(2,1)S(1)}, bf16[1104,128]{1,0:T(8,128)(2,1)S(1)}, u32[]{:S(2)}, u32[]{:S(2)}) %collective-permute-start.1) | collective-permute-done | bytes 282656 | tf_op jit(solution)/shard_map/ppermute | solution.py:65
  20.0 0.3 maximum_multiply_fusion
  20.4 0.6 conditional.7
  20.4 0.2 fusion.21
  20.9 4.3 %collective-permute-start.3 = (f32[32,512]{1,0:T(8,128)S(1)}, f32[32,512]{1,0:T(8,128)S(1)}, u32[]{:S(2)}, u32[]{:S(2)}) collective-permute-start(f32[32,512]{1,0:T(8,128)S(1)} %get-tuple-element.318), channel_id=1, source_target_pairs={{0,4},{1,5},{2,6},{3,7},{28,24},{29,25},{30,26},{31,27}} | collective-permute-start | bytes 196616 | tf_op jit(solution)/shard_map/ppermute | solution.py:128
  25.3 1.9 %collective-permute-done.3 = f32[32,512]{1,0:T(8,128)S(1)} collective-permute-done((f32[32,512]{1,0:T(8,128)S(1)}, f32[32,512]{1,0:T(8,128)S(1)}, u32[]{:S(2)}, u32[]{:S(2)}) %collective-permute-start.3) | collective-permute-done | bytes 65568 | tf_op jit(solution)/shard_map/ppermute | solution.py:128
  27.2 0.7 conditional.8
  27.2 0.3 fusion.37
  27.6 0.3 fusion.35
  27.9 0.7 collective-permute-start.4
  28.6 0.7 conditional.9
  28.7 0.3 fusion.76
  29.0 0.3 fusion.74
  29.3 0.7 collective-permute-start.5
  30.0 0.7 conditional.10
  30.1 0.3 fusion.115
  30.4 0.3 fusion.113
  30.7 0.7 collective-permute-start.6
  31.4 0.7 conditional.11
  31.5 0.3 fusion.154
  31.8 0.3 fusion.152
  32.1 0.7 collective-permute-start.7
  32.8 0.7 conditional.12
  32.9 0.3 fusion.193
  33.2 0.3 fusion.191
  33.5 0.7 collective-permute-start.8
  34.2 0.7 conditional.13
  34.3 0.3 fusion.232
  34.6 0.3 fusion.230
  34.9 1.3 %collective-permute-start.9 = (f32[32,512]{1,0:T(8,128)S(1)}, f32[32,512]{1,0:T(8,128)S(1)}, u32[]{:S(2)}, u32[]{:S(2)}) collective-permute-start(f32[32,512]{1,0:T(8,128)S(1)} %get-tuple-element.324), channel_id=1, source_target_pairs={{24,28},{25,29},{26,30},{27,31},{4,0},{5,1},{6,2},{7,3}} | collective-permute-start | bytes 196616 | tf_op jit(solution)/shard_map/ppermute | solution.py:128
  36.3 26.9 %collective-permute-done.9 = f32[32,512]{1,0:T(8,128)S(1)} collective-permute-done((f32[32,512]{1,0:T(8,128)S(1)}, f32[32,512]{1,0:T(8,128)S(1)}, u32[]{:S(2)}, u32[]{:S(2)}) %collective-permute-start.9) | collective-permute-done | bytes 65568 | tf_op jit(solution)/shard_map/ppermute | solution.py:128
  63.7 0.3 fusion.271
  64.2 1.6 %collective-permute-start.11 = (f32[2,2,32,128]{3,2,1,0:T(8,128)S(1)}, f32[2,2,32,128]{3,2,1,0:T(8,128)S(1)}, u32[]{:S(2)}, u32[]{:S(2)}) collective-permute-start(f32[2,2,32,128]{3,2,1,0:T(8,128)S(1)} %get-tuple-element.292), channel_id=1, source_target_pairs={{0,2},{1,3},{2,0},{3,1},{4,6},{5,7},{6,4},{7,5},{8,10},{9,11},{10,... | collective-permute-start | bytes 196616 | tf_op jit(solution)/shard_map/ppermute | solution.py:159
  65.8 1.4 %collective-permute-start.10 = (f32[2,2,32,128]{3,2,1,0:T(8,128)S(1)}, f32[2,2,32,128]{3,2,1,0:T(8,128)S(1)}, u32[]{:S(2)}, u32[]{:S(2)}) collective-permute-start(f32[2,2,32,128]{3,2,1,0:T(8,128)S(1)} %get-tuple-element.293), channel_id=1, source_target_pairs={{0,3},{1,0},{2,1},{3,2},{4,7},{5,4},{6,5},{7,6},{8,11},{9,8},{10,9... | collective-permute-start | bytes 196616 | tf_op jit(solution)/shard_map/ppermute | solution.py:159
  67.2 0.7 collective-permute-done.12
  67.9 0.8 %collective-permute-done.11 = f32[2,2,32,128]{3,2,1,0:T(8,128)S(1)} collective-permute-done((f32[2,2,32,128]{3,2,1,0:T(8,128)S(1)}, f32[2,2,32,128]{3,2,1,0:T(8,128)S(1)}, u32[]{:S(2)}, u32[]{:S(2)}) %collective-permute-start.11) | collective-permute-done | bytes 65568 | tf_op jit(solution)/shard_map/ppermute | solution.py:159
  68.7 0.5 collective-permute-done.10
  69.3 0.7 copy.17
  69.9 0.7 copy.16
  (91 shorter events, 2.6 us)
Async XLA Ops:
  0.6 7.5 %copy-start.1 = (s32[8,8]{1,0:T(8,128)S(1)}, s32[8,8]{1,0:T(8,128)}, u32[]{:S(2)}) copy-start(s32[8,8]{1,0:T(8,128)} %param.23) | copy-start | bytes 772
  3.4 7.2 %collective-permute-start.2 = (bf16[1104,128]{1,0:T(8,128)(2,1)S(1)}, bf16[1104,128]{1,0:T(8,128)(2,1)S(1)}, u32[]{:S(2)}, u32[]{:S(2)}) collective-permute-start(bf16[1104,128]{1,0:T(8,128)(2,1)S(1)} %get-tuple-element.284), channel_id=1, source_target_pairs={{0,1},{1,2},{2,3},{3,0},{4,5},{5,6},{6,7},{7,4},{8,9},{9,10},{10,1... | collective-permute-start | bytes 847880 | tf_op jit(solution)/shard_map/ppermute | solution.py:65
  3.9 9.1 %collective-permute-start = (bf16[1104,128]{1,0:T(8,128)(2,1)S(1)}, bf16[1104,128]{1,0:T(8,128)(2,1)S(1)}, u32[]{:S(2)}, u32[]{:S(2)}) collective-permute-start(bf16[1104,128]{1,0:T(8,128)(2,1)S(1)} %get-tuple-element.285), channel_id=1, source_target_pairs={{0,3},{1,0},{2,1},{3,2},{4,7},{5,4},{6,5},{7,6},{8,11},{9,8},{10,9... | collective-permute-start | bytes 847880 | tf_op jit(solution)/shard_map/ppermute | solution.py:65
  5.9 13.3 %collective-permute-start.1 = (bf16[1104,128]{1,0:T(8,128)(2,1)S(1)}, bf16[1104,128]{1,0:T(8,128)(2,1)S(1)}, u32[]{:S(2)}, u32[]{:S(2)}) collective-permute-start(bf16[1104,128]{1,0:T(8,128)(2,1)S(1)} %get-tuple-element.286), channel_id=1, source_target_pairs={{0,2},{1,3},{2,0},{3,1},{4,6},{5,7},{6,4},{7,5},{8,10},{9,11},{10,... | collective-permute-start | bytes 847880 | tf_op jit(solution)/shard_map/ppermute | solution.py:65
  8.3 10.8 %copy-start = (bf16[2,512,128]{2,1,0:T(8,128)(2,1)S(1)}, bf16[2,512,128]{2,1,0:T(8,128)(2,1)}, u32[]{:S(2)}) copy-start(bf16[2,512,128]{2,1,0:T(8,128)(2,1)} %param.22) | copy-start | bytes 786436
  20.9 6.2 %collective-permute-start.3 = (f32[32,512]{1,0:T(8,128)S(1)}, f32[32,512]{1,0:T(8,128)S(1)}, u32[]{:S(2)}, u32[]{:S(2)}) collective-permute-start(f32[32,512]{1,0:T(8,128)S(1)} %get-tuple-element.318), channel_id=1, source_target_pairs={{0,4},{1,5},{2,6},{3,7},{28,24},{29,25},{30,26},{31,27}} | collective-permute-start | bytes 196616 | tf_op jit(solution)/shard_map/ppermute | solution.py:128
  27.9 0.7 collective-permute-start.4
  29.3 0.7 collective-permute-start.5
  30.7 0.7 collective-permute-start.6
  32.1 0.7 collective-permute-start.7
  33.5 0.7 collective-permute-start.8
  34.9 28.2 %collective-permute-start.9 = (f32[32,512]{1,0:T(8,128)S(1)}, f32[32,512]{1,0:T(8,128)S(1)}, u32[]{:S(2)}, u32[]{:S(2)}) collective-permute-start(f32[32,512]{1,0:T(8,128)S(1)} %get-tuple-element.324), channel_id=1, source_target_pairs={{24,28},{25,29},{26,30},{27,31},{4,0},{5,1},{6,2},{7,3}} | collective-permute-start | bytes 196616 | tf_op jit(solution)/shard_map/ppermute | solution.py:128
  64.1 3.8 %collective-permute-start.12 = (f32[2,2,32,128]{3,2,1,0:T(8,128)S(1)}, f32[2,2,32,128]{3,2,1,0:T(8,128)S(1)}, u32[]{:S(2)}, u32[]{:S(2)}) collective-permute-start(f32[2,2,32,128]{3,2,1,0:T(8,128)S(1)} %get-tuple-element.215), channel_id=1, source_target_pairs={{0,1},{1,2},{2,3},{3,0},{4,5},{5,6},{6,7},{7,4},{8,9},{9,10},{10,1... | collective-permute-start | bytes 196616 | tf_op jit(solution)/shard_map/ppermute | solution.py:159
  64.2 4.5 %collective-permute-start.11 = (f32[2,2,32,128]{3,2,1,0:T(8,128)S(1)}, f32[2,2,32,128]{3,2,1,0:T(8,128)S(1)}, u32[]{:S(2)}, u32[]{:S(2)}) collective-permute-start(f32[2,2,32,128]{3,2,1,0:T(8,128)S(1)} %get-tuple-element.292), channel_id=1, source_target_pairs={{0,2},{1,3},{2,0},{3,1},{4,6},{5,7},{6,4},{7,5},{8,10},{9,11},{10,... | collective-permute-start | bytes 196616 | tf_op jit(solution)/shard_map/ppermute | solution.py:159
  65.8 3.4 %collective-permute-start.10 = (f32[2,2,32,128]{3,2,1,0:T(8,128)S(1)}, f32[2,2,32,128]{3,2,1,0:T(8,128)S(1)}, u32[]{:S(2)}, u32[]{:S(2)}) collective-permute-start(f32[2,2,32,128]{3,2,1,0:T(8,128)S(1)} %get-tuple-element.293), channel_id=1, source_target_pairs={{0,3},{1,0},{2,1},{3,2},{4,7},{5,4},{6,5},{7,6},{8,11},{9,8},{10,9... | collective-permute-start | bytes 196616 | tf_op jit(solution)/shard_map/ppermute | solution.py:159

commit v14 on v13

--- a/solution.py
+++ b/solution.py
@@ -72,7 +72,6 @@
         return out
 
     sourced = [from_source(j) for j in range(col_groups)]
-    packet = jnp.stack(sourced)
     n_coupling = step_count * state_width
     n_seen = step_count * own_rows
     mask = jnp.broadcast_to(
@@ -82,16 +81,20 @@
     weights = jnp.concatenate(
         [part[:n_coupling].reshape(step_count, state_width, cols) for part in sourced], axis=2
     ) * mask[None]
-    seen = (
-        packet[:, n_coupling : n_coupling + n_seen]
-        .reshape(col_groups, step_count, own_rows, cols)
-        .transpose(1, 2, 0, 3)
-        .reshape(step_count, own_rows, state_width)
+    seen = jnp.concatenate(
+        [part[n_coupling : n_coupling + n_seen].reshape(step_count, own_rows, cols) for part in sourced],
+        axis=2,
     )
-    small = packet[:, n_coupling + n_seen : n_coupling + n_seen + small_rows].astype(jnp.float32)
-    small = small.reshape(col_groups, 3, step_count + 1, cols)
-    small = (small[:, 0] + small[:, 1] + small[:, 2]).transpose(1, 0, 2)
-    small = small.reshape(step_count + 1, state_width)
+    small = jnp.concatenate(
+        [
+            part[n_coupling + n_seen : n_coupling + n_seen + small_rows]
+            .astype(jnp.float32)
+            .reshape(3, step_count + 1, cols)
+            for part in sourced
+        ],
+        axis=2,
+    )
+    small = small[0] + small[1] + small[2]
     diag = small[:step_count]
     gain = small[step_count]
     driven = gain[None, None, :] * seen.astype(jnp.float32)

time: 71.1 us -> 71 us (level)
  no operation moved by 1% of the time
where the time goes in v14:
time: 71 us; the launch traced here: 70.5 us
  waiting for transfers between devices  40.9 us (58%)
  starting transfers between devices  16.8 us (24%)
  matrix products  4.43 us (6%)
  other arithmetic  3.52 us (5%)
  local copies, waits for them, and re-layouts  3.26 us (5%)
  between operations  1.25 us (2%)
    ppermute x7, waiting for transfers between devices, local(): got = lax.ppermute(send, ('tm', 'col'), pairs)  28.8 us
    ppermute x3, waiting for transfers between devices, local(): chunk = lax.ppermute(chunk, ('tm', 'col'), pairs)  10.2 us
    ppermute x7, starting transfers between devices, local(): got = lax.ppermute(send, ('tm', 'col'), pairs)  8.95 us
    ppermute x3, starting transfers between devices, local(): chunk = lax.ppermute(chunk, ('tm', 'col'), pairs)  4.76 us
    dot_general x17, matrix products, split_dot(): lax.dot_general(both, weights, (((1,), (contract,)), ((), ())), preferred...  4.43 us
    ppermute x3, starting transfers between devices, local(): piece = lax.ppermute(piece, ('tm', 'col'), pairs)  3.06 us
    ppermute x3, waiting for transfers between devices, local(): piece = lax.ppermute(piece, ('tm', 'col'), pairs)  1.9 us
  transfers between devices with their start and end apart: 13, of which 8 were waited for; matrix products, arithmetic and copies ran while one was open for 1% of the time, Pallas kernels for 0%

profile of v14, /device:TPU:0, one launch (start us, length us, event | category | flops | bytes accessed | tf_op | source)
XLA Modules:
  0.0 70.5 jit_solution(4212728175078704335)
XLA Ops:
  0.7 0.7 %reduce-precision_convert_fusion.31 = (bf16[1,3,128]{2,1,0:T(4,128)(2,1)S(1)}, bf16[1,3,128]{2,1,0:T(4,128)(2,1)S(1)}, bf16[1,3,128]{2,1,0:T(4,128)(2,1)S(1)}) fusion(f32[1,1,128]{2,1,0:T(1,128)} %bitcast.350, f32[1,2,128]{2,1,0:T(2,128)} %bitcast.349), kind=kLoop, calls=%fused_computation.454 | loop fusion | flops 3072 | bytes 3840 | tf_op jit(solution)/shard_map/convert.67
  1.4 0.8 %copy.9 = bf16[4,2,32,128]{3,2,1,0:T(8,128)(2,1)S(1)} copy(bf16[4,2,32,128]{3,2,0,1:T(8,128)(2,1)} %bitcast.316) | data formatting | bytes 131072 | tf_op jit(solution)/shard_map/transpose | solution.py:52
  2.3 1.1 %fusion.273 = (bf16[1104,128]{1,0:T(8,128)(2,1)S(1)}, bf16[1104,128]{1,0:T(8,128)(2,1)S(1)}, bf16[1104,128]{1,0:T(8,128)(2,1)S(1)}) fusion(bf16[9,128]{1,0:T(8,128)(2,1)S(1)} %convert_element_type.38, bf16[64,128]{1,0:T(8,128)(2,1)S(1)} %get-tuple-element.309, bf16[1024,128]{1,0:T(8,128)(2,1)} %bitcast.298, bf16[64,128]{1,0:T(8,128)(2,1)S(1)} %get-tuple-element.311, ...), kind=kLoop, calls=%fused_computation.373 | loop fusion | flops 2260992 | bytes 1161472 | tf_op jit(solution)/shard_map/concatenate | solution.py:58
  3.4 0.5 collective-permute-start.2
  3.9 2.0 %collective-permute-start = (bf16[1104,128]{1,0:T(8,128)(2,1)S(1)}, bf16[1104,128]{1,0:T(8,128)(2,1)S(1)}, u32[]{:S(2)}, u32[]{:S(2)}) collective-permute-start(bf16[1104,128]{1,0:T(8,128)(2,1)S(1)} %get-tuple-element.285), channel_id=1, source_target_pairs={{0,3},{1,0},{2,1},{3,2},{4,7},{5,4},{6,5},{7,6},{8,11},{9,8},{10,9... | collective-permute-start | bytes 847880 | tf_op jit(solution)/shard_map/ppermute | solution.py:65
  5.9 2.2 %collective-permute-start.1 = (bf16[1104,128]{1,0:T(8,128)(2,1)S(1)}, bf16[1104,128]{1,0:T(8,128)(2,1)S(1)}, u32[]{:S(2)}, u32[]{:S(2)}) collective-permute-start(bf16[1104,128]{1,0:T(8,128)(2,1)S(1)} %get-tuple-element.286), channel_id=1, source_target_pairs={{0,2},{1,3},{2,0},{3,1},{4,6},{5,7},{6,4},{7,5},{8,10},{9,11},{10,... | collective-permute-start | bytes 847880 | tf_op jit(solution)/shard_map/ppermute | solution.py:65
  8.3 0.6 mul.324
  9.0 1.5 %collective-permute-done.2 = bf16[1104,128]{1,0:T(8,128)(2,1)S(1)} collective-permute-done((bf16[1104,128]{1,0:T(8,128)(2,1)S(1)}, bf16[1104,128]{1,0:T(8,128)(2,1)S(1)}, u32[]{:S(2)}, u32[]{:S(2)}) %collective-permute-start.2) | collective-permute-done | bytes 282656 | tf_op jit(solution)/shard_map/ppermute | solution.py:65
  10.5 2.5 %collective-permute-done = bf16[1104,128]{1,0:T(8,128)(2,1)S(1)} collective-permute-done((bf16[1104,128]{1,0:T(8,128)(2,1)S(1)}, bf16[1104,128]{1,0:T(8,128)(2,1)S(1)}, u32[]{:S(2)}, u32[]{:S(2)}) %collective-permute-start) | collective-permute-done | bytes 282656 | tf_op jit(solution)/shard_map/ppermute | solution.py:65
  13.0 6.2 %collective-permute-done.1 = bf16[1104,128]{1,0:T(8,128)(2,1)S(1)} collective-permute-done((bf16[1104,128]{1,0:T(8,128)(2,1)S(1)}, bf16[1104,128]{1,0:T(8,128)(2,1)S(1)}, u32[]{:S(2)}, u32[]{:S(2)}) %collective-permute-start.1) | collective-permute-done | bytes 282656 | tf_op jit(solution)/shard_map/ppermute | solution.py:65
  20.0 0.3 maximum_multiply_fusion
  20.3 0.6 conditional.7
  20.4 0.2 fusion.21
  20.9 4.3 %collective-permute-start.3 = (f32[32,512]{1,0:T(8,128)S(1)}, f32[32,512]{1,0:T(8,128)S(1)}, u32[]{:S(2)}, u32[]{:S(2)}) collective-permute-start(f32[32,512]{1,0:T(8,128)S(1)} %get-tuple-element.318), channel_id=1, source_target_pairs={{0,4},{1,5},{2,6},{3,7},{28,24},{29,25},{30,26},{31,27}} | collective-permute-start | bytes 196616 | tf_op jit(solution)/shard_map/ppermute | solution.py:131
  25.3 1.9 %collective-permute-done.3 = f32[32,512]{1,0:T(8,128)S(1)} collective-permute-done((f32[32,512]{1,0:T(8,128)S(1)}, f32[32,512]{1,0:T(8,128)S(1)}, u32[]{:S(2)}, u32[]{:S(2)}) %collective-permute-start.3) | collective-permute-done | bytes 65568 | tf_op jit(solution)/shard_map/ppermute | solution.py:131
  27.1 0.7 conditional.8
  27.2 0.3 fusion.37
  27.5 0.3 fusion.35
  27.8 0.7 collective-permute-start.4
  28.6 0.7 conditional.9
  28.6 0.3 fusion.76
  28.9 0.3 fusion.74
  29.3 0.7 collective-permute-start.5
  30.0 0.7 conditional.10
  30.0 0.3 fusion.115
  30.4 0.3 fusion.113
  30.7 0.7 collective-permute-start.6
  31.4 0.7 conditional.11
  31.4 0.3 fusion.154
  31.8 0.3 fusion.152
  32.1 0.7 collective-permute-start.7
  32.8 0.7 conditional.12
  32.8 0.3 fusion.193
  33.2 0.3 fusion.191
  33.5 0.7 collective-permute-start.8
  34.2 0.7 conditional.13
  34.2 0.3 fusion.232
  34.6 0.3 fusion.230
  34.9 1.3 %collective-permute-start.9 = (f32[32,512]{1,0:T(8,128)S(1)}, f32[32,512]{1,0:T(8,128)S(1)}, u32[]{:S(2)}, u32[]{:S(2)}) collective-permute-start(f32[32,512]{1,0:T(8,128)S(1)} %get-tuple-element.324), channel_id=1, source_target_pairs={{24,28},{25,29},{26,30},{27,31},{4,0},{5,1},{6,2},{7,3}} | collective-permute-start | bytes 196616 | tf_op jit(solution)/shard_map/ppermute | solution.py:131
  36.2 26.9 %collective-permute-done.9 = f32[32,512]{1,0:T(8,128)S(1)} collective-permute-done((f32[32,512]{1,0:T(8,128)S(1)}, f32[32,512]{1,0:T(8,128)S(1)}, u32[]{:S(2)}, u32[]{:S(2)}) %collective-permute-start.9) | collective-permute-done | bytes 65568 | tf_op jit(solution)/shard_map/ppermute | solution.py:131
  63.7 0.3 fusion.271
  64.2 1.6 %collective-permute-start.11 = (f32[2,2,32,128]{3,2,1,0:T(8,128)S(1)}, f32[2,2,32,128]{3,2,1,0:T(8,128)S(1)}, u32[]{:S(2)}, u32[]{:S(2)}) collective-permute-start(f32[2,2,32,128]{3,2,1,0:T(8,128)S(1)} %get-tuple-element.292), channel_id=1, source_target_pairs={{0,2},{1,3},{2,0},{3,1},{4,6},{5,7},{6,4},{7,5},{8,10},{9,11},{10,... | collective-permute-start | bytes 196616 | tf_op jit(solution)/shard_map/ppermute | solution.py:162
  65.7 1.4 %collective-permute-start.10 = (f32[2,2,32,128]{3,2,1,0:T(8,128)S(1)}, f32[2,2,32,128]{3,2,1,0:T(8,128)S(1)}, u32[]{:S(2)}, u32[]{:S(2)}) collective-permute-start(f32[2,2,32,128]{3,2,1,0:T(8,128)S(1)} %get-tuple-element.293), channel_id=1, source_target_pairs={{0,3},{1,0},{2,1},{3,2},{4,7},{5,4},{6,5},{7,6},{8,11},{9,8},{10,9... | collective-permute-start | bytes 196616 | tf_op jit(solution)/shard_map/ppermute | solution.py:162
  67.2 0.7 collective-permute-done.12
  67.8 0.8 %collective-permute-done.11 = f32[2,2,32,128]{3,2,1,0:T(8,128)S(1)} collective-permute-done((f32[2,2,32,128]{3,2,1,0:T(8,128)S(1)}, f32[2,2,32,128]{3,2,1,0:T(8,128)S(1)}, u32[]{:S(2)}, u32[]{:S(2)}) %collective-permute-start.11) | collective-permute-done | bytes 65568 | tf_op jit(solution)/shard_map/ppermute | solution.py:162
  68.6 0.5 collective-permute-done.10
  69.2 0.7 copy.11
  69.9 0.7 copy.10
  (98 shorter events, 2.6 us)
Async XLA Ops:
  0.6 7.5 %copy-start.1 = (s32[8,8]{1,0:T(8,128)S(1)}, s32[8,8]{1,0:T(8,128)}, u32[]{:S(2)}) copy-start(s32[8,8]{1,0:T(8,128)} %param.23) | copy-start | bytes 772
  3.4 7.2 %collective-permute-start.2 = (bf16[1104,128]{1,0:T(8,128)(2,1)S(1)}, bf16[1104,128]{1,0:T(8,128)(2,1)S(1)}, u32[]{:S(2)}, u32[]{:S(2)}) collective-permute-start(bf16[1104,128]{1,0:T(8,128)(2,1)S(1)} %get-tuple-element.284), channel_id=1, source_target_pairs={{0,1},{1,2},{2,3},{3,0},{4,5},{5,6},{6,7},{7,4},{8,9},{9,10},{10,1... | collective-permute-start | bytes 847880 | tf_op jit(solution)/shard_map/ppermute | solution.py:65
  3.9 9.1 %collective-permute-start = (bf16[1104,128]{1,0:T(8,128)(2,1)S(1)}, bf16[1104,128]{1,0:T(8,128)(2,1)S(1)}, u32[]{:S(2)}, u32[]{:S(2)}) collective-permute-start(bf16[1104,128]{1,0:T(8,128)(2,1)S(1)} %get-tuple-element.285), channel_id=1, source_target_pairs={{0,3},{1,0},{2,1},{3,2},{4,7},{5,4},{6,5},{7,6},{8,11},{9,8},{10,9... | collective-permute-start | bytes 847880 | tf_op jit(solution)/shard_map/ppermute | solution.py:65
  5.9 13.3 %collective-permute-start.1 = (bf16[1104,128]{1,0:T(8,128)(2,1)S(1)}, bf16[1104,128]{1,0:T(8,128)(2,1)S(1)}, u32[]{:S(2)}, u32[]{:S(2)}) collective-permute-start(bf16[1104,128]{1,0:T(8,128)(2,1)S(1)} %get-tuple-element.286), channel_id=1, source_target_pairs={{0,2},{1,3},{2,0},{3,1},{4,6},{5,7},{6,4},{7,5},{8,10},{9,11},{10,... | collective-permute-start | bytes 847880 | tf_op jit(solution)/shard_map/ppermute | solution.py:65
  8.3 10.8 %copy-start = (bf16[2,512,128]{2,1,0:T(8,128)(2,1)S(1)}, bf16[2,512,128]{2,1,0:T(8,128)(2,1)}, u32[]{:S(2)}) copy-start(bf16[2,512,128]{2,1,0:T(8,128)(2,1)} %param.22) | copy-start | bytes 786436
  20.9 6.2 %collective-permute-start.3 = (f32[32,512]{1,0:T(8,128)S(1)}, f32[32,512]{1,0:T(8,128)S(1)}, u32[]{:S(2)}, u32[]{:S(2)}) collective-permute-start(f32[32,512]{1,0:T(8,128)S(1)} %get-tuple-element.318), channel_id=1, source_target_pairs={{0,4},{1,5},{2,6},{3,7},{28,24},{29,25},{30,26},{31,27}} | collective-permute-start | bytes 196616 | tf_op jit(solution)/shard_map/ppermute | solution.py:131
  27.8 0.7 collective-permute-start.4
  29.3 0.7 collective-permute-start.5
  30.7 0.7 collective-permute-start.6
  32.1 0.7 collective-permute-start.7
  33.5 0.7 collective-permute-start.8
  34.9 28.2 %collective-permute-start.9 = (f32[32,512]{1,0:T(8,128)S(1)}, f32[32,512]{1,0:T(8,128)S(1)}, u32[]{:S(2)}, u32[]{:S(2)}) collective-permute-start(f32[32,512]{1,0:T(8,128)S(1)} %get-tuple-element.324), channel_id=1, source_target_pairs={{24,28},{25,29},{26,30},{27,31},{4,0},{5,1},{6,2},{7,3}} | collective-permute-start | bytes 196616 | tf_op jit(solution)/shard_map/ppermute | solution.py:131
  64.1 3.8 %collective-permute-start.12 = (f32[2,2,32,128]{3,2,1,0:T(8,128)S(1)}, f32[2,2,32,128]{3,2,1,0:T(8,128)S(1)}, u32[]{:S(2)}, u32[]{:S(2)}) collective-permute-start(f32[2,2,32,128]{3,2,1,0:T(8,128)S(1)} %get-tuple-element.215), channel_id=1, source_target_pairs={{0,1},{1,2},{2,3},{3,0},{4,5},{5,6},{6,7},{7,4},{8,9},{9,10},{10,1... | collective-permute-start | bytes 196616 | tf_op jit(solution)/shard_map/ppermute | solution.py:162
  64.2 4.5 %collective-permute-start.11 = (f32[2,2,32,128]{3,2,1,0:T(8,128)S(1)}, f32[2,2,32,128]{3,2,1,0:T(8,128)S(1)}, u32[]{:S(2)}, u32[]{:S(2)}) collective-permute-start(f32[2,2,32,128]{3,2,1,0:T(8,128)S(1)} %get-tuple-element.292), channel_id=1, source_target_pairs={{0,2},{1,3},{2,0},{3,1},{4,6},{5,7},{6,4},{7,5},{8,10},{9,11},{10,... | collective-permute-start | bytes 196616 | tf_op jit(solution)/shard_map/ppermute | solution.py:162
  65.7 3.4 %collective-permute-start.10 = (f32[2,2,32,128]{3,2,1,0:T(8,128)S(1)}, f32[2,2,32,128]{3,2,1,0:T(8,128)S(1)}, u32[]{:S(2)}, u32[]{:S(2)}) collective-permute-start(f32[2,2,32,128]{3,2,1,0:T(8,128)S(1)} %get-tuple-element.293), channel_id=1, source_target_pairs={{0,3},{1,0},{2,1},{3,2},{4,7},{5,4},{6,5},{7,6},{8,11},{9,8},{10,9... | collective-permute-start | bytes 196616 | tf_op jit(solution)/shard_map/ppermute | solution.py:162

commit v15 on v14

--- a/solution.py
+++ b/solution.py
@@ -49,12 +49,16 @@
     small_pad = -small_rows % 16
     small_pieces = jnp.pad(three_pieces(small).reshape(small_rows, cols), ((0, small_pad), (0, 0)))
     coupling_rows = coupling.reshape(step_count * state_width, cols)
-    seen_parts = observed.reshape(step_count, col_groups, own_rows, cols).transpose(1, 0, 2, 3)
-    seen_parts = seen_parts.reshape(col_groups, step_count * own_rows, cols)
+    seen_parts = [
+        observed[:, d * own_rows : (d + 1) * own_rows, :].reshape(step_count * own_rows, cols)
+        for d in range(col_groups)
+    ]
     chunks = []
     for shift in range(col_groups):
         dest = (col_pos + shift) % col_groups
-        seen_d = lax.dynamic_index_in_dim(seen_parts, dest, 0, keepdims=False)
+        seen_d = seen_parts[0]
+        for d in range(1, col_groups):
+            seen_d = jnp.where(dest == d, seen_parts[d], seen_d)
         chunk = jnp.concatenate([coupling_rows, seen_d, small_pieces], axis=0)
         if shift:
             pairs = [

time: 71 us -> 71.8 us (1.011)
  other arithmetic: 3.52 us -> 5.09 us
  local copies, waits for them, and re-layouts: 3.26 us -> 2.41 us
    select_n x0 -> x2, other arithmetic: none -> 1.57 us  [local(): seen_d = jnp.where(dest == d, seen_parts[d], seen_d)]
    transpose x1 -> x0, local copies, waits for them, and re-layouts: 0.84 us -> none  [local(): observed.reshape(step_count, col_groups, own_rows, cols)]
where the time goes in v15:
time: 71.8 us; the launch traced here: 71.3 us
  waiting for transfers between devices  40.9 us (57%)
  starting transfers between devices  16.8 us (23%)
  other arithmetic  5.09 us (7%)
  matrix products  4.43 us (6%)
  local copies, waits for them, and re-layouts  2.41 us (3%)
  between operations  1.23 us (2%)
    ppermute x7, waiting for transfers between devices, local(): got = lax.ppermute(send, ('tm', 'col'), pairs)  28.8 us
    ppermute x3, waiting for transfers between devices, local(): chunk = lax.ppermute(chunk, ('tm', 'col'), pairs)  10.2 us
    ppermute x7, starting transfers between devices, local(): got = lax.ppermute(send, ('tm', 'col'), pairs)  8.96 us
    ppermute x3, starting transfers between devices, local(): chunk = lax.ppermute(chunk, ('tm', 'col'), pairs)  4.76 us
    dot_general x17, matrix products, split_dot(): lax.dot_general(both, weights, (((1,), (contract,)), ((), ())), preferred...  4.43 us
    ppermute x3, starting transfers between devices, local(): piece = lax.ppermute(piece, ('tm', 'col'), pairs)  3.06 us
    ppermute x3, waiting for transfers between devices, local(): piece = lax.ppermute(piece, ('tm', 'col'), pairs)  1.9 us
    select_n x2, other arithmetic, local(): seen_d = jnp.where(dest == d, seen_parts[d], seen_d)  1.57 us
  transfers between devices with their start and end apart: 13, of which 8 were waited for; matrix products, arithmetic and copies ran while one was open for 1% of the time, Pallas kernels for 0%

profile of v15, /device:TPU:0, one launch (start us, length us, event | category | flops | bytes accessed | tf_op | source)
XLA Modules:
  0.0 71.3 jit_solution(17657294065995917362)
XLA Ops:
  0.7 0.7 reduce-precision_convert_fusion.31
  1.4 0.8 %select_select_fusion.8 = (bf16[2,32,128]{2,1,0:T(8,128)(2,1)S(1)}, bf16[2,32,128]{2,1,0:T(8,128)(2,1)S(1)}) fusion(pred[]{:T(512)S(6)} %eq.154, pred[]{:T(512)S(6)} %eq.150, pred[]{:T(512)S(6)} %eq.144, bf16[2,128,128]{2,1,0:T(8,128)(2,1)} %param.19, pred[]{:T(512)S(6)} %eq.157, pred[]{:T(512)S(6)} %eq.156, pred[]{:T(512)S(6)} %eq.155), kind=kLoop, calls=%fused_computation.442 | loop fusion | flops 49152 | bytes 98310 | tf_op jit(solution)/shard_map/jit(_where)/select_n | solution.py:61
  2.2 0.8 %select_select_fusion.10 = (bf16[2,32,128]{2,1,0:T(8,128)(2,1)S(1)}, bf16[2,32,128]{2,1,0:T(8,128)(2,1)S(1)}) fusion(pred[]{:T(512)S(6)} %eq.153, pred[]{:T(512)S(6)} %eq.152, pred[]{:T(512)S(6)} %eq.151, bf16[2,128,128]{2,1,0:T(8,128)(2,1)} %param.19, pred[]{:T(512)S(6)} %eq.149, pred[]{:T(512)S(6)} %eq.148, pred[]{:T(512)S(6)} %eq.145), kind=kLoop, calls=%fused_computation.444 | loop fusion | flops 49152 | bytes 98310 | tf_op jit(solution)/shard_map/jit(_where)/select_n | solution.py:61
  3.0 1.1 %fusion.273 = (bf16[1104,128]{1,0:T(8,128)(2,1)S(1)}, bf16[1104,128]{1,0:T(8,128)(2,1)S(1)}, bf16[1104,128]{1,0:T(8,128)(2,1)S(1)}) fusion(bf16[9,128]{1,0:T(8,128)(2,1)S(1)} %convert_element_type.38, bf16[64,128]{1,0:T(8,128)(2,1)S(1)} %bitcast.305, bf16[1024,128]{1,0:T(8,128)(2,1)} %bitcast.290, bf16[64,128]{1,0:T(8,128)(2,1)S(1)} %bitcast.307, ...), kind=kLoop, calls=%fused_computation.373 | loop fusion | flops 2260992 | bytes 1161472 | tf_op jit(solution)/shard_map/concatenate | solution.py:62
  4.1 0.5 collective-permute-start.2
  4.6 2.0 %collective-permute-start = (bf16[1104,128]{1,0:T(8,128)(2,1)S(1)}, bf16[1104,128]{1,0:T(8,128)(2,1)S(1)}, u32[]{:S(2)}, u32[]{:S(2)}) collective-permute-start(bf16[1104,128]{1,0:T(8,128)(2,1)S(1)} %get-tuple-element.285), channel_id=1, source_target_pairs={{0,3},{1,0},{2,1},{3,2},{4,7},{5,4},{6,5},{7,6},{8,11},{9,8},{10,9... | collective-permute-start | bytes 847880 | tf_op jit(solution)/shard_map/ppermute | solution.py:69
  6.6 2.2 %collective-permute-start.1 = (bf16[1104,128]{1,0:T(8,128)(2,1)S(1)}, bf16[1104,128]{1,0:T(8,128)(2,1)S(1)}, u32[]{:S(2)}, u32[]{:S(2)}) collective-permute-start(bf16[1104,128]{1,0:T(8,128)(2,1)S(1)} %get-tuple-element.286), channel_id=1, source_target_pairs={{0,2},{1,3},{2,0},{3,1},{4,6},{5,7},{6,4},{7,5},{8,10},{9,11},{10,... | collective-permute-start | bytes 847880 | tf_op jit(solution)/shard_map/ppermute | solution.py:69
  9.1 0.6 mul.324
  9.7 1.5 %collective-permute-done.2 = bf16[1104,128]{1,0:T(8,128)(2,1)S(1)} collective-permute-done((bf16[1104,128]{1,0:T(8,128)(2,1)S(1)}, bf16[1104,128]{1,0:T(8,128)(2,1)S(1)}, u32[]{:S(2)}, u32[]{:S(2)}) %collective-permute-start.2) | collective-permute-done | bytes 282656 | tf_op jit(solution)/shard_map/ppermute | solution.py:69
  11.2 2.5 %collective-permute-done = bf16[1104,128]{1,0:T(8,128)(2,1)S(1)} collective-permute-done((bf16[1104,128]{1,0:T(8,128)(2,1)S(1)}, bf16[1104,128]{1,0:T(8,128)(2,1)S(1)}, u32[]{:S(2)}, u32[]{:S(2)}) %collective-permute-start) | collective-permute-done | bytes 282656 | tf_op jit(solution)/shard_map/ppermute | solution.py:69
  13.7 6.2 %collective-permute-done.1 = bf16[1104,128]{1,0:T(8,128)(2,1)S(1)} collective-permute-done((bf16[1104,128]{1,0:T(8,128)(2,1)S(1)}, bf16[1104,128]{1,0:T(8,128)(2,1)S(1)}, u32[]{:S(2)}, u32[]{:S(2)}) %collective-permute-start.1) | collective-permute-done | bytes 282656 | tf_op jit(solution)/shard_map/ppermute | solution.py:69
  20.7 0.3 maximum_multiply_fusion
  21.0 0.6 conditional.7
  21.6 4.3 %collective-permute-start.3 = (f32[32,512]{1,0:T(8,128)S(1)}, f32[32,512]{1,0:T(8,128)S(1)}, u32[]{:S(2)}, u32[]{:S(2)}) collective-permute-start(f32[32,512]{1,0:T(8,128)S(1)} %get-tuple-element.318), channel_id=1, source_target_pairs={{0,4},{1,5},{2,6},{3,7},{28,24},{29,25},{30,26},{31,27}} | collective-permute-start | bytes 196616 | tf_op jit(solution)/shard_map/ppermute | solution.py:135
  26.0 1.9 %collective-permute-done.3 = f32[32,512]{1,0:T(8,128)S(1)} collective-permute-done((f32[32,512]{1,0:T(8,128)S(1)}, f32[32,512]{1,0:T(8,128)S(1)}, u32[]{:S(2)}, u32[]{:S(2)}) %collective-permute-start.3) | collective-permute-done | bytes 65568 | tf_op jit(solution)/shard_map/ppermute | solution.py:135
  27.9 0.7 conditional.8
  27.9 0.3 fusion.37
  28.3 0.3 fusion.35
  28.6 0.7 collective-permute-start.4
  29.3 0.7 conditional.9
  29.3 0.3 fusion.76
  29.7 0.3 fusion.74
  30.0 0.7 collective-permute-start.5
  30.7 0.7 conditional.10
  30.8 0.3 fusion.115
  31.1 0.3 fusion.113
  31.4 0.7 collective-permute-start.6
  32.1 0.7 conditional.11
  32.2 0.3 fusion.154
  32.5 0.3 fusion.152
  32.8 0.7 collective-permute-start.7
  33.5 0.7 conditional.12
  33.6 0.3 fusion.193
  33.9 0.3 fusion.191
  34.2 0.7 collective-permute-start.8
  34.9 0.7 conditional.13
  35.0 0.3 fusion.232
  35.3 0.3 fusion.230
  35.6 1.3 %collective-permute-start.9 = (f32[32,512]{1,0:T(8,128)S(1)}, f32[32,512]{1,0:T(8,128)S(1)}, u32[]{:S(2)}, u32[]{:S(2)}) collective-permute-start(f32[32,512]{1,0:T(8,128)S(1)} %get-tuple-element.324), channel_id=1, source_target_pairs={{24,28},{25,29},{26,30},{27,31},{4,0},{5,1},{6,2},{7,3}} | collective-permute-start | bytes 196616 | tf_op jit(solution)/shard_map/ppermute | solution.py:135
  36.9 26.9 %collective-permute-done.9 = f32[32,512]{1,0:T(8,128)S(1)} collective-permute-done((f32[32,512]{1,0:T(8,128)S(1)}, f32[32,512]{1,0:T(8,128)S(1)}, u32[]{:S(2)}, u32[]{:S(2)}) %collective-permute-start.9) | collective-permute-done | bytes 65568 | tf_op jit(solution)/shard_map/ppermute | solution.py:135
  64.4 0.3 fusion.271
  64.9 1.6 %collective-permute-start.11 = (f32[2,2,32,128]{3,2,1,0:T(8,128)S(1)}, f32[2,2,32,128]{3,2,1,0:T(8,128)S(1)}, u32[]{:S(2)}, u32[]{:S(2)}) collective-permute-start(f32[2,2,32,128]{3,2,1,0:T(8,128)S(1)} %get-tuple-element.292), channel_id=1, source_target_pairs={{0,2},{1,3},{2,0},{3,1},{4,6},{5,7},{6,4},{7,5},{8,10},{9,11},{10,... | collective-permute-start | bytes 196616 | tf_op jit(solution)/shard_map/ppermute | solution.py:166
  66.5 1.4 %collective-permute-start.10 = (f32[2,2,32,128]{3,2,1,0:T(8,128)S(1)}, f32[2,2,32,128]{3,2,1,0:T(8,128)S(1)}, u32[]{:S(2)}, u32[]{:S(2)}) collective-permute-start(f32[2,2,32,128]{3,2,1,0:T(8,128)S(1)} %get-tuple-element.293), channel_id=1, source_target_pairs={{0,3},{1,0},{2,1},{3,2},{4,7},{5,4},{6,5},{7,6},{8,11},{9,8},{10,9... | collective-permute-start | bytes 196616 | tf_op jit(solution)/shard_map/ppermute | solution.py:166
  67.9 0.7 collective-permute-done.12
  68.6 0.8 %collective-permute-done.11 = f32[2,2,32,128]{3,2,1,0:T(8,128)S(1)} collective-permute-done((f32[2,2,32,128]{3,2,1,0:T(8,128)S(1)}, f32[2,2,32,128]{3,2,1,0:T(8,128)S(1)}, u32[]{:S(2)}, u32[]{:S(2)}) %collective-permute-start.11) | collective-permute-done | bytes 65568 | tf_op jit(solution)/shard_map/ppermute | solution.py:166
  69.3 0.5 collective-permute-done.10
  69.9 0.7 copy.8
  70.6 0.7 copy.7
  (98 shorter events, 2.8 us)
Async XLA Ops:
  0.6 8.2 %copy-start.1 = (s32[8,8]{1,0:T(8,128)S(1)}, s32[8,8]{1,0:T(8,128)}, u32[]{:S(2)}) copy-start(s32[8,8]{1,0:T(8,128)} %param.23) | copy-start | bytes 772
  4.1 7.2 %collective-permute-start.2 = (bf16[1104,128]{1,0:T(8,128)(2,1)S(1)}, bf16[1104,128]{1,0:T(8,128)(2,1)S(1)}, u32[]{:S(2)}, u32[]{:S(2)}) collective-permute-start(bf16[1104,128]{1,0:T(8,128)(2,1)S(1)} %get-tuple-element.284), channel_id=1, source_target_pairs={{0,1},{1,2},{2,3},{3,0},{4,5},{5,6},{6,7},{7,4},{8,9},{9,10},{10,1... | collective-permute-start | bytes 847880 | tf_op jit(solution)/shard_map/ppermute | solution.py:69
  4.6 9.1 %collective-permute-start = (bf16[1104,128]{1,0:T(8,128)(2,1)S(1)}, bf16[1104,128]{1,0:T(8,128)(2,1)S(1)}, u32[]{:S(2)}, u32[]{:S(2)}) collective-permute-start(bf16[1104,128]{1,0:T(8,128)(2,1)S(1)} %get-tuple-element.285), channel_id=1, source_target_pairs={{0,3},{1,0},{2,1},{3,2},{4,7},{5,4},{6,5},{7,6},{8,11},{9,8},{10,9... | collective-permute-start | bytes 847880 | tf_op jit(solution)/shard_map/ppermute | solution.py:69
  6.6 13.3 %collective-permute-start.1 = (bf16[1104,128]{1,0:T(8,128)(2,1)S(1)}, bf16[1104,128]{1,0:T(8,128)(2,1)S(1)}, u32[]{:S(2)}, u32[]{:S(2)}) collective-permute-start(bf16[1104,128]{1,0:T(8,128)(2,1)S(1)} %get-tuple-element.286), channel_id=1, source_target_pairs={{0,2},{1,3},{2,0},{3,1},{4,6},{5,7},{6,4},{7,5},{8,10},{9,11},{10,... | collective-permute-start | bytes 847880 | tf_op jit(solution)/shard_map/ppermute | solution.py:69
  9.1 10.8 %copy-start = (bf16[2,512,128]{2,1,0:T(8,128)(2,1)S(1)}, bf16[2,512,128]{2,1,0:T(8,128)(2,1)}, u32[]{:S(2)}) copy-start(bf16[2,512,128]{2,1,0:T(8,128)(2,1)} %param.22) | copy-start | bytes 786436
  21.6 6.2 %collective-permute-start.3 = (f32[32,512]{1,0:T(8,128)S(1)}, f32[32,512]{1,0:T(8,128)S(1)}, u32[]{:S(2)}, u32[]{:S(2)}) collective-permute-start(f32[32,512]{1,0:T(8,128)S(1)} %get-tuple-element.318), channel_id=1, source_target_pairs={{0,4},{1,5},{2,6},{3,7},{28,24},{29,25},{30,26},{31,27}} | collective-permute-start | bytes 196616 | tf_op jit(solution)/shard_map/ppermute | solution.py:135
  28.6 0.7 collective-permute-start.4
  30.0 0.7 collective-permute-start.5
  31.4 0.7 collective-permute-start.6
  32.8 0.7 collective-permute-start.7
  34.2 0.7 collective-permute-start.8
  35.6 28.2 %collective-permute-start.9 = (f32[32,512]{1,0:T(8,128)S(1)}, f32[32,512]{1,0:T(8,128)S(1)}, u32[]{:S(2)}, u32[]{:S(2)}) collective-permute-start(f32[32,512]{1,0:T(8,128)S(1)} %get-tuple-element.324), channel_id=1, source_target_pairs={{24,28},{25,29},{26,30},{27,31},{4,0},{5,1},{6,2},{7,3}} | collective-permute-start | bytes 196616 | tf_op jit(solution)/shard_map/ppermute | solution.py:135
  64.8 3.8 %collective-permute-start.12 = (f32[2,2,32,128]{3,2,1,0:T(8,128)S(1)}, f32[2,2,32,128]{3,2,1,0:T(8,128)S(1)}, u32[]{:S(2)}, u32[]{:S(2)}) collective-permute-start(f32[2,2,32,128]{3,2,1,0:T(8,128)S(1)} %get-tuple-element.215), channel_id=1, source_target_pairs={{0,1},{1,2},{2,3},{3,0},{4,5},{5,6},{6,7},{7,4},{8,9},{9,10},{10,1... | collective-permute-start | bytes 196616 | tf_op jit(solution)/shard_map/ppermute | solution.py:166
  64.9 4.4 %collective-permute-start.11 = (f32[2,2,32,128]{3,2,1,0:T(8,128)S(1)}, f32[2,2,32,128]{3,2,1,0:T(8,128)S(1)}, u32[]{:S(2)}, u32[]{:S(2)}) collective-permute-start(f32[2,2,32,128]{3,2,1,0:T(8,128)S(1)} %get-tuple-element.292), channel_id=1, source_target_pairs={{0,2},{1,3},{2,0},{3,1},{4,6},{5,7},{6,4},{7,5},{8,10},{9,11},{10,... | collective-permute-start | bytes 196616 | tf_op jit(solution)/shard_map/ppermute | solution.py:166
  66.5 3.4 %collective-permute-start.10 = (f32[2,2,32,128]{3,2,1,0:T(8,128)S(1)}, f32[2,2,32,128]{3,2,1,0:T(8,128)S(1)}, u32[]{:S(2)}, u32[]{:S(2)}) collective-permute-start(f32[2,2,32,128]{3,2,1,0:T(8,128)S(1)} %get-tuple-element.293), channel_id=1, source_target_pairs={{0,3},{1,0},{2,1},{3,2},{4,7},{5,4},{6,5},{7,6},{8,11},{9,8},{10,9... | collective-permute-start | bytes 196616 | tf_op jit(solution)/shard_map/ppermute | solution.py:166

commit v16 on v14

--- a/solution.py
+++ b/solution.py
@@ -51,46 +51,57 @@
     coupling_rows = coupling.reshape(step_count * state_width, cols)
     seen_parts = observed.reshape(step_count, col_groups, own_rows, cols).transpose(1, 0, 2, 3)
     seen_parts = seen_parts.reshape(col_groups, step_count * own_rows, cols)
-    chunks = []
+    n_coupling = step_count * state_width
+    n_seen = step_count * own_rows
+    lead = col_groups // 2
+    couplings, extras = [], []
     for shift in range(col_groups):
         dest = (col_pos + shift) % col_groups
         seen_d = lax.dynamic_index_in_dim(seen_parts, dest, 0, keepdims=False)
-        chunk = jnp.concatenate([coupling_rows, seen_d, small_pieces], axis=0)
-        if shift:
-            pairs = [
-                (t * col_groups + c, t * col_groups + (c + shift) % col_groups)
-                for t in range(time_groups)
-                for c in range(col_groups)
-            ]
+        extra = jnp.concatenate([seen_d, small_pieces], axis=0)
+        pairs = [
+            (t * col_groups + c, t * col_groups + (c + shift) % col_groups)
+            for t in range(time_groups)
+            for c in range(col_groups)
+        ]
+        if shift == 0:
+            couplings.append(coupling_rows)
+            extras.append(extra)
+        elif shift == lead:
+            couplings.append(lax.ppermute(coupling_rows, ("tm", "col"), pairs))
+            extras.append(lax.ppermute(extra, ("tm", "col"), pairs))
+        else:
+            chunk = jnp.concatenate([coupling_rows, extra], axis=0)
             chunk = lax.ppermute(chunk, ("tm", "col"), pairs)
-        chunks.append(chunk)
-    def from_source(j):
+            couplings.append(chunk[:n_coupling])
+            extras.append(chunk[n_coupling:])
+
+    def from_source(options, j):
         which = (col_pos - j) % col_groups
-        out = chunks[0]
+        out = options[0]
         for shift in range(1, col_groups):
-            out = jnp.where(which == shift, chunks[shift], out)
+            out = jnp.where(which == shift, options[shift], out)
         return out
 
-    sourced = [from_source(j) for j in range(col_groups)]
-    n_coupling = step_count * state_width
-    n_seen = step_count * own_rows
+    sourced_c = [from_source(couplings, j) for j in range(col_groups)]
+    sourced_x = [from_source(extras, j) for j in range(col_groups)]
     mask = jnp.broadcast_to(
         pattern.astype(jnp.bfloat16)[:, None, :, None],
         (block_count, block_size, block_count, block_size),
     ).reshape(state_width, state_width)
     weights = jnp.concatenate(
-        [part[:n_coupling].reshape(step_count, state_width, cols) for part in sourced], axis=2
+        [part.reshape(step_count, state_width, cols) for part in sourced_c], axis=2
     ) * mask[None]
     seen = jnp.concatenate(
-        [part[n_coupling : n_coupling + n_seen].reshape(step_count, own_rows, cols) for part in sourced],
+        [part[:n_seen].reshape(step_count, own_rows, cols) for part in sourced_x],
         axis=2,
     )
     small = jnp.concatenate(
         [
-            part[n_coupling + n_seen : n_coupling + n_seen + small_rows]
+            part[n_seen : n_seen + small_rows]
             .astype(jnp.float32)
             .reshape(3, step_count + 1, cols)
-            for part in sourced
+            for part in sourced_x
         ],
         axis=2,
     )

time: 71 us -> 70.3 us (level)
  starting transfers between devices: 16.8 us -> 16 us
    ppermute x3 -> x2, waiting for transfers between devices: 10.2 us -> 1.33 us  [local(): chunk = lax.ppermute(chunk, ('tm', 'col'), pairs)]
    ppermute x0 -> x2, waiting for transfers between devices: none -> 8.84 us  [the longest x1 4.84 us: local(): extras.append(lax.ppermute(extra, ('tm', 'col'), pairs))]
    ppermute x3 -> x2, starting transfers between devices: 4.76 us -> 2.46 us  [local(): chunk = lax.ppermute(chunk, ('tm', 'col'), pairs)]
    ppermute x0 -> x2, starting transfers between devices: none -> 2.03 us  [the longest x1 1.07 us: local(): extras.append(lax.ppermute(extra, ('tm', 'col'), pairs))]
    ppermute x7, starting transfers between devices: 8.95 us -> 8.14 us  [local(): got = lax.ppermute(send, ('tm', 'col'), pairs)]
  transfers between devices with their start and end apart: 13 -> 14, of which waited for: 8 -> 8; matrix products, arithmetic and copies ran while one was open for 1% -> 1% of each run, Pallas kernels for 0% -> 0%
where the time goes in v16:
time: 70.3 us; the launch traced here: 70 us
  waiting for transfers between devices  41.3 us (59%)
  starting transfers between devices  16 us (23%)
  matrix products  4.43 us (6%)
  other arithmetic  3.34 us (5%)
  local copies, waits for them, and re-layouts  3.2 us (5%)
  between operations  1.23 us (2%)
    ppermute x7, waiting for transfers between devices, local(): got = lax.ppermute(send, ('tm', 'col'), pairs)  29.2 us
    ppermute x7, starting transfers between devices, local(): got = lax.ppermute(send, ('tm', 'col'), pairs)  8.14 us
    ppermute x1, waiting for transfers between devices, local(): extras.append(lax.ppermute(extra, ('tm', 'col'), pairs))  4.84 us
    dot_general x17, matrix products, split_dot(): lax.dot_general(both, weights, (((1,), (contract,)), ((), ())), preferred...  4.43 us
    ppermute x1, waiting for transfers between devices, local(): couplings.append(lax.ppermute(coupling_rows, ('tm', 'col'), pairs))  4 us
    ppermute x3, starting transfers between devices, local(): piece = lax.ppermute(piece, ('tm', 'col'), pairs)  3.42 us
    ppermute x2, starting transfers between devices, local(): chunk = lax.ppermute(chunk, ('tm', 'col'), pairs)  2.46 us
    ppermute x3, waiting for transfers between devices, local(): piece = lax.ppermute(piece, ('tm', 'col'), pairs)  1.9 us
  transfers between devices with their start and end apart: 14, of which 8 were waited for; matrix products, arithmetic and copies ran while one was open for 1% of the time, Pallas kernels for 0%

profile of v16, /device:TPU:0, one launch (start us, length us, event | category | flops | bytes accessed | tf_op | source)
XLA Modules:
  0.0 70.0 jit_solution(4144634077154990308)
XLA Ops:
  0.7 0.7 %reduce-precision_convert_fusion.31 = (bf16[1,3,128]{2,1,0:T(4,128)(2,1)S(1)}, bf16[1,3,128]{2,1,0:T(4,128)(2,1)S(1)}, bf16[1,3,128]{2,1,0:T(4,128)(2,1)S(1)}) fusion(f32[1,1,128]{2,1,0:T(1,128)} %bitcast.353, f32[1,2,128]{2,1,0:T(2,128)} %bitcast.352), kind=kLoop, calls=%fused_computation.456 | loop fusion | flops 3072 | bytes 3840 | tf_op jit(solution)/shard_map/convert.67
  1.5 0.8 %copy.9 = bf16[4,2,32,128]{3,2,1,0:T(8,128)(2,1)S(1)} copy(bf16[4,2,32,128]{3,2,0,1:T(8,128)(2,1)} %bitcast.319) | data formatting | bytes 131072 | tf_op jit(solution)/shard_map/transpose | solution.py:52
  2.4 1.0 %pad_maximum_fusion.1 = (bf16[1104,128]{1,0:T(8,128)(2,1)S(1)}, bf16[1104,128]{1,0:T(8,128)(2,1)S(1)}) fusion(bf16[16,128]{1,0:T(8,128)(2,1)S(1)} %pad.5, bf16[64,128]{1,0:T(8,128)(2,1)S(1)} %get-tuple-element.313, bf16[1024,128]{1,0:T(8,128)(2,1)} %bitcast.302, bf16[64,128]{1,0:T(8,128)(2,1)S(1)} %get-tuple-element.311), kind=kLoop, calls=%fused_computation.366 | loop fusion | flops 1413120 | bytes 864256 | tf_op jit(solution)/shard_map/concatenate | solution.py:74
  3.4 2.5 %collective-permute-start = (bf16[1104,128]{1,0:T(8,128)(2,1)S(1)}, bf16[1104,128]{1,0:T(8,128)(2,1)S(1)}, u32[]{:S(2)}, u32[]{:S(2)}) collective-permute-start(bf16[1104,128]{1,0:T(8,128)(2,1)S(1)} %get-tuple-element.287), channel_id=1, source_target_pairs={{0,3},{1,0},{2,1},{3,2},{4,7},{5,4},{6,5},{7,6},{8,11},{9,8},{10,9... | collective-permute-start | bytes 847880 | tf_op jit(solution)/shard_map/ppermute | solution.py:75
  5.8 1.1 %collective-permute-start.1 = (bf16[80,128]{1,0:T(8,128)(2,1)S(1)}, bf16[80,128]{1,0:T(8,128)(2,1)S(1)}, u32[]{:S(2)}, u32[]{:S(2)}) collective-permute-start(bf16[80,128]{1,0:T(8,128)(2,1)S(1)} %pad_maximum_fusion.5), channel_id=1, source_target_pairs={{0,2},{1,3},{2,0},{3,1},{4,6},{5,7},{6,4},{7,5},{8,10},{9,11},{10,... | collective-permute-start | bytes 61448 | tf_op jit(solution)/shard_map/ppermute | solution.py:72
  6.9 1.0 %collective-permute-start.3 = (bf16[1024,128]{1,0:T(8,128)(2,1)S(1)}, bf16[1024,128]{1,0:T(8,128)(2,1)S(1)}, u32[]{:S(2)}, u32[]{:S(2)}) collective-permute-start(bf16[1024,128]{1,0:T(8,128)(2,1)S(1)} %bitcast.303), channel_id=1, source_target_pairs={{0,2},{1,3},{2,0},{3,1},{4,6},{5,7},{6,4},{7,5},{8,10},{9,11},{10,... | collective-permute-start | bytes 786440 | tf_op jit(solution)/shard_map/ppermute | solution.py:71
  8.1 0.6 mul.324
  8.7 4.8 %collective-permute-done.1 = bf16[80,128]{1,0:T(8,128)(2,1)S(1)} collective-permute-done((bf16[80,128]{1,0:T(8,128)(2,1)S(1)}, bf16[80,128]{1,0:T(8,128)(2,1)S(1)}, u32[]{:S(2)}, u32[]{:S(2)}) %collective-permute-start.1) | collective-permute-done | bytes 20512 | tf_op jit(solution)/shard_map/ppermute | solution.py:72
  13.6 1.3 %collective-permute-done.2 = bf16[1104,128]{1,0:T(8,128)(2,1)S(1)} collective-permute-done((bf16[1104,128]{1,0:T(8,128)(2,1)S(1)}, bf16[1104,128]{1,0:T(8,128)(2,1)S(1)}, u32[]{:S(2)}, u32[]{:S(2)}) %collective-permute-start.2) | collective-permute-done | bytes 282656 | tf_op jit(solution)/shard_map/ppermute | solution.py:75
  15.2 4.0 %collective-permute-done.3 = bf16[1024,128]{1,0:T(8,128)(2,1)S(1)} collective-permute-done((bf16[1024,128]{1,0:T(8,128)(2,1)S(1)}, bf16[1024,128]{1,0:T(8,128)(2,1)S(1)}, u32[]{:S(2)}, u32[]{:S(2)}) %collective-permute-start.3) | collective-permute-done | bytes 262176 | tf_op jit(solution)/shard_map/ppermute | solution.py:71
  19.4 0.3 maximum_multiply_fusion
  19.7 0.6 conditional.7
  19.8 0.2 fusion.21
  20.3 3.5 %collective-permute-start.4 = (f32[32,512]{1,0:T(8,128)S(1)}, f32[32,512]{1,0:T(8,128)S(1)}, u32[]{:S(2)}, u32[]{:S(2)}) collective-permute-start(f32[32,512]{1,0:T(8,128)S(1)} %get-tuple-element.320), channel_id=1, source_target_pairs={{0,4},{1,5},{2,6},{3,7},{28,24},{29,25},{30,26},{31,27}} | collective-permute-start | bytes 196616 | tf_op jit(solution)/shard_map/ppermute | solution.py:142
  23.9 2.2 %collective-permute-done.4 = f32[32,512]{1,0:T(8,128)S(1)} collective-permute-done((f32[32,512]{1,0:T(8,128)S(1)}, f32[32,512]{1,0:T(8,128)S(1)}, u32[]{:S(2)}, u32[]{:S(2)}) %collective-permute-start.4) | collective-permute-done | bytes 65568 | tf_op jit(solution)/shard_map/ppermute | solution.py:142
  26.1 0.7 conditional.8
  26.1 0.3 fusion.37
  26.5 0.3 fusion.35
  26.8 0.7 collective-permute-start.5
  27.5 0.7 conditional.9
  27.6 0.3 fusion.76
  27.9 0.3 fusion.74
  28.2 0.7 collective-permute-start.6
  28.9 0.7 conditional.10
  29.0 0.3 fusion.115
  29.3 0.3 fusion.113
  29.6 0.7 collective-permute-start.7
  30.3 0.7 conditional.11
  30.4 0.3 fusion.154
  30.7 0.3 fusion.152
  31.0 0.7 collective-permute-start.8
  31.7 0.7 conditional.12
  31.8 0.3 fusion.193
  32.1 0.3 fusion.191
  32.4 0.7 collective-permute-start.9
  33.1 0.7 conditional.13
  33.2 0.3 fusion.232
  33.5 0.3 fusion.230
  33.8 1.3 %collective-permute-start.10 = (f32[32,512]{1,0:T(8,128)S(1)}, f32[32,512]{1,0:T(8,128)S(1)}, u32[]{:S(2)}, u32[]{:S(2)}) collective-permute-start(f32[32,512]{1,0:T(8,128)S(1)} %get-tuple-element.326), channel_id=1, source_target_pairs={{24,28},{25,29},{26,30},{27,31},{4,0},{5,1},{6,2},{7,3}} | collective-permute-start | bytes 196616 | tf_op jit(solution)/shard_map/ppermute | solution.py:142
  35.2 27.0 %collective-permute-done.10 = f32[32,512]{1,0:T(8,128)S(1)} collective-permute-done((f32[32,512]{1,0:T(8,128)S(1)}, f32[32,512]{1,0:T(8,128)S(1)}, u32[]{:S(2)}, u32[]{:S(2)}) %collective-permute-start.10) | collective-permute-done | bytes 65568 | tf_op jit(solution)/shard_map/ppermute | solution.py:142
  62.8 0.3 fusion.270
  63.3 1.9 %collective-permute-start.12 = (f32[2,2,32,128]{3,2,1,0:T(8,128)S(1)}, f32[2,2,32,128]{3,2,1,0:T(8,128)S(1)}, u32[]{:S(2)}, u32[]{:S(2)}) collective-permute-start(f32[2,2,32,128]{3,2,1,0:T(8,128)S(1)} %get-tuple-element.294), channel_id=1, source_target_pairs={{0,2},{1,3},{2,0},{3,1},{4,6},{5,7},{6,4},{7,5},{8,10},{9,11},{10,... | collective-permute-start | bytes 196616 | tf_op jit(solution)/shard_map/ppermute | solution.py:173
  65.2 1.4 %collective-permute-start.11 = (f32[2,2,32,128]{3,2,1,0:T(8,128)S(1)}, f32[2,2,32,128]{3,2,1,0:T(8,128)S(1)}, u32[]{:S(2)}, u32[]{:S(2)}) collective-permute-start(f32[2,2,32,128]{3,2,1,0:T(8,128)S(1)} %get-tuple-element.295), channel_id=1, source_target_pairs={{0,3},{1,0},{2,1},{3,2},{4,7},{5,4},{6,5},{7,6},{8,11},{9,8},{10,9... | collective-permute-start | bytes 196616 | tf_op jit(solution)/shard_map/ppermute | solution.py:173
  66.6 0.3 collective-permute-done.13
  66.9 0.7 %collective-permute-done.12 = f32[2,2,32,128]{3,2,1,0:T(8,128)S(1)} collective-permute-done((f32[2,2,32,128]{3,2,1,0:T(8,128)S(1)}, f32[2,2,32,128]{3,2,1,0:T(8,128)S(1)}, u32[]{:S(2)}, u32[]{:S(2)}) %collective-permute-start.12) | collective-permute-done | bytes 65568 | tf_op jit(solution)/shard_map/ppermute | solution.py:173
  67.7 0.9 %collective-permute-done.11 = f32[2,2,32,128]{3,2,1,0:T(8,128)S(1)} collective-permute-done((f32[2,2,32,128]{3,2,1,0:T(8,128)S(1)}, f32[2,2,32,128]{3,2,1,0:T(8,128)S(1)}, u32[]{:S(2)}, u32[]{:S(2)}) %collective-permute-start.11) | collective-permute-done | bytes 65568 | tf_op jit(solution)/shard_map/ppermute | solution.py:173
  68.6 0.7 copy.11
  69.3 0.7 copy.10
  (100 shorter events, 2.3 us)
Async XLA Ops:
  0.6 6.3 %copy-start = (bf16[2,512,128]{2,1,0:T(8,128)(2,1)S(1)}, bf16[2,512,128]{2,1,0:T(8,128)(2,1)}, u32[]{:S(2)}) copy-start(bf16[2,512,128]{2,1,0:T(8,128)(2,1)} %param.22) | copy-start | bytes 786436
  0.6 7.2 %copy-start.1 = (s32[8,8]{1,0:T(8,128)S(1)}, s32[8,8]{1,0:T(8,128)}, u32[]{:S(2)}) copy-start(s32[8,8]{1,0:T(8,128)} %param.23) | copy-start | bytes 772
  3.4 10.2 %collective-permute-start = (bf16[1104,128]{1,0:T(8,128)(2,1)S(1)}, bf16[1104,128]{1,0:T(8,128)(2,1)S(1)}, u32[]{:S(2)}, u32[]{:S(2)}) collective-permute-start(bf16[1104,128]{1,0:T(8,128)(2,1)S(1)} %get-tuple-element.287), channel_id=1, source_target_pairs={{0,3},{1,0},{2,1},{3,2},{4,7},{5,4},{6,5},{7,6},{8,11},{9,8},{10,9... | collective-permute-start | bytes 847880 | tf_op jit(solution)/shard_map/ppermute | solution.py:75
  5.8 9.0 %collective-permute-start.2 = (bf16[1104,128]{1,0:T(8,128)(2,1)S(1)}, bf16[1104,128]{1,0:T(8,128)(2,1)S(1)}, u32[]{:S(2)}, u32[]{:S(2)}) collective-permute-start(bf16[1104,128]{1,0:T(8,128)(2,1)S(1)} %get-tuple-element.288), channel_id=1, source_target_pairs={{0,1},{1,2},{2,3},{3,0},{4,5},{5,6},{6,7},{7,4},{8,9},{9,10},{10,1... | collective-permute-start | bytes 847880 | tf_op jit(solution)/shard_map/ppermute | solution.py:75
  5.8 7.7 %collective-permute-start.1 = (bf16[80,128]{1,0:T(8,128)(2,1)S(1)}, bf16[80,128]{1,0:T(8,128)(2,1)S(1)}, u32[]{:S(2)}, u32[]{:S(2)}) collective-permute-start(bf16[80,128]{1,0:T(8,128)(2,1)S(1)} %pad_maximum_fusion.5), channel_id=1, source_target_pairs={{0,2},{1,3},{2,0},{3,1},{4,6},{5,7},{6,4},{7,5},{8,10},{9,11},{10,... | collective-permute-start | bytes 61448 | tf_op jit(solution)/shard_map/ppermute | solution.py:72
  6.9 12.2 %collective-permute-start.3 = (bf16[1024,128]{1,0:T(8,128)(2,1)S(1)}, bf16[1024,128]{1,0:T(8,128)(2,1)S(1)}, u32[]{:S(2)}, u32[]{:S(2)}) collective-permute-start(bf16[1024,128]{1,0:T(8,128)(2,1)S(1)} %bitcast.303), channel_id=1, source_target_pairs={{0,2},{1,3},{2,0},{3,1},{4,6},{5,7},{6,4},{7,5},{8,10},{9,11},{10,... | collective-permute-start | bytes 786440 | tf_op jit(solution)/shard_map/ppermute | solution.py:71
  20.3 5.7 %collective-permute-start.4 = (f32[32,512]{1,0:T(8,128)S(1)}, f32[32,512]{1,0:T(8,128)S(1)}, u32[]{:S(2)}, u32[]{:S(2)}) collective-permute-start(f32[32,512]{1,0:T(8,128)S(1)} %get-tuple-element.320), channel_id=1, source_target_pairs={{0,4},{1,5},{2,6},{3,7},{28,24},{29,25},{30,26},{31,27}} | collective-permute-start | bytes 196616 | tf_op jit(solution)/shard_map/ppermute | solution.py:142
  26.8 0.7 collective-permute-start.5
  28.2 0.7 collective-permute-start.6
  29.6 0.7 collective-permute-start.7
  31.0 0.7 collective-permute-start.8
  32.4 0.7 collective-permute-start.9
  33.8 28.4 %collective-permute-start.10 = (f32[32,512]{1,0:T(8,128)S(1)}, f32[32,512]{1,0:T(8,128)S(1)}, u32[]{:S(2)}, u32[]{:S(2)}) collective-permute-start(f32[32,512]{1,0:T(8,128)S(1)} %get-tuple-element.326), channel_id=1, source_target_pairs={{24,28},{25,29},{26,30},{27,31},{4,0},{5,1},{6,2},{7,3}} | collective-permute-start | bytes 196616 | tf_op jit(solution)/shard_map/ppermute | solution.py:142
  63.2 3.8 %collective-permute-start.13 = (f32[2,2,32,128]{3,2,1,0:T(8,128)S(1)}, f32[2,2,32,128]{3,2,1,0:T(8,128)S(1)}, u32[]{:S(2)}, u32[]{:S(2)}) collective-permute-start(f32[2,2,32,128]{3,2,1,0:T(8,128)S(1)} %get-tuple-element.215), channel_id=1, source_target_pairs={{0,1},{1,2},{2,3},{3,0},{4,5},{5,6},{6,7},{7,4},{8,9},{9,10},{10,1... | collective-permute-start | bytes 196616 | tf_op jit(solution)/shard_map/ppermute | solution.py:173
  63.3 4.4 %collective-permute-start.12 = (f32[2,2,32,128]{3,2,1,0:T(8,128)S(1)}, f32[2,2,32,128]{3,2,1,0:T(8,128)S(1)}, u32[]{:S(2)}, u32[]{:S(2)}) collective-permute-start(f32[2,2,32,128]{3,2,1,0:T(8,128)S(1)} %get-tuple-element.294), channel_id=1, source_target_pairs={{0,2},{1,3},{2,0},{3,1},{4,6},{5,7},{6,4},{7,5},{8,10},{9,11},{10,... | collective-permute-start | bytes 196616 | tf_op jit(solution)/shard_map/ppermute | solution.py:173
  65.2 3.4 %collective-permute-start.11 = (f32[2,2,32,128]{3,2,1,0:T(8,128)S(1)}, f32[2,2,32,128]{3,2,1,0:T(8,128)S(1)}, u32[]{:S(2)}, u32[]{:S(2)}) collective-permute-start(f32[2,2,32,128]{3,2,1,0:T(8,128)S(1)} %get-tuple-element.295), channel_id=1, source_target_pairs={{0,3},{1,0},{2,1},{3,2},{4,7},{5,4},{6,5},{7,6},{8,11},{9,8},{10,9... | collective-permute-start | bytes 196616 | tf_op jit(solution)/shard_map/ppermute | solution.py:173

commit v17 on v16

--- a/solution.py
+++ b/solution.py
@@ -51,9 +51,7 @@
     coupling_rows = coupling.reshape(step_count * state_width, cols)
     seen_parts = observed.reshape(step_count, col_groups, own_rows, cols).transpose(1, 0, 2, 3)
     seen_parts = seen_parts.reshape(col_groups, step_count * own_rows, cols)
-    n_coupling = step_count * state_width
     n_seen = step_count * own_rows
-    lead = col_groups // 2
     couplings, extras = [], []
     for shift in range(col_groups):
         dest = (col_pos + shift) % col_groups
@@ -67,14 +65,9 @@
         if shift == 0:
             couplings.append(coupling_rows)
             extras.append(extra)
-        elif shift == lead:
+        else:
             couplings.append(lax.ppermute(coupling_rows, ("tm", "col"), pairs))
             extras.append(lax.ppermute(extra, ("tm", "col"), pairs))
-        else:
-            chunk = jnp.concatenate([coupling_rows, extra], axis=0)
-            chunk = lax.ppermute(chunk, ("tm", "col"), pairs)
-            couplings.append(chunk[:n_coupling])
-            extras.append(chunk[n_coupling:])
 
     def from_source(options, j):
         which = (col_pos - j) % col_groups

time: 70.3 us -> 71.5 us (1.017)
  waiting for transfers between devices: 41.3 us -> 43.4 us
    ppermute x1 -> x3, waiting for transfers between devices: 4 us -> 10.2 us  [local(): couplings.append(lax.ppermute(coupling_rows, ('tm', 'col'), pairs))]
    ppermute x1 -> x3, waiting for transfers between devices: 4.84 us -> 0.01 us  [local(): extras.append(lax.ppermute(extra, ('tm', 'col'), pairs))]
    ppermute x3, starting transfers between devices: 3.42 us -> 0.91 us  [local(): piece = lax.ppermute(piece, ('tm', 'col'), pairs)]
    ppermute x2 -> x0, starting transfers between devices: 2.46 us -> none  [local(): chunk = lax.ppermute(chunk, ('tm', 'col'), pairs)]
    ppermute x3, waiting for transfers between devices: 1.9 us -> 4.34 us  [local(): piece = lax.ppermute(piece, ('tm', 'col'), pairs)]
    ppermute x1 -> x3, starting transfers between devices: 1.07 us -> 3.25 us  [local(): extras.append(lax.ppermute(extra, ('tm', 'col'), pairs))]
    ppermute x1 -> x3, starting transfers between devices: 0.96 us -> 2.98 us  [local(): couplings.append(lax.ppermute(coupling_rows, ('tm', 'col'), pairs))]
    ppermute x2 -> x0, waiting for transfers between devices: 1.33 us -> none  [local(): chunk = lax.ppermute(chunk, ('tm', 'col'), pairs)]
  transfers between devices with their start and end apart: 14 -> 16, of which waited for: 8 -> 7; matrix products, arithmetic and copies ran while one was open for 1% -> 2% of each run, Pallas kernels for 0% -> 0%
where the time goes in v17:
time: 71.5 us; the launch traced here: 71.2 us
  waiting for transfers between devices  43.4 us (61%)
  starting transfers between devices  15.3 us (21%)
  matrix products  4.42 us (6%)
  local copies, waits for them, and re-layouts  3.49 us (5%)
  other arithmetic  2.88 us (4%)
  between operations  1.26 us (2%)
    ppermute x7, waiting for transfers between devices, local(): got = lax.ppermute(send, ('tm', 'col'), pairs)  28.8 us
    ppermute x3, waiting for transfers between devices, local(): couplings.append(lax.ppermute(coupling_rows, ('tm', 'col'), pairs))  10.2 us
    ppermute x7, starting transfers between devices, local(): got = lax.ppermute(send, ('tm', 'col'), pairs)  8.14 us
    dot_general x17, matrix products, split_dot(): lax.dot_general(both, weights, (((1,), (contract,)), ((), ())), preferred...  4.42 us
    ppermute x3, waiting for transfers between devices, local(): piece = lax.ppermute(piece, ('tm', 'col'), pairs)  4.34 us
    ppermute x3, starting transfers between devices, local(): extras.append(lax.ppermute(extra, ('tm', 'col'), pairs))  3.25 us
    ppermute x3, starting transfers between devices, local(): couplings.append(lax.ppermute(coupling_rows, ('tm', 'col'), pairs))  2.98 us
  transfers between devices with their start and end apart: 16, of which 7 were waited for; matrix products, arithmetic and copies ran while one was open for 2% of the time, Pallas kernels for 0%

profile of v17, /device:TPU:0, one launch (start us, length us, event | category | flops | bytes accessed | tf_op | source)
XLA Modules:
  0.0 71.2 jit_solution(15550618672074925925)
XLA Ops:
  0.7 0.8 %copy.9 = bf16[4,2,32,128]{3,2,1,0:T(8,128)(2,1)S(1)} copy(bf16[4,2,32,128]{3,2,0,1:T(8,128)(2,1)} %bitcast.320) | data formatting | bytes 131072 | tf_op jit(solution)/shard_map/transpose | solution.py:52
  1.5 0.7 reduce-precision_convert_fusion.31
  2.3 2.5 %collective-permute-start = (bf16[80,128]{1,0:T(8,128)(2,1)S(1)}, bf16[80,128]{1,0:T(8,128)(2,1)S(1)}, u32[]{:S(2)}, u32[]{:S(2)}) collective-permute-start(bf16[80,128]{1,0:T(8,128)(2,1)S(1)} %get-tuple-element.316), channel_id=1, source_target_pairs={{0,3},{1,0},{2,1},{3,2},{4,7},{5,4},{6,5},{7,6},{8,11},{9,8},{10,9... | collective-permute-start | bytes 61448 | tf_op jit(solution)/shard_map/ppermute | solution.py:70
  4.8 0.6 collective-permute-start.1
  5.6 1.6 %collective-permute-start.3 = (bf16[1024,128]{1,0:T(8,128)(2,1)}, bf16[1024,128]{1,0:T(8,128)(2,1)S(1)}, u32[]{:S(2)}, u32[]{:S(2)}) collective-permute-start(bf16[1024,128]{1,0:T(8,128)(2,1)} %bitcast.310), channel_id=1, source_target_pairs={{0,3},{1,0},{2,1},{3,2},{4,7},{5,4},{6,5},{7,6},{8,11},{9,8},{10,9... | collective-permute-start | bytes 786440 | tf_op jit(solution)/shard_map/ppermute | solution.py:69
  7.2 1.4 %collective-permute-start.4 = (bf16[1024,128]{1,0:T(8,128)(2,1)}, bf16[1024,128]{1,0:T(8,128)(2,1)S(1)}, u32[]{:S(2)}, u32[]{:S(2)}) collective-permute-start(bf16[1024,128]{1,0:T(8,128)(2,1)} %bitcast.311), channel_id=1, source_target_pairs={{0,2},{1,3},{2,0},{3,1},{4,6},{5,7},{6,4},{7,5},{8,10},{9,11},{10,... | collective-permute-start | bytes 786440 | tf_op jit(solution)/shard_map/ppermute | solution.py:69
  8.6 0.7 convert_element_type.54
  9.2 0.2 broadcast_in_dim.15
  9.5 0.6 mul.324
  10.1 0.3 copy-done
  10.7 3.5 %collective-permute-done.3 = bf16[1024,128]{1,0:T(8,128)(2,1)S(1)} collective-permute-done((bf16[1024,128]{1,0:T(8,128)(2,1)}, bf16[1024,128]{1,0:T(8,128)(2,1)S(1)}, u32[]{:S(2)}, u32[]{:S(2)}) %collective-permute-start.3) | collective-permute-done | bytes 262176 | tf_op jit(solution)/shard_map/ppermute | solution.py:69
  14.2 6.8 %collective-permute-done.4 = bf16[1024,128]{1,0:T(8,128)(2,1)S(1)} collective-permute-done((bf16[1024,128]{1,0:T(8,128)(2,1)}, bf16[1024,128]{1,0:T(8,128)(2,1)S(1)}, u32[]{:S(2)}, u32[]{:S(2)}) %collective-permute-start.4) | collective-permute-done | bytes 262176 | tf_op jit(solution)/shard_map/ppermute | solution.py:69
  21.1 0.3 maximum_multiply_fusion
  21.5 0.6 conditional.7
  21.5 0.2 fusion.21
  22.1 3.5 %collective-permute-start.6 = (f32[32,512]{1,0:T(8,128)S(1)}, f32[32,512]{1,0:T(8,128)S(1)}, u32[]{:S(2)}, u32[]{:S(2)}) collective-permute-start(f32[32,512]{1,0:T(8,128)S(1)} %get-tuple-element.321), channel_id=1, source_target_pairs={{0,4},{1,5},{2,6},{3,7},{28,24},{29,25},{30,26},{31,27}} | collective-permute-start | bytes 196616 | tf_op jit(solution)/shard_map/ppermute | solution.py:135
  25.6 1.9 %collective-permute-done.6 = f32[32,512]{1,0:T(8,128)S(1)} collective-permute-done((f32[32,512]{1,0:T(8,128)S(1)}, f32[32,512]{1,0:T(8,128)S(1)}, u32[]{:S(2)}, u32[]{:S(2)}) %collective-permute-start.6) | collective-permute-done | bytes 65568 | tf_op jit(solution)/shard_map/ppermute | solution.py:135
  27.5 0.7 conditional.8
  27.5 0.3 fusion.37
  27.9 0.3 fusion.35
  28.2 0.7 collective-permute-start.7
  28.9 0.7 conditional.9
  28.9 0.3 fusion.76
  29.3 0.3 fusion.74
  29.6 0.7 collective-permute-start.8
  30.3 0.7 conditional.10
  30.4 0.3 fusion.115
  30.7 0.3 fusion.113
  31.0 0.7 collective-permute-start.9
  31.7 0.7 conditional.11
  31.8 0.3 fusion.154
  32.1 0.3 fusion.152
  32.4 0.7 collective-permute-start.10
  33.1 0.7 conditional.12
  33.2 0.3 fusion.193
  33.5 0.3 fusion.191
  33.8 0.7 collective-permute-start.11
  34.5 0.7 conditional.13
  34.6 0.3 fusion.232
  34.9 0.3 fusion.230
  35.2 1.3 %collective-permute-start.12 = (f32[32,512]{1,0:T(8,128)S(1)}, f32[32,512]{1,0:T(8,128)S(1)}, u32[]{:S(2)}, u32[]{:S(2)}) collective-permute-start(f32[32,512]{1,0:T(8,128)S(1)} %get-tuple-element.327), channel_id=1, source_target_pairs={{24,28},{25,29},{26,30},{27,31},{4,0},{5,1},{6,2},{7,3}} | collective-permute-start | bytes 196616 | tf_op jit(solution)/shard_map/ppermute | solution.py:135
  36.6 26.9 %collective-permute-done.12 = f32[32,512]{1,0:T(8,128)S(1)} collective-permute-done((f32[32,512]{1,0:T(8,128)S(1)}, f32[32,512]{1,0:T(8,128)S(1)}, u32[]{:S(2)}, u32[]{:S(2)}) %collective-permute-start.12) | collective-permute-done | bytes 65568 | tf_op jit(solution)/shard_map/ppermute | solution.py:135
  64.0 0.3 fusion.270
  64.5 0.7 collective-permute-start.14
  65.4 1.4 %collective-permute-done.13 = f32[2,2,32,128]{3,2,1,0:T(8,128)S(1)} collective-permute-done((f32[2,2,32,128]{3,2,1,0:T(8,128)S(1)}, f32[2,2,32,128]{3,2,1,0:T(8,128)S(1)}, u32[]{:S(2)}, u32[]{:S(2)}) %collective-permute-start.13) | collective-permute-done | bytes 65568 | tf_op jit(solution)/shard_map/ppermute | solution.py:166
  66.8 2.7 %collective-permute-done.14 = f32[2,2,32,128]{3,2,1,0:T(8,128)S(1)} collective-permute-done((f32[2,2,32,128]{3,2,1,0:T(8,128)S(1)}, f32[2,2,32,128]{3,2,1,0:T(8,128)S(1)}, u32[]{:S(2)}, u32[]{:S(2)}) %collective-permute-start.14) | collective-permute-done | bytes 65568 | tf_op jit(solution)/shard_map/ppermute | solution.py:166
  69.8 0.7 copy.10
  70.5 0.7 copy.11
  (99 shorter events, 2.5 us)
Async XLA Ops:
  2.3 7.8 %collective-permute-start = (bf16[80,128]{1,0:T(8,128)(2,1)S(1)}, bf16[80,128]{1,0:T(8,128)(2,1)S(1)}, u32[]{:S(2)}, u32[]{:S(2)}) collective-permute-start(bf16[80,128]{1,0:T(8,128)(2,1)S(1)} %get-tuple-element.316), channel_id=1, source_target_pairs={{0,3},{1,0},{2,1},{3,2},{4,7},{5,4},{6,5},{7,6},{8,11},{9,8},{10,9... | collective-permute-start | bytes 61448 | tf_op jit(solution)/shard_map/ppermute | solution.py:70
  4.8 5.6 %collective-permute-start.1 = (bf16[80,128]{1,0:T(8,128)(2,1)S(1)}, bf16[80,128]{1,0:T(8,128)(2,1)S(1)}, u32[]{:S(2)}, u32[]{:S(2)}) collective-permute-start(bf16[80,128]{1,0:T(8,128)(2,1)S(1)} %get-tuple-element.317), channel_id=1, source_target_pairs={{0,2},{1,3},{2,0},{3,1},{4,6},{5,7},{6,4},{7,5},{8,10},{9,11},{10,... | collective-permute-start | bytes 61448 | tf_op jit(solution)/shard_map/ppermute | solution.py:70
  5.4 5.0 %collective-permute-start.2 = (bf16[80,128]{1,0:T(8,128)(2,1)S(1)}, bf16[80,128]{1,0:T(8,128)(2,1)S(1)}, u32[]{:S(2)}, u32[]{:S(2)}) collective-permute-start(bf16[80,128]{1,0:T(8,128)(2,1)S(1)} %get-tuple-element.315), channel_id=1, source_target_pairs={{0,1},{1,2},{2,3},{3,0},{4,5},{5,6},{6,7},{7,4},{8,9},{9,10},{10,1... | collective-permute-start | bytes 61448 | tf_op jit(solution)/shard_map/ppermute | solution.py:70
  5.6 8.6 %collective-permute-start.3 = (bf16[1024,128]{1,0:T(8,128)(2,1)}, bf16[1024,128]{1,0:T(8,128)(2,1)S(1)}, u32[]{:S(2)}, u32[]{:S(2)}) collective-permute-start(bf16[1024,128]{1,0:T(8,128)(2,1)} %bitcast.310), channel_id=1, source_target_pairs={{0,3},{1,0},{2,1},{3,2},{4,7},{5,4},{6,5},{7,6},{8,11},{9,8},{10,9... | collective-permute-start | bytes 786440 | tf_op jit(solution)/shard_map/ppermute | solution.py:69
  7.2 13.8 %collective-permute-start.4 = (bf16[1024,128]{1,0:T(8,128)(2,1)}, bf16[1024,128]{1,0:T(8,128)(2,1)S(1)}, u32[]{:S(2)}, u32[]{:S(2)}) collective-permute-start(bf16[1024,128]{1,0:T(8,128)(2,1)} %bitcast.311), channel_id=1, source_target_pairs={{0,2},{1,3},{2,0},{3,1},{4,6},{5,7},{6,4},{7,5},{8,10},{9,11},{10,... | collective-permute-start | bytes 786440 | tf_op jit(solution)/shard_map/ppermute | solution.py:69
  9.5 1.0 %copy-start = (bf16[2,512,128]{2,1,0:T(8,128)(2,1)S(1)}, bf16[2,512,128]{2,1,0:T(8,128)(2,1)}, u32[]{:S(2)}) copy-start(bf16[2,512,128]{2,1,0:T(8,128)(2,1)} %param.22) | copy-start | bytes 786436
  10.4 10.6 %collective-permute-start.5 = (bf16[1024,128]{1,0:T(8,128)(2,1)S(1)}, bf16[1024,128]{1,0:T(8,128)(2,1)S(1)}, u32[]{:S(2)}, u32[]{:S(2)}) collective-permute-start(bf16[1024,128]{1,0:T(8,128)(2,1)S(1)} %bitcast.312), channel_id=1, source_target_pairs={{0,1},{1,2},{2,3},{3,0},{4,5},{5,6},{6,7},{7,4},{8,9},{9,10},{10,1... | collective-permute-start | bytes 786440 | tf_op jit(solution)/shard_map/ppermute | solution.py:69
  22.1 5.4 %collective-permute-start.6 = (f32[32,512]{1,0:T(8,128)S(1)}, f32[32,512]{1,0:T(8,128)S(1)}, u32[]{:S(2)}, u32[]{:S(2)}) collective-permute-start(f32[32,512]{1,0:T(8,128)S(1)} %get-tuple-element.321), channel_id=1, source_target_pairs={{0,4},{1,5},{2,6},{3,7},{28,24},{29,25},{30,26},{31,27}} | collective-permute-start | bytes 196616 | tf_op jit(solution)/shard_map/ppermute | solution.py:135
  28.2 0.7 collective-permute-start.7
  29.6 0.7 collective-permute-start.8
  31.0 0.7 collective-permute-start.9
  32.4 0.7 collective-permute-start.10
  33.8 0.7 collective-permute-start.11
  35.2 28.2 %collective-permute-start.12 = (f32[32,512]{1,0:T(8,128)S(1)}, f32[32,512]{1,0:T(8,128)S(1)}, u32[]{:S(2)}, u32[]{:S(2)}) collective-permute-start(f32[32,512]{1,0:T(8,128)S(1)} %get-tuple-element.327), channel_id=1, source_target_pairs={{24,28},{25,29},{26,30},{27,31},{4,0},{5,1},{6,2},{7,3}} | collective-permute-start | bytes 196616 | tf_op jit(solution)/shard_map/ppermute | solution.py:135
  64.4 2.4 %collective-permute-start.13 = (f32[2,2,32,128]{3,2,1,0:T(8,128)S(1)}, f32[2,2,32,128]{3,2,1,0:T(8,128)S(1)}, u32[]{:S(2)}, u32[]{:S(2)}) collective-permute-start(f32[2,2,32,128]{3,2,1,0:T(8,128)S(1)} %get-tuple-element.290), channel_id=1, source_target_pairs={{0,3},{1,0},{2,1},{3,2},{4,7},{5,4},{6,5},{7,6},{8,11},{9,8},{10,9... | collective-permute-start | bytes 196616 | tf_op jit(solution)/shard_map/ppermute | solution.py:166
  64.5 5.0 %collective-permute-start.14 = (f32[2,2,32,128]{3,2,1,0:T(8,128)S(1)}, f32[2,2,32,128]{3,2,1,0:T(8,128)S(1)}, u32[]{:S(2)}, u32[]{:S(2)}) collective-permute-start(f32[2,2,32,128]{3,2,1,0:T(8,128)S(1)} %get-tuple-element.289), channel_id=1, source_target_pairs={{0,2},{1,3},{2,0},{3,1},{4,6},{5,7},{6,4},{7,5},{8,10},{9,11},{10,... | collective-permute-start | bytes 196616 | tf_op jit(solution)/shard_map/ppermute | solution.py:166
  65.2 4.5 %collective-permute-start.15 = (f32[2,2,32,128]{3,2,1,0:T(8,128)S(1)}, f32[2,2,32,128]{3,2,1,0:T(8,128)S(1)}, u32[]{:S(2)}, u32[]{:S(2)}) collective-permute-start(f32[2,2,32,128]{3,2,1,0:T(8,128)S(1)} %get-tuple-element.215), channel_id=1, source_target_pairs={{0,1},{1,2},{2,3},{3,0},{4,5},{5,6},{6,7},{7,4},{8,9},{9,10},{10,1... | collective-permute-start | bytes 196616 | tf_op jit(solution)/shard_map/ppermute | solution.py:166
